TPU v7x, 32 devices: a whole 2x2x4 slice. The times are simulated.
32 devices in a mesh: dom: 8 (over z, y), ka: 4 (over x, core).
Axes of the slice: x: 2, y: 2, z: 4, core: 2. Of those that a mesh axis runs over, the one named last changes fastest.
Arguments:
- cell_coordinates_frac: float32 [3, 49152], P(None, 'dom'), may hold values from 0 to 1
- site_strengths: bfloat16 [32, 49152], P(None, 'dom'), may hold values from -6 to 6
- miller_indices: int32 [3, 2048], P(None, 'ka'), may hold values from -11 to 16, as said below
- occupied_site_tally: int32 [8], P('dom'), may hold values from 3072 to 6144, as said below
- gaussian_spread: float32 [32], replicated, may hold values from 0.5 to 4
Outputs:
- potential: float32 [32, 49152], P(None, ('dom', 'ka'))
- forces: float32 [3, 49152], P(None, ('dom', 'ka'))
Inputs may be any that keep to these rules, and one draw needn't show every extreme that they name: `miller_indices`: the vectors are distinct; h and k lie in -11 to 11 and l in 1 to 16, so none is zero; the extreme vectors (-11, -11, 1) and (11, 11, 16) occur. `occupied_site_tally`: some domain is full and some holds exactly half of its slots.
All inputs are finite; a program needn't handle non-finite values.
Results may differ from a plain program's by a relative error of at most 0.0044.
Values may be sent and summed in bfloat16 or wider, within the bound.
No kernel may reach another device: no remote copies, remote signals or barrier semaphores. Data moves between devices by JAX's collectives and lax.ppermute only.
A program may use at most 64 MiB of HBM per device.

v0:
```python
import math

import jax
import jax.numpy as jnp
from jax import lax
from jax.sharding import PartitionSpec as P

two_pi = 6.283185307179586
box_length = 125.0

_COS_C = [(-1) ** n * two_pi ** (2 * n) / float(math.factorial(2 * n)) for n in range(6)]
_SIN_C = [(-1) ** n * two_pi ** (2 * n + 1) / float(math.factorial(2 * n + 1)) for n in range(6)]


def turns_cos_sin(t):
    r = t - jnp.floor(t + 0.5)
    q = jnp.floor(4.0 * r + 0.5)
    u = r - 0.25 * q
    u2 = u * u
    c = jnp.float32(_COS_C[4])
    for coef in _COS_C[3::-1]:
        c = c * u2 + jnp.float32(coef)
    s = jnp.float32(_SIN_C[4])
    for coef in _SIN_C[3::-1]:
        s = s * u2 + jnp.float32(coef)
    s = s * u
    odd = jnp.abs(q) == 1.0
    cos_mag = jnp.where(odd, s, c)
    sin_mag = jnp.where(odd, c, s)
    cos_out = jnp.where((q == 1.0) | (jnp.abs(q) == 2.0), -cos_mag, cos_mag)
    sin_out = jnp.where((q == -1.0) | (jnp.abs(q) == 2.0), -sin_mag, sin_mag)
    return cos_out, sin_out


def reciprocal_filter_weight(s_cos, s_sin, cartesian_mode_vector, gaussian_spread, atoms_total):
    norm_sq = (
        cartesian_mode_vector[0] * cartesian_mode_vector[0]
        + cartesian_mode_vector[1] * cartesian_mode_vector[1]
        + cartesian_mode_vector[2] * cartesian_mode_vector[2]
    )
    scale = two_pi / box_length
    wavevector_norm_squared = scale * scale * norm_sq
    kernel = (
        2.0
        * jnp.exp(
            -0.5 * (gaussian_spread * gaussian_spread)[:, None] * wavevector_norm_squared[None, :]
        )
        / norm_sq[None, :]
        / jnp.sqrt(jnp.float32(atoms_total))
    )
    partial_first_term = kernel * s_cos
    partial_second_term = kernel * s_sin
    cos_side = jnp.concatenate(
        [
            partial_first_term,
            -scale * cartesian_mode_vector[0] * partial_second_term,
            -scale * cartesian_mode_vector[1] * partial_second_term,
            -scale * cartesian_mode_vector[2] * partial_second_term,
        ],
        0,
    )
    sin_side = jnp.concatenate(
        [
            partial_second_term,
            scale * cartesian_mode_vector[0] * partial_first_term,
            scale * cartesian_mode_vector[1] * partial_first_term,
            scale * cartesian_mode_vector[2] * partial_first_term,
        ],
        0,
    )
    return (cos_side.astype(jnp.bfloat16), sin_side.astype(jnp.bfloat16))


def butterfly_sum(x, axis, n):
    step = 1
    while step < n:
        x = x + lax.ppermute(x, axis, [(i, i ^ step) for i in range(n)])
        step *= 2
    return x


def halving_scatter(x, axis, n):
    rows_all = x.shape[1]
    rows = rows_all // n
    me = lax.axis_index(axis)
    held = x.reshape(x.shape[0], n, rows)
    step = 1
    while step < n:
        m = held.shape[1]
        pairs = held.reshape(held.shape[0], m // 2, 2, rows)
        bit = (me // step) % 2
        keep = jnp.where(bit == 0, pairs[:, :, 0], pairs[:, :, 1])
        send = jnp.where(bit == 0, pairs[:, :, 1], pairs[:, :, 0])
        held = keep + lax.ppermute(send, axis, [(i, i ^ step) for i in range(n)])
        step *= 2
    return held.reshape(held.shape[0], rows)


def make_local(n_dom, n_ka):
    def local(
        cell_coordinates_frac, site_strengths, miller_indices, occupied_site_tally, gaussian_spread
    ):
        channels = site_strengths.shape[0]
        n_local = cell_coordinates_frac.shape[1]
        atoms_total = n_local * n_dom
        live = jnp.arange(n_local) < occupied_site_tally[0]
        charge_live = jnp.where(live[None, :], site_strengths, jnp.zeros_like(site_strengths))
        cartesian_mode_vector = miller_indices.astype(jnp.float32)
        t = (
            cartesian_mode_vector[0][:, None] * cell_coordinates_frac[0][None, :]
            + cartesian_mode_vector[1][:, None] * cell_coordinates_frac[1][None, :]
            + cartesian_mode_vector[2][:, None] * cell_coordinates_frac[2][None, :]
        )
        cos_f, sin_f = turns_cos_sin(t)
        cos_table = cos_f.astype(jnp.bfloat16)
        sin_table = sin_f.astype(jnp.bfloat16)
        cos_table, sin_table = lax.optimization_barrier((cos_table, sin_table))
        tensor_product = (((1,), (1,)), ((), ()))
        s_cos = lax.dot_general(
            charge_live, cos_table, tensor_product, preferred_element_type=jnp.float32
        )
        s_sin = lax.dot_general(
            charge_live, sin_table, tensor_product, preferred_element_type=jnp.float32
        )
        s_both = butterfly_sum(jnp.stack([s_cos, s_sin], 0), "dom", n_dom)
        cos_side, sin_side = reciprocal_filter_weight(
            s_both[0], s_both[1], cartesian_mode_vector, gaussian_spread, atoms_total
        )
        field = jnp.dot(cos_side, cos_table, preferred_element_type=jnp.float32)
        field = field + jnp.dot(sin_side, sin_table, preferred_element_type=jnp.float32)
        charge_f = charge_live.astype(jnp.float32)
        head = jnp.where(live[None, :], field[:channels], 0.0)
        force_rows = [
            jnp.sum(charge_f * field[channels * (1 + d) : channels * (2 + d)], 0, keepdims=True)
            for d in range(3)
        ]
        partial = jnp.concatenate([head] + force_rows, 0)
        own = halving_scatter(partial, "ka", n_ka)
        return (own[:channels], own[channels:])

    return local


def solution(mesh):
    placed = (P(None, "dom"), P(None, "dom"), P(None, "ka"), P("dom"), P())
    return jax.shard_map(
        make_local(mesh.shape["dom"], mesh.shape["ka"]),
        mesh=mesh,
        in_specs=placed,
        out_specs=(P(None, ("dom", "ka")), P(None, ("dom", "ka"))),
        check_vma=False,
    )
```

profile of v0, /device:TPU:0, one launch (start us, length us, event | category | flops | bytes accessed | tf_op | source)
XLA Modules:
  0.0 66.4 jit_solution(7023502908573457216)
XLA Ops:
  0.6 0.7 %convert_element_type.14 = f32[3,512]{1,0:T(4,128)S(1)} convert(s32[3,512]{1,0:T(4,128)} %param.7) | non-fusion elementwise | flops 1536 | bytes 12288 | tf_op jit(solution)/shard_map/convert_element_type | solution.py:108
  1.4 1.1 %fusion.33 = (f32[1,6144]{1,0:T(1,128)S(1)}, f32[1,6144]{1,0:T(1,128)S(1)}, f32[1,6144]{1,0:T(1,128)S(1)}) fusion(f32[3,6144]{1,0:T(4,128)} %param.5), kind=kLoop, calls=%fused_computation.77 | loop fusion | bytes 147456 | tf_op jit(solution)/shard_map/slice | solution.py:110
  2.5 0.0 copy-start.2
  2.5 21.2 %fusion.1 = (bf16[512,6144]{1,0:T(8,128)(2,1)S(1)}, bf16[512,6144]{1,0:T(8,128)(2,1)S(1)}) fusion(f32[6144]{0:T(1024)S(1)} %bitcast.53, f32[512]{0:T(512)S(1)} %bitcast.63, f32[6144]{0:T(1024)S(1)} %bitcast.54, f32[512]{0:T(512)S(1)} %bitcast.64, f32[6144]{0:T(1024)S(1)} %bitcast.52, f32[512]{0:T(512)S(1)} %bitcast.65), kind=kLoop, calls=%fused_computation.3 | loop fusion | flops 144703488 | bytes 12662784 | tf_op jit(solution)/shard_map/convert_element_type | solution.py:116
  23.7 0.0 copy-start
  23.7 0.0 copy-start.1
  24.4 0.0 copy-done.2
  24.4 0.0 copy-start.3
  24.4 2.0 %convolution_bitcast_fusion = f32[1,32,512]{2,1,0:T(8,128)S(1)} fusion(bf16[512,6144]{1,0:T(8,128)(2,1)S(1)} %get-tuple-element.5, bf16[32,6144]{1,0:T(8,128)(2,1)S(1)} %copy-done.2, pred[6144]{0:T(1024)(128)(4,1)S(1)} %iota_compare_fusion), kind=kOutput, calls=%fused_computation.19 | convolution fusion | flops 201523200 | bytes 6756352 | tf_op jit(solution)/shard_map/dot_general | solution.py:122
  26.4 2.0 %convolution_bitcast_fusion.1 = f32[1,32,512]{2,1,0:T(8,128)S(1)} fusion(bf16[512,6144]{1,0:T(8,128)(2,1)S(1)} %get-tuple-element.4, bf16[32,6144]{1,0:T(8,128)(2,1)S(1)} %copy-done.2, pred[6144]{0:T(1024)(128)(4,1)S(1)} %iota_compare_fusion), kind=kOutput, calls=%fused_computation.20 | convolution fusion | flops 201523200 | bytes 6756352 | tf_op jit(solution)/shard_map/dot_general | solution.py:119
  28.4 0.0 copy-done
  28.4 0.0 copy-done.1
  28.4 3.0 %collective-permute-start = (f32[2,32,512]{2,1,0:T(8,128)S(1)}, f32[2,32,512]{2,1,0:T(8,128)S(1)}, u32[]{:S(2)}, u32[]{:S(2)}) collective-permute-start(f32[2,32,512]{2,1,0:T(8,128)S(1)} %pad_maximum_fusion.1), channel_id=1, source_target_pairs={{0,4},{4,0},{8,12},{12,8},{16,20},{20,16},{24,28},{28,24},{1,5},{5... | collective-permute-start | bytes 393224 | tf_op jit(solution)/shard_map/ppermute | solution.py:77
  31.5 3.5 %collective-permute-done = f32[2,32,512]{2,1,0:T(8,128)S(1)} collective-permute-done((f32[2,32,512]{2,1,0:T(8,128)S(1)}, f32[2,32,512]{2,1,0:T(8,128)S(1)}, u32[]{:S(2)}, u32[]{:S(2)}) %collective-permute-start) | collective-permute-done | bytes 131104 | tf_op jit(solution)/shard_map/ppermute | solution.py:77
  35.0 1.9 %collective-permute-start.1 = (f32[2,32,512]{2,1,0:T(8,128)S(1)}, f32[2,32,512]{2,1,0:T(8,128)S(1)}, u32[]{:S(2)}, u32[]{:S(2)}) collective-permute-start(f32[2,32,512]{2,1,0:T(8,128)S(1)} %fusion.29), channel_id=1, source_target_pairs={{0,8},{4,12},{8,0},{12,4},{16,24},{20,28},{24,16},{28,20},{1,9},{5... | collective-permute-start | bytes 393224 | tf_op jit(solution)/shard_map/ppermute | solution.py:77
  36.8 3.2 %collective-permute-done.1 = f32[2,32,512]{2,1,0:T(8,128)S(1)} collective-permute-done((f32[2,32,512]{2,1,0:T(8,128)S(1)}, f32[2,32,512]{2,1,0:T(8,128)S(1)}, u32[]{:S(2)}, u32[]{:S(2)}) %collective-permute-start.1) | collective-permute-done | bytes 131104 | tf_op jit(solution)/shard_map/ppermute | solution.py:77
  40.0 2.9 %collective-permute-start.2 = (f32[2,32,512]{2,1,0:T(8,128)S(1)}, f32[2,32,512]{2,1,0:T(8,128)S(1)}, u32[]{:S(2)}, u32[]{:S(2)}) collective-permute-start(f32[2,32,512]{2,1,0:T(8,128)S(1)} %fusion.38), channel_id=1, source_target_pairs={{0,16},{4,20},{8,24},{12,28},{16,0},{20,4},{24,8},{28,12},{1,17},{... | collective-permute-start | bytes 393224 | tf_op jit(solution)/shard_map/ppermute | solution.py:77
  42.9 0.0 copy-done.3
  42.9 4.5 %collective-permute-done.2 = f32[2,32,512]{2,1,0:T(8,128)S(1)} collective-permute-done((f32[2,32,512]{2,1,0:T(8,128)S(1)}, f32[2,32,512]{2,1,0:T(8,128)S(1)}, u32[]{:S(2)}, u32[]{:S(2)}) %collective-permute-start.2) | collective-permute-done | bytes 131104 | tf_op jit(solution)/shard_map/ppermute | solution.py:77
  47.4 0.1 multiply_convert_fusion.2
  47.5 0.0 slice-start
  47.5 0.0 slice-start.1
  47.6 4.0 %fusion.8 = f32[128,6144]{1,0:T(8,128)S(1)} fusion(bf16[512,6144]{1,0:T(8,128)(2,1)} %copy-done.1, bf16[32,512]{1,0:T(8,128)(2,1)S(1)} %get-tuple-element.41, bf16[32,512]{1,0:T(8,128)(2,1)S(1)} %get-tuple-element.40, bf16[32,512]{1,0:T(8,128)(2,1)S(1)} %get-tuple-element.42, bf16[32,512]{1,0:T(8,128)(2,1)S(1)} %get-tuple-element.25), kind=kOutput, calls=%fused_computation.34 | convolution fusion | flops 805830656 | bytes 9568256 | tf_op jit(solution)/shard_map/dot_general | solution.py:129
  51.6 0.0 slice-done
  51.6 0.6 slice-done.1
  52.2 1.0 %convolution_add_fusion = f32[128,6144]{1,0:T(8,128)S(1)} fusion(f32[128,6144]{1,0:T(8,128)S(1)} %fusion.8, bf16[512,6144]{1,0:T(8,128)(2,1)S(1)} %bitcast.51, bf16[32,512]{1,0:T(8,128)(2,1)S(1)} %get-tuple-element.24, bf16[32,512]{1,0:T(8,128)(2,1)S(1)} %get-tuple-element.23, bf16[32,512]{1,0:T(8,128)(2,1)S(1)} %get-tuple-element.11, ...), kind=kOutput, calls=%fused_computation.15 | convolution fusion | flops 806617088 | bytes 12713984 | tf_op jit(solution)/shard_map/dot_general | solution.py:130
  53.2 0.4 fusion.4
  53.6 0.7 %concatenate.22 = f32[32,2,2,1536]{3,2,1,0:T(2,128)S(1)} reshape(f32[32,6144]{1,0:T(8,128)S(1)} %get-tuple-element.15) | data formatting | bytes 1572864 | tf_op jit(solution)/shard_map/concatenate | solution.py:137
  54.3 0.3 copy.8
  54.8 0.1 pad_maximum_fusion
  54.9 0.1 select_bitcast_fusion
  54.9 0.1 collective-permute-start.3
  55.0 1.8 %collective-permute-done.3 = f32[35,2,1536]{2,0,1:T(8,128)S(1)} collective-permute-done((f32[35,2,1536]{2,0,1:T(8,128)S(1)}, f32[35,2,1536]{2,0,1:T(8,128)S(1)}, u32[]{:S(2)}, u32[]{:S(2)}) %collective-permute-start.3) | collective-permute-done | bytes 430112 | tf_op jit(solution)/shard_map/ppermute | solution.py:94
  56.9 0.1 fusion.7
  57.0 1.8 %collective-permute-start.4 = (f32[35,1,1536]{2,0,1:T(8,128)S(1)}, f32[35,1,1536]{2,0,1:T(8,128)S(1)}, u32[]{:S(2)}, u32[]{:S(2)}) collective-permute-start(f32[35,1,1536]{2,0,1:T(8,128)S(1)} %select_bitcast_fusion.1), channel_id=1, source_target_pairs={{0,2},{1,3},{2,0},{3,1},{4,6},{5,7},{6,4},{7,5},{8,10},{9,11},{10,... | collective-permute-start | bytes 645128 | tf_op jit(solution)/shard_map/ppermute | solution.py:94
  58.8 6.3 %collective-permute-done.4 = f32[35,1,1536]{2,0,1:T(8,128)S(1)} collective-permute-done((f32[35,1,1536]{2,0,1:T(8,128)S(1)}, f32[35,1,1536]{2,0,1:T(8,128)S(1)}, u32[]{:S(2)}, u32[]{:S(2)}) %collective-permute-start.4) | collective-permute-done | bytes 215072 | tf_op jit(solution)/shard_map/ppermute | solution.py:94
  65.0 0.1 bitcast_add_fusion.1
  65.1 0.7 %slice_bitcast_fusion = f32[32,1536]{1,0:T(8,128)} fusion(f32[35,1,1536]{2,0,1:T(8,128)S(1)} %bitcast_add_fusion.1), kind=kLoop, calls=%fused_computation.32 | loop fusion | bytes 393216 | tf_op jit(solution)/shard_map/slice | solution.py:139
  65.8 0.6 slice_bitcast_fusion.3
  (16 shorter events, 0.3 us)
Async XLA Ops:
  2.5 22.0 %copy-start.2 = (bf16[32,6144]{1,0:T(8,128)(2,1)S(1)}, bf16[32,6144]{1,0:T(8,128)(2,1)}, u32[]{:S(2)}) copy-start(bf16[32,6144]{1,0:T(8,128)(2,1)} %param.6) | copy-start | bytes 1179652
  23.7 4.7 %copy-start = (bf16[512,6144]{1,0:T(8,128)(2,1)}, bf16[512,6144]{1,0:T(8,128)(2,1)S(1)}, u32[]{:S(2)}) copy-start(bf16[512,6144]{1,0:T(8,128)(2,1)S(1)} %get-tuple-element.5) | copy-start | bytes 18874372
  23.7 4.7 %copy-start.1 = (bf16[512,6144]{1,0:T(8,128)(2,1)}, bf16[512,6144]{1,0:T(8,128)(2,1)S(1)}, u32[]{:S(2)}) copy-start(bf16[512,6144]{1,0:T(8,128)(2,1)S(1)} %get-tuple-element.4) | copy-start | bytes 18874372
  24.4 18.5 %copy-start.3 = (f32[32]{0:T(128)S(1)}, f32[32]{0:T(128)}, u32[]{:S(2)}) copy-start(f32[32]{0:T(128)} %param.9) | copy-start | bytes 388
  28.4 6.5 %collective-permute-start = (f32[2,32,512]{2,1,0:T(8,128)S(1)}, f32[2,32,512]{2,1,0:T(8,128)S(1)}, u32[]{:S(2)}, u32[]{:S(2)}) collective-permute-start(f32[2,32,512]{2,1,0:T(8,128)S(1)} %pad_maximum_fusion.1), channel_id=1, source_target_pairs={{0,4},{4,0},{8,12},{12,8},{16,20},{20,16},{24,28},{28,24},{1,5},{5... | collective-permute-start | bytes 393224 | tf_op jit(solution)/shard_map/ppermute | solution.py:77
  35.0 5.0 %collective-permute-start.1 = (f32[2,32,512]{2,1,0:T(8,128)S(1)}, f32[2,32,512]{2,1,0:T(8,128)S(1)}, u32[]{:S(2)}, u32[]{:S(2)}) collective-permute-start(f32[2,32,512]{2,1,0:T(8,128)S(1)} %fusion.29), channel_id=1, source_target_pairs={{0,8},{4,12},{8,0},{12,4},{16,24},{20,28},{24,16},{28,20},{1,9},{5... | collective-permute-start | bytes 393224 | tf_op jit(solution)/shard_map/ppermute | solution.py:77
  40.0 7.3 %collective-permute-start.2 = (f32[2,32,512]{2,1,0:T(8,128)S(1)}, f32[2,32,512]{2,1,0:T(8,128)S(1)}, u32[]{:S(2)}, u32[]{:S(2)}) collective-permute-start(f32[2,32,512]{2,1,0:T(8,128)S(1)} %fusion.38), channel_id=1, source_target_pairs={{0,16},{4,20},{8,24},{12,28},{16,0},{20,4},{24,8},{28,12},{1,17},{... | collective-permute-start | bytes 393224 | tf_op jit(solution)/shard_map/ppermute | solution.py:77
  47.5 4.1 %slice-start = ((s8[6291456]{0:T(1024)(128)(4,1)}), s8[4194304]{0:T(1024)(128)(4,1)S(1)}, s32[]{:S(2)}) async-start(s8[6291456]{0:T(1024)(128)(4,1)} %bitcast.50), calls=%async_computation | async-start | bytes 8388608
  47.5 4.6 %slice-start.1 = ((s8[6291456]{0:T(1024)(128)(4,1)}), s8[2097152]{0:T(1024)(128)(4,1)S(1)}, s32[]{:S(2)}) async-start(s8[6291456]{0:T(1024)(128)(4,1)} %bitcast.50), calls=%async_computation.1 | async-start | bytes 4194304
  54.9 1.9 %collective-permute-start.3 = (f32[35,2,1536]{2,0,1:T(8,128)S(1)}, f32[35,2,1536]{2,0,1:T(8,128)S(1)}, u32[]{:S(2)}, u32[]{:S(2)}) collective-permute-start(f32[35,2,1536]{2,0,1:T(8,128)S(1)} %select_bitcast_fusion), channel_id=1, source_target_pairs={{0,1},{1,0},{2,3},{3,2},{4,5},{5,4},{6,7},{7,6},{8,9},{9,8},{10,11... | collective-permute-start | bytes 1290248 | tf_op jit(solution)/shard_map/ppermute | solution.py:94
  57.0 8.1 %collective-permute-start.4 = (f32[35,1,1536]{2,0,1:T(8,128)S(1)}, f32[35,1,1536]{2,0,1:T(8,128)S(1)}, u32[]{:S(2)}, u32[]{:S(2)}) collective-permute-start(f32[35,1,1536]{2,0,1:T(8,128)S(1)} %select_bitcast_fusion.1), channel_id=1, source_target_pairs={{0,2},{1,3},{2,0},{3,1},{4,6},{5,7},{6,4},{7,5},{8,10},{9,11},{10,... | collective-permute-start | bytes 645128 | tf_op jit(solution)/shard_map/ppermute | solution.py:94
where the time goes:
time: 66.6 us; the launch traced here: 66.4 us
  other arithmetic  22.9 us (34%)
  waiting for transfers between devices  19.2 us (29%)
  starting transfers between devices  9.62 us (14%)
  matrix products  8.92 us (13%)
  local copies, waits for them, and re-layouts  4.13 us (6%)
  between operations  1.58 us (2%)
    convert_element_type x1, other arithmetic, local(): sin_table = sin_f.astype(jnp.bfloat16)  21.2 us
    ppermute x3, waiting for transfers between devices, butterfly_sum(): x = x + lax.ppermute(x, axis, [(i, i ^ step) for i in range(n)])  11.1 us
    ppermute x2, waiting for transfers between devices, halving_scatter(): held = keep + lax.ppermute(send, axis, [(i, i ^ step) for i in range(n)])  8.1 us
    ppermute x3, starting transfers between devices, butterfly_sum(): x = x + lax.ppermute(x, axis, [(i, i ^ step) for i in range(n)])  7.77 us
    dot_general x1, matrix products, local(): field = jnp.dot(cos_side, cos_table, preferred_element_type=jnp.float32)  4 us
    dot_general x1, matrix products, local(): lax.dot_general(charge_live, cos_table, tensor_product, preferred_element...  1.97 us
    dot_general x1, matrix products, local(): lax.dot_general(charge_live, sin_table, tensor_product, preferred_element...  1.95 us
    ppermute x2, starting transfers between devices, halving_scatter(): held = keep + lax.ppermute(send, axis, [(i, i ^ step) for i in range(n)])  1.85 us
  transfers between devices with their start and end apart: 5, of which 5 were waited for; matrix products, arithmetic and copies ran while one was open for 0% of the time, Pallas kernels for 0%

commit v1 on v0

--- a/solution.py
+++ b/solution.py
@@ -106,28 +106,37 @@
         live = jnp.arange(n_local) < occupied_site_tally[0]
         charge_live = jnp.where(live[None, :], site_strengths, jnp.zeros_like(site_strengths))
         cartesian_mode_vector = miller_indices.astype(jnp.float32)
-        t = (
-            cartesian_mode_vector[0][:, None] * cell_coordinates_frac[0][None, :]
-            + cartesian_mode_vector[1][:, None] * cell_coordinates_frac[1][None, :]
-            + cartesian_mode_vector[2][:, None] * cell_coordinates_frac[2][None, :]
-        )
-        cos_f, sin_f = turns_cos_sin(t)
-        cos_table = cos_f.astype(jnp.bfloat16)
-        sin_table = sin_f.astype(jnp.bfloat16)
-        cos_table, sin_table = lax.optimization_barrier((cos_table, sin_table))
+        n_k = cartesian_mode_vector.shape[1]
+        chunk = 128 if n_k % 128 == 0 else n_k
         tensor_product = (((1,), (1,)), ((), ()))
-        s_cos = lax.dot_general(
-            charge_live, cos_table, tensor_product, preferred_element_type=jnp.float32
-        )
-        s_sin = lax.dot_general(
-            charge_live, sin_table, tensor_product, preferred_element_type=jnp.float32
-        )
-        s_both = butterfly_sum(jnp.stack([s_cos, s_sin], 0), "dom", n_dom)
-        cos_side, sin_side = reciprocal_filter_weight(
-            s_both[0], s_both[1], cartesian_mode_vector, gaussian_spread, atoms_total
-        )
-        field = jnp.dot(cos_side, cos_table, preferred_element_type=jnp.float32)
-        field = field + jnp.dot(sin_side, sin_table, preferred_element_type=jnp.float32)
+        field = None
+        pos = cell_coordinates_frac
+        for start in range(0, n_k, chunk):
+            mode = cartesian_mode_vector[:, start : start + chunk]
+            t = (
+                mode[0][:, None] * pos[0][None, :]
+                + mode[1][:, None] * pos[1][None, :]
+                + mode[2][:, None] * pos[2][None, :]
+            )
+            cos_f, sin_f = turns_cos_sin(t)
+            cos_table = cos_f.astype(jnp.bfloat16)
+            sin_table = sin_f.astype(jnp.bfloat16)
+            cos_table, sin_table = lax.optimization_barrier((cos_table, sin_table))
+            s_cos = lax.dot_general(
+                charge_live, cos_table, tensor_product, preferred_element_type=jnp.float32
+            )
+            s_sin = lax.dot_general(
+                charge_live, sin_table, tensor_product, preferred_element_type=jnp.float32
+            )
+            s_both = jnp.stack([s_cos, s_sin], 0)
+            pos, s_both = lax.optimization_barrier((pos, s_both))
+            s_both = butterfly_sum(s_both, "dom", n_dom)
+            cos_side, sin_side = reciprocal_filter_weight(
+                s_both[0], s_both[1], mode, gaussian_spread, atoms_total
+            )
+            part = jnp.dot(cos_side, cos_table, preferred_element_type=jnp.float32)
+            part = part + jnp.dot(sin_side, sin_table, preferred_element_type=jnp.float32)
+            field = part if field is None else field + part
         charge_f = charge_live.astype(jnp.float32)
         head = jnp.where(live[None, :], field[:channels], 0.0)
         force_rows = [

time: 66.6 us -> 83.2 us (1.25)
  other arithmetic: 22.9 us -> 34.3 us
  starting transfers between devices: 9.62 us -> 18.4 us
  waiting for transfers between devices: 19.2 us -> 10.8 us
  local copies, waits for them, and re-layouts: 4.13 us -> 7.61 us
    ppermute x3 -> x12, starting transfers between devices: 7.77 us -> 16.7 us  [butterfly_sum(): x = x + lax.ppermute(x, axis, [(i, i ^ step) for i in range(n)])]
    ppermute x3 -> x12, waiting for transfers between devices: 11.1 us -> 2.47 us  [butterfly_sum(): x = x + lax.ppermute(x, axis, [(i, i ^ step) for i in range(n)])]
    add x3 -> x12, other arithmetic: 0.07 us -> 5.65 us  [butterfly_sum(): x = x + lax.ppermute(x, axis, [(i, i ^ step) for i in range(n)])]
    another operation x3 -> x11, other arithmetic: 0.14 us -> 3.81 us
    unnamed x12 -> x44, local copies, waits for them, and re-layouts: 0.66 us -> 3.99 us
    dot_general x1 -> x4, matrix products: 4 us -> 2.24 us  [local(): part = jnp.dot(cos_side, cos_table, preferred_element_type=jnp.float32)]
    dot_general x1 -> x4, matrix products: 1 us -> 2.35 us  [local(): jnp.dot(sin_side, sin_table, preferred_element_type=jnp.float32)]
    dot_general x1 -> x4, matrix products: 1.97 us -> 2.52 us  [local(): lax.dot_general(charge_live, cos_table, tensor_product, preferred_element...]
  transfers between devices with their start and end apart: 5 -> 14, of which waited for: 5 -> 3; matrix products, arithmetic and copies ran while one was open for 0% -> 34% of each run, Pallas kernels for 0% -> 0%
where the time goes in v1:
time: 83.2 us; the launch traced here: 82.6 us
  other arithmetic  34.3 us (41%)
  starting transfers between devices  18.4 us (22%)
  waiting for transfers between devices  10.8 us (13%)
  matrix products  9.56 us (11%)
  local copies, waits for them, and re-layouts  7.61 us (9%)
  between operations  1.91 us (2%)
    convert_element_type x4, other arithmetic, local(): sin_table = sin_f.astype(jnp.bfloat16)  21.5 us
    ppermute x12, starting transfers between devices, butterfly_sum(): x = x + lax.ppermute(x, axis, [(i, i ^ step) for i in range(n)])  16.7 us
    ppermute x2, waiting for transfers between devices, halving_scatter(): held = keep + lax.ppermute(send, axis, [(i, i ^ step) for i in range(n)])  8.33 us
    add x12, other arithmetic, butterfly_sum(): x = x + lax.ppermute(x, axis, [(i, i ^ step) for i in range(n)])  5.65 us
    unnamed x44, local copies, waits for them, and re-layouts  3.99 us
    another operation x7, other arithmetic  3.76 us
    dot_general x4, matrix products, local(): lax.dot_general(charge_live, cos_table, tensor_product, preferred_element...  2.52 us
    ppermute x12, waiting for transfers between devices, butterfly_sum(): x = x + lax.ppermute(x, axis, [(i, i ^ step) for i in range(n)])  2.47 us
  transfers between devices with their start and end apart: 14, of which 3 were waited for; matrix products, arithmetic and copies ran while one was open for 34% of the time, Pallas kernels for 0%

profile of v1, /device:TPU:0, one launch (start us, length us, event | category | flops | bytes accessed | tf_op | source)
XLA Modules:
  0.0 82.6 jit_solution(11581278306276903595)
XLA Ops:
  0.6 0.8 convert_element_type.38
  1.4 0.6 multiply_bitcast_fusion.1
  2.6 1.1 %fusion.114 = (f32[1,6144]{1,0:T(1,128)S(1)}, f32[1,6144]{1,0:T(1,128)S(1)}, f32[1,6144]{1,0:T(1,128)S(1)}) fusion(f32[3,6144]{1,0:T(4,128)} %param.5), kind=kLoop, calls=%fused_computation.260 | loop fusion | bytes 147456 | tf_op jit(solution)/shard_map/slice | solution.py:117
  3.8 5.3 %fusion.4 = (bf16[128,6144]{1,0:T(8,128)(2,1)S(1)}, bf16[128,6144]{1,0:T(8,128)(2,1)S(1)}) fusion(f32[6144]{0:T(1024)S(1)} %bitcast.188, f32[128]{0:T(128)S(1)} %get-tuple-element.117, f32[6144]{0:T(1024)S(1)} %bitcast.187, f32[128]{0:T(128)S(1)} %get-tuple-element.152, f32[6144]{0:T(1024)S(1)} %bitcast.186, f32[128]{0:T(128)S(1)} %get-tuple-element.153), kind=kLoop, calls=%fused_computation.16 | loop fusion | flops 36175872 | bytes 3220992 | tf_op jit(solution)/shard_map/convert_element_type | solution.py:123
  9.8 0.6 convolution_bitcast_fusion.6
  10.4 0.6 convolution_bitcast_fusion.7
  11.0 3.0 %collective-permute-start = (f32[2,32,128]{2,1,0:T(8,128)S(1)}, f32[2,32,128]{2,1,0:T(8,128)S(1)}, u32[]{:S(2)}, u32[]{:S(2)}) collective-permute-start(f32[2,32,128]{2,1,0:T(8,128)S(1)} %pad_maximum_fusion.1), channel_id=1, source_target_pairs={{0,4},{4,0},{8,12},{12,8},{16,20},{20,16},{24,28},{28,24},{1,5},{5... | collective-permute-start | bytes 98312 | tf_op jit(solution)/shard_map/ppermute | solution.py:77
  14.1 0.6 multiply_bitcast_fusion
  14.8 5.3 %fusion.6 = (bf16[128,6144]{1,0:T(8,128)(2,1)S(1)}, bf16[128,6144]{1,0:T(8,128)(2,1)S(1)}) fusion(f32[6144]{0:T(1024)S(1)} %bitcast.190, f32[128]{0:T(128)S(1)} %get-tuple-element.124, f32[6144]{0:T(1024)S(1)} %bitcast.191, f32[128]{0:T(128)S(1)} %get-tuple-element.148, f32[6144]{0:T(1024)S(1)} %bitcast.189, f32[128]{0:T(128)S(1)} %get-tuple-element.149), kind=kLoop, calls=%fused_computation.18 | loop fusion | flops 36175872 | bytes 3220992 | tf_op jit(solution)/shard_map/convert_element_type | solution.py:123
  20.1 0.6 convolution_bitcast_fusion.4
  20.7 0.6 convolution_bitcast_fusion.5
  21.5 5.3 %fusion.8 = (bf16[128,6144]{1,0:T(8,128)(2,1)S(1)}, bf16[128,6144]{1,0:T(8,128)(2,1)S(1)}) fusion(f32[6144]{0:T(1024)S(1)} %bitcast.193, f32[128]{0:T(128)S(1)} %get-tuple-element.132, f32[6144]{0:T(1024)S(1)} %bitcast.194, f32[128]{0:T(128)S(1)} %get-tuple-element.146, f32[6144]{0:T(1024)S(1)} %bitcast.192, f32[128]{0:T(128)S(1)} %get-tuple-element.147), kind=kLoop, calls=%fused_computation.20 | loop fusion | flops 36175872 | bytes 3220992 | tf_op jit(solution)/shard_map/convert_element_type | solution.py:123
  26.8 0.6 convolution_bitcast_fusion.2
  27.4 0.6 convolution_bitcast_fusion.3
  28.2 5.5 %fusion.10 = (bf16[128,6144]{1,0:T(8,128)(2,1)S(1)}, bf16[128,6144]{1,0:T(8,128)(2,1)S(1)}) fusion(f32[6144]{0:T(1024)S(1)} %bitcast.196, f32[128]{0:T(128)S(1)} %get-tuple-element.138, f32[6144]{0:T(1024)S(1)} %bitcast.197, f32[128]{0:T(128)S(1)} %get-tuple-element.142, f32[6144]{0:T(1024)S(1)} %bitcast.195, f32[128]{0:T(128)S(1)} %get-tuple-element.143), kind=kLoop, calls=%fused_computation.22 | loop fusion | flops 36175872 | bytes 3220992 | tf_op jit(solution)/shard_map/convert_element_type | solution.py:123
  33.7 0.6 convolution_bitcast_fusion
  34.9 0.6 convolution_bitcast_fusion.1
  35.6 2.0 %collective-permute-start.3 = (f32[2,32,128]{2,1,0:T(8,128)S(1)}, f32[2,32,128]{2,1,0:T(8,128)S(1)}, u32[]{:S(2)}, u32[]{:S(2)}) collective-permute-start(f32[2,32,128]{2,1,0:T(8,128)S(1)} %pad_maximum_fusion.2), channel_id=1, source_target_pairs={{0,4},{4,0},{8,12},{12,8},{16,20},{20,16},{24,28},{28,24},{1,5},{5... | collective-permute-start | bytes 98312 | tf_op jit(solution)/shard_map/ppermute | solution.py:77
  37.7 2.1 %collective-permute-start.1 = (f32[2,32,128]{2,1,0:T(8,128)S(1)}, f32[2,32,128]{2,1,0:T(8,128)S(1)}, u32[]{:S(2)}, u32[]{:S(2)}) collective-permute-start(f32[2,32,128]{2,1,0:T(8,128)S(1)} %add.272), channel_id=1, source_target_pairs={{0,8},{4,12},{8,0},{12,4},{16,24},{20,28},{24,16},{28,20},{1,9},{5... | collective-permute-start | bytes 98312 | tf_op jit(solution)/shard_map/ppermute | solution.py:77
  39.8 0.6 add.328
  40.4 1.6 %collective-permute-start.10 = (f32[2,32,128]{2,1,0:T(8,128)}, f32[2,32,128]{2,1,0:T(8,128)}, u32[]{:S(2)}, u32[]{:S(2)}) collective-permute-start(f32[2,32,128]{2,1,0:T(8,128)} %add.328), channel_id=1, source_target_pairs={{0,8},{4,12},{8,0},{12,4},{16,24},{20,28},{24,16},{28,20},{1,9},{5... | collective-permute-start | bytes 98312 | tf_op jit(solution)/shard_map/ppermute | solution.py:77
  42.0 0.6 add.290
  43.1 0.6 add.309
  43.7 1.6 %collective-permute-start.7 = (f32[2,32,128]{2,1,0:T(8,128)}, f32[2,32,128]{2,1,0:T(8,128)}, u32[]{:S(2)}, u32[]{:S(2)}) collective-permute-start(f32[2,32,128]{2,1,0:T(8,128)} %add.309), channel_id=1, source_target_pairs={{0,8},{4,12},{8,0},{12,4},{16,24},{20,28},{24,16},{28,20},{1,9},{5... | collective-permute-start | bytes 98312 | tf_op jit(solution)/shard_map/ppermute | solution.py:77
  45.3 0.6 add.273
  45.9 2.6 %collective-permute-start.2 = (f32[2,32,128]{2,1,0:T(8,128)}, f32[2,32,128]{2,1,0:T(8,128)}, u32[]{:S(2)}, u32[]{:S(2)}) collective-permute-start(f32[2,32,128]{2,1,0:T(8,128)} %add.273), channel_id=1, source_target_pairs={{0,16},{4,20},{8,24},{12,28},{16,0},{20,4},{24,8},{28,12},{1,17},{... | collective-permute-start | bytes 98312 | tf_op jit(solution)/shard_map/ppermute | solution.py:77
  48.5 0.8 add.329
  49.7 0.8 add.291
  50.4 2.6 %collective-permute-start.5 = (f32[2,32,128]{2,1,0:T(8,128)S(1)}, f32[2,32,128]{2,1,0:T(8,128)S(1)}, u32[]{:S(2)}, u32[]{:S(2)}) collective-permute-start(f32[2,32,128]{2,1,0:T(8,128)S(1)} %add.291), channel_id=1, source_target_pairs={{0,16},{4,20},{8,24},{12,28},{16,0},{20,4},{24,8},{28,12},{1,17},{... | collective-permute-start | bytes 98312 | tf_op jit(solution)/shard_map/ppermute | solution.py:77
  53.0 0.8 add.310
  54.2 0.8 add.274
  54.9 0.8 multiply_convert_fusion.20
  55.7 0.7 multiply_convert_fusion.23
  56.4 2.4 %collective-permute-done.8 = f32[2,32,128]{2,1,0:T(8,128)S(1)} collective-permute-done((f32[2,32,128]{2,1,0:T(8,128)S(1)}, f32[2,32,128]{2,1,0:T(8,128)S(1)}, u32[]{:S(2)}, u32[]{:S(2)}) %collective-permute-start.8) | collective-permute-done | bytes 32800 | tf_op jit(solution)/shard_map/ppermute | solution.py:77
  58.9 0.8 multiply_convert_fusion.2
  59.6 0.7 multiply_convert_fusion.17
  61.0 0.8 multiply_convert_fusion.11
  63.1 0.7 copy-done.4
  64.5 0.6 convolution_add_fusion.3
  65.1 0.8 copy-done.8
  66.5 0.8 copy-done.10
  67.9 0.8 copy-done.12
  70.0 0.7 concatenate.52
  71.2 1.8 %collective-permute-done.12 = f32[35,2,1536]{2,0,1:T(8,128)S(1)} collective-permute-done((f32[35,2,1536]{2,0,1:T(8,128)S(1)}, f32[35,2,1536]{2,0,1:T(8,128)S(1)}, u32[]{:S(2)}, u32[]{:S(2)}) %collective-permute-start.12) | collective-permute-done | bytes 430112 | tf_op jit(solution)/shard_map/ppermute | solution.py:94
  73.1 1.6 %collective-permute-start.13 = (f32[35,1,1536]{2,0,1:T(8,128)S(1)}, f32[35,1,1536]{2,0,1:T(8,128)S(1)}, u32[]{:S(2)}, u32[]{:S(2)}) collective-permute-start(f32[35,1,1536]{2,0,1:T(8,128)S(1)} %select_bitcast_fusion.1), channel_id=1, source_target_pairs={{0,2},{1,3},{2,0},{3,1},{4,6},{5,7},{6,4},{7,5},{8,10},{9,11},{10,... | collective-permute-start | bytes 645128 | tf_op jit(solution)/shard_map/ppermute | solution.py:94
  74.7 6.5 %collective-permute-done.13 = f32[35,1,1536]{2,0,1:T(8,128)S(1)} collective-permute-done((f32[35,1,1536]{2,0,1:T(8,128)S(1)}, f32[35,1,1536]{2,0,1:T(8,128)S(1)}, u32[]{:S(2)}, u32[]{:S(2)}) %collective-permute-start.13) | collective-permute-done | bytes 215072 | tf_op jit(solution)/shard_map/ppermute | solution.py:94
  81.3 0.7 slice_bitcast_fusion
  81.9 0.6 slice_bitcast_fusion.1
  (93 shorter events, 8.3 us)
Async XLA Ops:
  0.6 9.1 %copy-start = (bf16[32,6144]{1,0:T(8,128)(2,1)S(1)}, bf16[32,6144]{1,0:T(8,128)(2,1)}, u32[]{:S(2)}) copy-start(bf16[32,6144]{1,0:T(8,128)(2,1)} %param.6) | copy-start | bytes 1179652
  3.7 11.0 %copy-start.13 = (f32[3,6144]{1,0:T(4,128)S(1)}, f32[3,6144]{1,0:T(4,128)}, u32[]{:S(2)}) copy-start(f32[3,6144]{1,0:T(4,128)} %param.5) | copy-start | bytes 221188
  9.1 11.0 %copy-start.5 = (bf16[128,6144]{1,0:T(8,128)(2,1)}, bf16[128,6144]{1,0:T(8,128)(2,1)S(1)}, u32[]{:S(2)}) copy-start(bf16[128,6144]{1,0:T(8,128)(2,1)S(1)} %get-tuple-element.18) | copy-start | bytes 4718596
  11.0 26.7 %collective-permute-start = (f32[2,32,128]{2,1,0:T(8,128)S(1)}, f32[2,32,128]{2,1,0:T(8,128)S(1)}, u32[]{:S(2)}, u32[]{:S(2)}) collective-permute-start(f32[2,32,128]{2,1,0:T(8,128)S(1)} %pad_maximum_fusion.1), channel_id=1, source_target_pairs={{0,4},{4,0},{8,12},{12,8},{16,20},{20,16},{24,28},{28,24},{1,5},{5... | collective-permute-start | bytes 98312 | tf_op jit(solution)/shard_map/ppermute | solution.py:77
  20.1 6.7 %copy-start.7 = (bf16[128,6144]{1,0:T(8,128)(2,1)}, bf16[128,6144]{1,0:T(8,128)(2,1)S(1)}, u32[]{:S(2)}) copy-start(bf16[128,6144]{1,0:T(8,128)(2,1)S(1)} %get-tuple-element.22) | copy-start | bytes 4718596
  26.8 6.9 %copy-start.1 = (bf16[128,6144]{1,0:T(8,128)(2,1)}, bf16[128,6144]{1,0:T(8,128)(2,1)S(1)}, u32[]{:S(2)}) copy-start(bf16[128,6144]{1,0:T(8,128)(2,1)S(1)} %get-tuple-element.25) | copy-start | bytes 4718596
  26.8 6.9 %copy-start.9 = (bf16[128,6144]{1,0:T(8,128)(2,1)}, bf16[128,6144]{1,0:T(8,128)(2,1)S(1)}, u32[]{:S(2)}) copy-start(bf16[128,6144]{1,0:T(8,128)(2,1)S(1)} %get-tuple-element.26) | copy-start | bytes 4718596
  28.1 20.4 %copy-start.21 = (f32[32]{0:T(128)S(1)}, f32[32]{0:T(128)}, u32[]{:S(2)}) copy-start(f32[32]{0:T(128)} %param.9) | copy-start | bytes 388
  33.7 1.2 %copy-start.3 = (bf16[128,6144]{1,0:T(8,128)(2,1)}, bf16[128,6144]{1,0:T(8,128)(2,1)S(1)}, u32[]{:S(2)}) copy-start(bf16[128,6144]{1,0:T(8,128)(2,1)S(1)} %get-tuple-element.29) | copy-start | bytes 4718596
  33.7 1.8 %copy-start.11 = (bf16[128,6144]{1,0:T(8,128)(2,1)}, bf16[128,6144]{1,0:T(8,128)(2,1)S(1)}, u32[]{:S(2)}) copy-start(bf16[128,6144]{1,0:T(8,128)(2,1)S(1)} %get-tuple-element.30) | copy-start | bytes 4718596
  35.5 4.3 %collective-permute-start.9 = (f32[2,32,128]{2,1,0:T(8,128)S(1)}, f32[2,32,128]{2,1,0:T(8,128)S(1)}, u32[]{:S(2)}, u32[]{:S(2)}) collective-permute-start(f32[2,32,128]{2,1,0:T(8,128)S(1)} %pad_maximum_fusion.4), channel_id=1, source_target_pairs={{0,4},{4,0},{8,12},{12,8},{16,20},{20,16},{24,28},{28,24},{1,5},{5... | collective-permute-start | bytes 98312 | tf_op jit(solution)/shard_map/ppermute | solution.py:77
  35.6 6.4 %collective-permute-start.3 = (f32[2,32,128]{2,1,0:T(8,128)S(1)}, f32[2,32,128]{2,1,0:T(8,128)S(1)}, u32[]{:S(2)}, u32[]{:S(2)}) collective-permute-start(f32[2,32,128]{2,1,0:T(8,128)S(1)} %pad_maximum_fusion.2), channel_id=1, source_target_pairs={{0,4},{4,0},{8,12},{12,8},{16,20},{20,16},{24,28},{28,24},{1,5},{5... | collective-permute-start | bytes 98312 | tf_op jit(solution)/shard_map/ppermute | solution.py:77
  37.6 5.5 %collective-permute-start.6 = (f32[2,32,128]{2,1,0:T(8,128)S(1)}, f32[2,32,128]{2,1,0:T(8,128)S(1)}, u32[]{:S(2)}, u32[]{:S(2)}) collective-permute-start(f32[2,32,128]{2,1,0:T(8,128)S(1)} %pad_maximum_fusion.3), channel_id=1, source_target_pairs={{0,4},{4,0},{8,12},{12,8},{16,20},{20,16},{24,28},{28,24},{1,5},{5... | collective-permute-start | bytes 98312 | tf_op jit(solution)/shard_map/ppermute | solution.py:77
  37.7 7.6 %collective-permute-start.1 = (f32[2,32,128]{2,1,0:T(8,128)S(1)}, f32[2,32,128]{2,1,0:T(8,128)S(1)}, u32[]{:S(2)}, u32[]{:S(2)}) collective-permute-start(f32[2,32,128]{2,1,0:T(8,128)S(1)} %add.272), channel_id=1, source_target_pairs={{0,8},{4,12},{8,0},{12,4},{16,24},{20,28},{24,16},{28,20},{1,9},{5... | collective-permute-start | bytes 98312 | tf_op jit(solution)/shard_map/ppermute | solution.py:77
  40.4 8.1 %collective-permute-start.10 = (f32[2,32,128]{2,1,0:T(8,128)}, f32[2,32,128]{2,1,0:T(8,128)}, u32[]{:S(2)}, u32[]{:S(2)}) collective-permute-start(f32[2,32,128]{2,1,0:T(8,128)} %add.328), channel_id=1, source_target_pairs={{0,8},{4,12},{8,0},{12,4},{16,24},{20,28},{24,16},{28,20},{1,9},{5... | collective-permute-start | bytes 98312 | tf_op jit(solution)/shard_map/ppermute | solution.py:77
  42.6 7.0 %collective-permute-start.4 = (f32[2,32,128]{2,1,0:T(8,128)}, f32[2,32,128]{2,1,0:T(8,128)}, u32[]{:S(2)}, u32[]{:S(2)}) collective-permute-start(f32[2,32,128]{2,1,0:T(8,128)} %add.290), channel_id=1, source_target_pairs={{0,8},{4,12},{8,0},{12,4},{16,24},{20,28},{24,16},{28,20},{1,9},{5... | collective-permute-start | bytes 98312 | tf_op jit(solution)/shard_map/ppermute | solution.py:77
  43.7 9.3 %collective-permute-start.7 = (f32[2,32,128]{2,1,0:T(8,128)}, f32[2,32,128]{2,1,0:T(8,128)}, u32[]{:S(2)}, u32[]{:S(2)}) collective-permute-start(f32[2,32,128]{2,1,0:T(8,128)} %add.309), channel_id=1, source_target_pairs={{0,8},{4,12},{8,0},{12,4},{16,24},{20,28},{24,16},{28,20},{1,9},{5... | collective-permute-start | bytes 98312 | tf_op jit(solution)/shard_map/ppermute | solution.py:77
  45.9 8.2 %collective-permute-start.2 = (f32[2,32,128]{2,1,0:T(8,128)}, f32[2,32,128]{2,1,0:T(8,128)}, u32[]{:S(2)}, u32[]{:S(2)}) collective-permute-start(f32[2,32,128]{2,1,0:T(8,128)} %add.273), channel_id=1, source_target_pairs={{0,16},{4,20},{8,24},{12,28},{16,0},{20,4},{24,8},{28,12},{1,17},{... | collective-permute-start | bytes 98312 | tf_op jit(solution)/shard_map/ppermute | solution.py:77
  49.3 7.1 %collective-permute-start.11 = (f32[2,32,128]{2,1,0:T(8,128)S(1)}, f32[2,32,128]{2,1,0:T(8,128)S(1)}, u32[]{:S(2)}, u32[]{:S(2)}) collective-permute-start(f32[2,32,128]{2,1,0:T(8,128)S(1)} %add.329), channel_id=1, source_target_pairs={{0,16},{4,20},{8,24},{12,28},{16,0},{20,4},{24,8},{28,12},{1,17},{... | collective-permute-start | bytes 98312 | tf_op jit(solution)/shard_map/ppermute | solution.py:77
  50.4 6.0 %collective-permute-start.5 = (f32[2,32,128]{2,1,0:T(8,128)S(1)}, f32[2,32,128]{2,1,0:T(8,128)S(1)}, u32[]{:S(2)}, u32[]{:S(2)}) collective-permute-start(f32[2,32,128]{2,1,0:T(8,128)S(1)} %add.291), channel_id=1, source_target_pairs={{0,16},{4,20},{8,24},{12,28},{16,0},{20,4},{24,8},{28,12},{1,17},{... | collective-permute-start | bytes 98312 | tf_op jit(solution)/shard_map/ppermute | solution.py:77
  53.8 5.1 %collective-permute-start.8 = (f32[2,32,128]{2,1,0:T(8,128)S(1)}, f32[2,32,128]{2,1,0:T(8,128)S(1)}, u32[]{:S(2)}, u32[]{:S(2)}) collective-permute-start(f32[2,32,128]{2,1,0:T(8,128)S(1)} %add.310), channel_id=1, source_target_pairs={{0,16},{4,20},{8,24},{12,28},{16,0},{20,4},{24,8},{28,12},{1,17},{... | collective-permute-start | bytes 98312 | tf_op jit(solution)/shard_map/ppermute | solution.py:77
  60.9 1.5 %copy-start.14 = (f32[128]{0:T(128)S(1)}, f32[128]{0:T(128)}, u32[]{:S(2)}) copy-start(f32[128]{0:T(128)} %get-tuple-element.112) | copy-start | bytes 1540
  60.9 1.5 %copy-start.15 = (f32[128]{0:T(128)S(1)}, f32[128]{0:T(128)}, u32[]{:S(2)}) copy-start(f32[128]{0:T(128)} %get-tuple-element.130) | copy-start | bytes 1540
  60.9 1.5 %copy-start.19 = (f32[128]{0:T(128)S(1)}, f32[128]{0:T(128)}, u32[]{:S(2)}) copy-start(f32[128]{0:T(128)} %get-tuple-element.131) | copy-start | bytes 1540
  60.9 1.5 %copy-start.20 = (f32[128]{0:T(128)S(1)}, f32[128]{0:T(128)}, u32[]{:S(2)}) copy-start(f32[128]{0:T(128)} %get-tuple-element.134) | copy-start | bytes 1540
  60.9 1.5 %copy-start.2 = (bf16[128,6144]{1,0:T(8,128)(2,1)S(1)}, bf16[128,6144]{1,0:T(8,128)(2,1)}, u32[]{:S(2)}) copy-start(bf16[128,6144]{1,0:T(8,128)(2,1)} %copy-done.1) | copy-start | bytes 4718596
  62.3 0.7 copy-start.16
  62.3 0.7 copy-start.17
  62.4 0.7 copy-start.18
  62.4 1.4 %copy-start.4 = (bf16[128,6144]{1,0:T(8,128)(2,1)S(1)}, bf16[128,6144]{1,0:T(8,128)(2,1)}, u32[]{:S(2)}) copy-start(bf16[128,6144]{1,0:T(8,128)(2,1)} %copy-done.3) | copy-start | bytes 4718596
  63.0 1.5 %copy-start.6 = (bf16[128,6144]{1,0:T(8,128)(2,1)S(1)}, bf16[128,6144]{1,0:T(8,128)(2,1)}, u32[]{:S(2)}) copy-start(bf16[128,6144]{1,0:T(8,128)(2,1)} %copy-done.5) | copy-start | bytes 4718596
  64.5 1.4 %copy-start.8 = (bf16[128,6144]{1,0:T(8,128)(2,1)S(1)}, bf16[128,6144]{1,0:T(8,128)(2,1)}, u32[]{:S(2)}) copy-start(bf16[128,6144]{1,0:T(8,128)(2,1)} %copy-done.7) | copy-start | bytes 4718596
  65.9 1.4 %copy-start.10 = (bf16[128,6144]{1,0:T(8,128)(2,1)S(1)}, bf16[128,6144]{1,0:T(8,128)(2,1)}, u32[]{:S(2)}) copy-start(bf16[128,6144]{1,0:T(8,128)(2,1)} %copy-done.9) | copy-start | bytes 4718596
  67.4 1.4 %copy-start.12 = (bf16[128,6144]{1,0:T(8,128)(2,1)S(1)}, bf16[128,6144]{1,0:T(8,128)(2,1)}, u32[]{:S(2)}) copy-start(bf16[128,6144]{1,0:T(8,128)(2,1)} %copy-done.11) | copy-start | bytes 4718596
  71.1 1.9 %collective-permute-start.12 = (f32[35,2,1536]{2,0,1:T(8,128)S(1)}, f32[35,2,1536]{2,0,1:T(8,128)S(1)}, u32[]{:S(2)}, u32[]{:S(2)}) collective-permute-start(f32[35,2,1536]{2,0,1:T(8,128)S(1)} %select_bitcast_fusion), channel_id=1, source_target_pairs={{0,1},{1,0},{2,3},{3,2},{4,5},{5,4},{6,7},{7,6},{8,9},{9,8},{10,11... | collective-permute-start | bytes 1290248 | tf_op jit(solution)/shard_map/ppermute | solution.py:94
  73.1 8.1 %collective-permute-start.13 = (f32[35,1,1536]{2,0,1:T(8,128)S(1)}, f32[35,1,1536]{2,0,1:T(8,128)S(1)}, u32[]{:S(2)}, u32[]{:S(2)}) collective-permute-start(f32[35,1,1536]{2,0,1:T(8,128)S(1)} %select_bitcast_fusion.1), channel_id=1, source_target_pairs={{0,2},{1,3},{2,0},{3,1},{4,6},{5,7},{6,4},{7,5},{8,10},{9,11},{10,... | collective-permute-start | bytes 645128 | tf_op jit(solution)/shard_map/ppermute | solution.py:94

commit v2 on v0

--- a/solution.py
+++ b/solution.py
@@ -3,6 +3,7 @@
 import jax
 import jax.numpy as jnp
 from jax import lax
+from jax.experimental import pallas as pl
 from jax.sharding import PartitionSpec as P
 
 two_pi = 6.283185307179586
@@ -30,6 +31,57 @@
     cos_out = jnp.where((q == 1.0) | (jnp.abs(q) == 2.0), -cos_mag, cos_mag)
     sin_out = jnp.where((q == -1.0) | (jnp.abs(q) == 2.0), -sin_mag, sin_mag)
     return cos_out, sin_out
+
+
+ROWS = 16
+def table_kernel(mode_ref, pos_ref, q_ref, cos_ref, sin_ref, sc_ref, ss_ref):
+    @pl.when(pl.program_id(0) == 0)
+    def _():
+        sc_ref[...] = jnp.zeros_like(sc_ref)
+        ss_ref[...] = jnp.zeros_like(ss_ref)
+    x = pos_ref[0:1, :]
+    y = pos_ref[1:2, :]
+    z = pos_ref[2:3, :]
+    def body(g, carry):
+        r0 = pl.multiple_of(g * ROWS, ROWS)
+        m = mode_ref[pl.ds(r0, ROWS), :]
+        t = m[:, 0:1] * x + m[:, 1:2] * y + m[:, 2:3] * z
+        c, s = turns_cos_sin(t)
+        cos_ref[pl.ds(r0, ROWS), :] = c.astype(jnp.bfloat16)
+        sin_ref[pl.ds(r0, ROWS), :] = s.astype(jnp.bfloat16)
+        return carry
+    lax.fori_loop(0, cos_ref.shape[0] // ROWS, body, 0)
+    nt = (((1,), (1,)), ((), ()))
+    q = q_ref[...]
+    sc_ref[...] += lax.dot_general(q, cos_ref[...], nt, preferred_element_type=jnp.float32)
+    ss_ref[...] += lax.dot_general(q, sin_ref[...], nt, preferred_element_type=jnp.float32)
+
+def tables_and_sums(mode_t, pos, charge, block=1536):
+    n_k = mode_t.shape[0]
+    n_at = pos.shape[1]
+    ch = charge.shape[0]
+    nb = n_at // block
+    return pl.pallas_call(
+        table_kernel,
+        grid=(nb,),
+        in_specs=[
+            pl.BlockSpec((n_k, 3), lambda j: (0, 0)),
+            pl.BlockSpec((3, block), lambda j: (0, j)),
+            pl.BlockSpec((ch, block), lambda j: (0, j)),
+        ],
+        out_specs=[
+            pl.BlockSpec((n_k, block), lambda j: (0, j)),
+            pl.BlockSpec((n_k, block), lambda j: (0, j)),
+            pl.BlockSpec((ch, n_k), lambda j: (0, 0)),
+            pl.BlockSpec((ch, n_k), lambda j: (0, 0)),
+        ],
+        out_shape=[
+            jax.ShapeDtypeStruct((n_k, n_at), jnp.bfloat16),
+            jax.ShapeDtypeStruct((n_k, n_at), jnp.bfloat16),
+            jax.ShapeDtypeStruct((ch, n_k), jnp.float32),
+            jax.ShapeDtypeStruct((ch, n_k), jnp.float32),
+        ],
+    )(mode_t, pos, charge)
 
 
 def reciprocal_filter_weight(s_cos, s_sin, cartesian_mode_vector, gaussian_spread, atoms_total):
@@ -106,21 +158,8 @@
         live = jnp.arange(n_local) < occupied_site_tally[0]
         charge_live = jnp.where(live[None, :], site_strengths, jnp.zeros_like(site_strengths))
         cartesian_mode_vector = miller_indices.astype(jnp.float32)
-        t = (
-            cartesian_mode_vector[0][:, None] * cell_coordinates_frac[0][None, :]
-            + cartesian_mode_vector[1][:, None] * cell_coordinates_frac[1][None, :]
-            + cartesian_mode_vector[2][:, None] * cell_coordinates_frac[2][None, :]
-        )
-        cos_f, sin_f = turns_cos_sin(t)
-        cos_table = cos_f.astype(jnp.bfloat16)
-        sin_table = sin_f.astype(jnp.bfloat16)
-        cos_table, sin_table = lax.optimization_barrier((cos_table, sin_table))
-        tensor_product = (((1,), (1,)), ((), ()))
-        s_cos = lax.dot_general(
-            charge_live, cos_table, tensor_product, preferred_element_type=jnp.float32
-        )
-        s_sin = lax.dot_general(
-            charge_live, sin_table, tensor_product, preferred_element_type=jnp.float32
+        cos_table, sin_table, s_cos, s_sin = tables_and_sums(
+            cartesian_mode_vector.T, cell_coordinates_frac, charge_live
         )
         s_both = butterfly_sum(jnp.stack([s_cos, s_sin], 0), "dom", n_dom)
         cos_side, sin_side = reciprocal_filter_weight(

time: 66.6 us -> 83.8 us (1.26)
  Pallas kernels: 0 us -> 38 us
  other arithmetic: 22.9 us -> 8.74 us
  matrix products: 8.92 us -> 5 us
  waiting for transfers between devices: 19.2 us -> 16.6 us
    pallas_call x0 -> x1, Pallas kernels: none -> 38 us  [tables_and_sums(): pl.pallas_call(table_kernel, grid=(nb,), in_specs=[pl.BlockSpec((n_k, 3),...]
    convert_element_type x1 -> x0, other arithmetic: 21.2 us -> none  [local(): sin_table = sin_f.astype(jnp.bfloat16)]
    dot_general x2 -> x0, matrix products: 3.92 us -> none  [the longest x1 1.97 us: local(): lax.dot_general(charge_live, cos_table, tensor_product, preferred_element...]
    ppermute x3, waiting for transfers between devices: 11.1 us -> 8.46 us  [butterfly_sum(): x = x + lax.ppermute(x, axis, [(i, i ^ step) for i in range(n)])]
    mul x1, other arithmetic: 0.02 us -> 1.99 us  [reciprocal_filter_weight(): scale * cartesian_mode_vector[0] * partial_first_term]
    select_n x0 -> x1, other arithmetic: none -> 1.81 us  [local(): jnp.where(live[None, :], site_strengths, jnp.zeros_like(site_strengths))]
    add x3, other arithmetic: 0.07 us -> 1.81 us  [butterfly_sum(): x = x + lax.ppermute(x, axis, [(i, i ^ step) for i in range(n)])]
    slice x1 -> x0, local copies, waits for them, and re-layouts: 1.12 us -> none  [local(): cell_coordinates_frac[0][None, :]]
  transfers between devices with their start and end apart: 5 -> 5, of which waited for: 5 -> 5; matrix products, arithmetic and copies ran while one was open for 0% -> 3% of each run, Pallas kernels for 0% -> 0%
where the time goes in v2:
time: 83.8 us; the launch traced here: 83.3 us
  Pallas kernels  38 us (45%)
  waiting for transfers between devices  16.6 us (20%)
  starting transfers between devices  9.63 us (11%)
  other arithmetic  8.74 us (10%)
  matrix products  5 us (6%)
  local copies, waits for them, and re-layouts  3.87 us (5%)
  between operations  1.5 us (2%)
    pallas_call x1, Pallas kernels, tables_and_sums(): pl.pallas_call(table_kernel, grid=(nb,), in_specs=[pl.BlockSpec((n_k, 3),...  38 us
    ppermute x3, waiting for transfers between devices, butterfly_sum(): x = x + lax.ppermute(x, axis, [(i, i ^ step) for i in range(n)])  8.46 us
    ppermute x2, waiting for transfers between devices, halving_scatter(): held = keep + lax.ppermute(send, axis, [(i, i ^ step) for i in range(n)])  8.09 us
    ppermute x3, starting transfers between devices, butterfly_sum(): x = x + lax.ppermute(x, axis, [(i, i ^ step) for i in range(n)])  7.77 us
    dot_general x1, matrix products, local(): field = jnp.dot(cos_side, cos_table, preferred_element_type=jnp.float32)  4 us
    mul x1, other arithmetic, reciprocal_filter_weight(): scale * cartesian_mode_vector[0] * partial_first_term  1.99 us
    ppermute x2, starting transfers between devices, halving_scatter(): held = keep + lax.ppermute(send, axis, [(i, i ^ step) for i in range(n)])  1.86 us
    select_n x1, other arithmetic, local(): jnp.where(live[None, :], site_strengths, jnp.zeros_like(site_strengths))  1.81 us
  transfers between devices with their start and end apart: 5, of which 5 were waited for; matrix products, arithmetic and copies ran while one was open for 3% of the time, Pallas kernels for 0%

profile of v2, /device:TPU:0, one launch (start us, length us, event | category | flops | bytes accessed | tf_op | source)
XLA Modules:
  0.0 83.3 jit_solution(14285202963948670990)
XLA Ops:
  1.3 0.7 convert_element_type.8
  2.0 0.9 %copy.12 = f32[3,512]{0,1:T(8,128)} copy(f32[3,512]{1,0:T(4,128)S(1)} %convert_element_type.8) | data formatting | bytes 12288 | tf_op jit(solution)/shard_map/convert_element_type | solution.py:160
  2.9 1.8 %broadcast_select_fusion.q_ref = bf16[32,6144]{1,0:T(8,128)(2,1)} fusion(bf16[32,6144]{1,0:T(8,128)(2,1)} %param.6, pred[6144]{0:T(1024)(128)(4,1)S(1)} %iota_compare_fusion), kind=kLoop, calls=%fused_computation.12 | loop fusion | flops 196608 | bytes 792576 | tf_op jit(solution)/shard_map/jit(_where)/select_n | solution.py:159
  4.7 38.0 %shard_map.68 = (bf16[512,6144]{1,0:T(8,128)(2,1)}, bf16[512,6144]{1,0:T(8,128)(2,1)}, f32[32,512]{1,0:T(8,128)}, f32[32,512]{1,0:T(8,128)}) custom-call(f32[512,3]{1,0:T(8,128)} %bitcast.35, f32[3,6144]{1,0:T(4,128)} %pos_ref.1, bf16[32,6144]{1,0:T(8,128)(2,1)} %broadcast_select_fusion.q_ref), custom_call_target="tpu_custom_call" | custom-call | tf_op jit(solution)/shard_map/pallas_call | solution.py:64
  42.7 0.9 %pad_maximum_fusion.1 = f32[2,32,512]{2,1,0:T(8,128)S(1)} fusion(f32[1,32,512]{2,1,0:T(8,128)} %bitcast.39, f32[1,32,512]{2,1,0:T(8,128)} %bitcast.36), kind=kLoop, calls=%fused_computation.24 | loop fusion | flops 32768 | bytes 262144 | tf_op jit(solution)/shard_map/stack | solution.py:164
  43.6 3.0 %collective-permute-start = (f32[2,32,512]{2,1,0:T(8,128)S(1)}, f32[2,32,512]{2,1,0:T(8,128)S(1)}, u32[]{:S(2)}, u32[]{:S(2)}) collective-permute-start(f32[2,32,512]{2,1,0:T(8,128)S(1)} %pad_maximum_fusion.1), channel_id=1, source_target_pairs={{0,4},{4,0},{8,12},{12,8},{16,20},{20,16},{24,28},{28,24},{1,5},{5... | collective-permute-start | bytes 393224 | tf_op jit(solution)/shard_map/ppermute | solution.py:129
  46.7 3.5 %collective-permute-done = f32[2,32,512]{2,1,0:T(8,128)S(1)} collective-permute-done((f32[2,32,512]{2,1,0:T(8,128)S(1)}, f32[2,32,512]{2,1,0:T(8,128)S(1)}, u32[]{:S(2)}, u32[]{:S(2)}) %collective-permute-start) | collective-permute-done | bytes 131104 | tf_op jit(solution)/shard_map/ppermute | solution.py:129
  50.1 0.9 %fusion.23 = f32[2,32,512]{2,1,0:T(8,128)S(1)} fusion(f32[2,32,512]{2,1,0:T(8,128)S(1)} %collective-permute-done, f32[1,32,512]{2,1,0:T(8,128)} %bitcast.40, f32[1,32,512]{2,1,0:T(8,128)} %bitcast.37), kind=kLoop, calls=%fused_computation.56 | loop fusion | flops 65536 | bytes 393216 | tf_op jit(solution)/shard_map/add | solution.py:129
  51.0 1.9 %collective-permute-start.1 = (f32[2,32,512]{2,1,0:T(8,128)S(1)}, f32[2,32,512]{2,1,0:T(8,128)S(1)}, u32[]{:S(2)}, u32[]{:S(2)}) collective-permute-start(f32[2,32,512]{2,1,0:T(8,128)S(1)} %fusion.23), channel_id=1, source_target_pairs={{0,8},{4,12},{8,0},{12,4},{16,24},{20,28},{24,16},{28,20},{1,9},{5... | collective-permute-start | bytes 393224 | tf_op jit(solution)/shard_map/ppermute | solution.py:129
  52.9 0.7 multiply_multiply_fusion
  53.6 2.5 %collective-permute-done.1 = f32[2,32,512]{2,1,0:T(8,128)S(1)} collective-permute-done((f32[2,32,512]{2,1,0:T(8,128)S(1)}, f32[2,32,512]{2,1,0:T(8,128)S(1)}, u32[]{:S(2)}, u32[]{:S(2)}) %collective-permute-start.1) | collective-permute-done | bytes 131104 | tf_op jit(solution)/shard_map/ppermute | solution.py:129
  56.1 0.9 %fusion.30 = f32[2,32,512]{2,1,0:T(8,128)S(1)} fusion(f32[2,32,512]{2,1,0:T(8,128)S(1)} %collective-permute-done.1, f32[2,32,512]{2,1,0:T(8,128)S(1)} %collective-permute-done, f32[1,32,512]{2,1,0:T(8,128)} %bitcast.41, f32[1,32,512]{2,1,0:T(8,128)} %bitcast.38), kind=kLoop, calls=%fused_computation.59 | loop fusion | flops 98304 | bytes 524288 | tf_op jit(solution)/shard_map/add | solution.py:129
  57.0 2.9 %collective-permute-start.2 = (f32[2,32,512]{2,1,0:T(8,128)S(1)}, f32[2,32,512]{2,1,0:T(8,128)S(1)}, u32[]{:S(2)}, u32[]{:S(2)}) collective-permute-start(f32[2,32,512]{2,1,0:T(8,128)S(1)} %fusion.30), channel_id=1, source_target_pairs={{0,16},{4,20},{8,24},{12,28},{16,0},{20,4},{24,8},{28,12},{1,17},{... | collective-permute-start | bytes 393224 | tf_op jit(solution)/shard_map/ppermute | solution.py:129
  59.9 2.0 %multiply_reduce_fusion.2 = (f32[512]{0:T(512)S(1)}, f32[512]{0:T(512)S(1)}, f32[512]{0:T(512)S(1)}, f32[512]{0:T(512)S(1)}, f32[512]{0:T(512)S(1)}, /*index=5*/f32[512]{0:T(512)S(1)}, f32[512]{0:T(512)S(1)}, f32[512]{0:T(512)S(1)}) fusion(f32[3,512]{0,1:T(8,128)} %copy.12), kind=kLoop, calls=%fused_computation.15 | loop fusion | flops 6144 | bytes 22528 | tf_op jit(solution)/shard_map/mul | solution.py:117
  61.8 2.5 %collective-permute-done.2 = f32[2,32,512]{2,1,0:T(8,128)S(1)} collective-permute-done((f32[2,32,512]{2,1,0:T(8,128)S(1)}, f32[2,32,512]{2,1,0:T(8,128)S(1)}, u32[]{:S(2)}, u32[]{:S(2)}) %collective-permute-start.2) | collective-permute-done | bytes 131104 | tf_op jit(solution)/shard_map/ppermute | solution.py:129
  64.3 0.1 multiply_convert_fusion.2
  64.4 0.0 slice-start
  64.5 0.0 slice-start.1
  64.5 4.0 %fusion.4 = f32[128,6144]{1,0:T(8,128)S(1)} fusion(bf16[512,6144]{1,0:T(8,128)(2,1)} %get-tuple-element.8, bf16[32,512]{1,0:T(8,128)(2,1)S(1)} %get-tuple-element.35, bf16[32,512]{1,0:T(8,128)(2,1)S(1)} %get-tuple-element.34, bf16[32,512]{1,0:T(8,128)(2,1)S(1)} %get-tuple-element.36, bf16[32,512]{1,0:T(8,128)(2,1)S(1)} %get-tuple-element.30), kind=kOutput, calls=%fused_computation.25 | convolution fusion | flops 805830656 | bytes 9568256 | tf_op jit(solution)/shard_map/dot_general | solution.py:168
  68.5 0.0 slice-done
  68.5 0.6 slice-done.1
  69.1 0.0 copy-start
  69.1 1.0 %convolution_add_fusion = f32[128,6144]{1,0:T(8,128)S(1)} fusion(f32[128,6144]{1,0:T(8,128)S(1)} %fusion.4, bf16[512,6144]{1,0:T(8,128)(2,1)S(1)} %bitcast.34, bf16[32,512]{1,0:T(8,128)(2,1)S(1)} %get-tuple-element.29, bf16[32,512]{1,0:T(8,128)(2,1)S(1)} %get-tuple-element.28, bf16[32,512]{1,0:T(8,128)(2,1)S(1)} %get-tuple-element.23, ...), kind=kOutput, calls=%fused_computation | convolution fusion | flops 806617088 | bytes 12713984 | tf_op jit(solution)/shard_map/dot_general | solution.py:169
  70.1 0.0 copy-done
  70.1 0.4 fusion
  70.6 0.7 concatenate.22
  71.3 0.3 copy.16
  71.7 0.1 pad_maximum_fusion
  71.8 0.1 select_bitcast_fusion
  71.9 0.1 collective-permute-start.3
  72.0 1.8 %collective-permute-done.3 = f32[35,2,1536]{2,0,1:T(8,128)S(1)} collective-permute-done((f32[35,2,1536]{2,0,1:T(8,128)S(1)}, f32[35,2,1536]{2,0,1:T(8,128)S(1)}, u32[]{:S(2)}, u32[]{:S(2)}) %collective-permute-start.3) | collective-permute-done | bytes 430112 | tf_op jit(solution)/shard_map/ppermute | solution.py:146
  73.8 0.1 fusion.3
  73.9 1.8 %collective-permute-start.4 = (f32[35,1,1536]{2,0,1:T(8,128)S(1)}, f32[35,1,1536]{2,0,1:T(8,128)S(1)}, u32[]{:S(2)}, u32[]{:S(2)}) collective-permute-start(f32[35,1,1536]{2,0,1:T(8,128)S(1)} %select_bitcast_fusion.1), channel_id=1, source_target_pairs={{0,2},{1,3},{2,0},{3,1},{4,6},{5,7},{6,4},{7,5},{8,10},{9,11},{10,... | collective-permute-start | bytes 645128 | tf_op jit(solution)/shard_map/ppermute | solution.py:146
  75.7 6.3 %collective-permute-done.4 = f32[35,1,1536]{2,0,1:T(8,128)S(1)} collective-permute-done((f32[35,1,1536]{2,0,1:T(8,128)S(1)}, f32[35,1,1536]{2,0,1:T(8,128)S(1)}, u32[]{:S(2)}, u32[]{:S(2)}) %collective-permute-start.4) | collective-permute-done | bytes 215072 | tf_op jit(solution)/shard_map/ppermute | solution.py:146
  82.0 0.1 bitcast_add_fusion.1
  82.0 0.7 slice_bitcast_fusion
  82.7 0.6 slice_bitcast_fusion.3
  (11 shorter events, 0.2 us)
Async XLA Ops:
  43.6 6.5 %collective-permute-start = (f32[2,32,512]{2,1,0:T(8,128)S(1)}, f32[2,32,512]{2,1,0:T(8,128)S(1)}, u32[]{:S(2)}, u32[]{:S(2)}) collective-permute-start(f32[2,32,512]{2,1,0:T(8,128)S(1)} %pad_maximum_fusion.1), channel_id=1, source_target_pairs={{0,4},{4,0},{8,12},{12,8},{16,20},{20,16},{24,28},{28,24},{1,5},{5... | collective-permute-start | bytes 393224 | tf_op jit(solution)/shard_map/ppermute | solution.py:129
  51.0 5.0 %collective-permute-start.1 = (f32[2,32,512]{2,1,0:T(8,128)S(1)}, f32[2,32,512]{2,1,0:T(8,128)S(1)}, u32[]{:S(2)}, u32[]{:S(2)}) collective-permute-start(f32[2,32,512]{2,1,0:T(8,128)S(1)} %fusion.23), channel_id=1, source_target_pairs={{0,8},{4,12},{8,0},{12,4},{16,24},{20,28},{24,16},{28,20},{1,9},{5... | collective-permute-start | bytes 393224 | tf_op jit(solution)/shard_map/ppermute | solution.py:129
  57.0 7.3 %collective-permute-start.2 = (f32[2,32,512]{2,1,0:T(8,128)S(1)}, f32[2,32,512]{2,1,0:T(8,128)S(1)}, u32[]{:S(2)}, u32[]{:S(2)}) collective-permute-start(f32[2,32,512]{2,1,0:T(8,128)S(1)} %fusion.30), channel_id=1, source_target_pairs={{0,16},{4,20},{8,24},{12,28},{16,0},{20,4},{24,8},{28,12},{1,17},{... | collective-permute-start | bytes 393224 | tf_op jit(solution)/shard_map/ppermute | solution.py:129
  64.4 4.1 %slice-start = ((s8[6291456]{0:T(1024)(128)(4,1)}), s8[4194304]{0:T(1024)(128)(4,1)S(1)}, s32[]{:S(2)}) async-start(s8[6291456]{0:T(1024)(128)(4,1)} %bitcast.33), calls=%async_computation | async-start | bytes 8388608
  64.5 4.6 %slice-start.1 = ((s8[6291456]{0:T(1024)(128)(4,1)}), s8[2097152]{0:T(1024)(128)(4,1)S(1)}, s32[]{:S(2)}) async-start(s8[6291456]{0:T(1024)(128)(4,1)} %bitcast.33), calls=%async_computation.1 | async-start | bytes 4194304
  69.1 1.0 %copy-start = (bf16[32,6144]{1,0:T(8,128)(2,1)S(1)}, bf16[32,6144]{1,0:T(8,128)(2,1)}, u32[]{:S(2)}) copy-start(bf16[32,6144]{1,0:T(8,128)(2,1)} %param.6) | copy-start | bytes 1179652
  71.9 1.9 %collective-permute-start.3 = (f32[35,2,1536]{2,0,1:T(8,128)S(1)}, f32[35,2,1536]{2,0,1:T(8,128)S(1)}, u32[]{:S(2)}, u32[]{:S(2)}) collective-permute-start(f32[35,2,1536]{2,0,1:T(8,128)S(1)} %select_bitcast_fusion), channel_id=1, source_target_pairs={{0,1},{1,0},{2,3},{3,2},{4,5},{5,4},{6,7},{7,6},{8,9},{9,8},{10,11... | collective-permute-start | bytes 1290248 | tf_op jit(solution)/shard_map/ppermute | solution.py:146
  73.9 8.1 %collective-permute-start.4 = (f32[35,1,1536]{2,0,1:T(8,128)S(1)}, f32[35,1,1536]{2,0,1:T(8,128)S(1)}, u32[]{:S(2)}, u32[]{:S(2)}) collective-permute-start(f32[35,1,1536]{2,0,1:T(8,128)S(1)} %select_bitcast_fusion.1), channel_id=1, source_target_pairs={{0,2},{1,3},{2,0},{3,1},{4,6},{5,7},{6,4},{7,5},{8,10},{9,11},{10,... | collective-permute-start | bytes 645128 | tf_op jit(solution)/shard_map/ppermute | solution.py:146

commit v3 on v0

--- a/solution.py
+++ b/solution.py
@@ -8,27 +8,22 @@
 two_pi = 6.283185307179586
 box_length = 125.0
 
-_COS_C = [(-1) ** n * two_pi ** (2 * n) / float(math.factorial(2 * n)) for n in range(6)]
-_SIN_C = [(-1) ** n * two_pi ** (2 * n + 1) / float(math.factorial(2 * n + 1)) for n in range(6)]
+_SIN_C = [(-1) ** n * math.pi ** (2 * n + 1) / float(math.factorial(2 * n + 1)) for n in range(6)]
+_COS_C = [(-1) ** n * math.pi ** (2 * n) / float(math.factorial(2 * n)) for n in range(7)]
 
 
 def turns_cos_sin(t):
     r = t - jnp.floor(t + 0.5)
-    q = jnp.floor(4.0 * r + 0.5)
-    u = r - 0.25 * q
-    u2 = u * u
-    c = jnp.float32(_COS_C[4])
-    for coef in _COS_C[3::-1]:
-        c = c * u2 + jnp.float32(coef)
-    s = jnp.float32(_SIN_C[4])
-    for coef in _SIN_C[3::-1]:
-        s = s * u2 + jnp.float32(coef)
-    s = s * u
-    odd = jnp.abs(q) == 1.0
-    cos_mag = jnp.where(odd, s, c)
-    sin_mag = jnp.where(odd, c, s)
-    cos_out = jnp.where((q == 1.0) | (jnp.abs(q) == 2.0), -cos_mag, cos_mag)
-    sin_out = jnp.where((q == -1.0) | (jnp.abs(q) == 2.0), -sin_mag, sin_mag)
+    r2 = r * r
+    s = jnp.float32(_SIN_C[-1])
+    for coef in _SIN_C[-2::-1]:
+        s = s * r2 + jnp.float32(coef)
+    s = s * r
+    c = jnp.float32(_COS_C[-1])
+    for coef in _COS_C[-2::-1]:
+        c = c * r2 + jnp.float32(coef)
+    cos_out = 1.0 - 2.0 * (s * s)
+    sin_out = 2.0 * (s * c)
     return cos_out, sin_out
 
 

time: 66.6 us -> 61.7 us (0.926)
  other arithmetic: 22.9 us -> 18 us
    convert_element_type x1, other arithmetic: 21.2 us -> 16.3 us  [local(): sin_table = sin_f.astype(jnp.bfloat16)]
where the time goes in v3:
time: 61.7 us; the launch traced here: 61.5 us
  waiting for transfers between devices  19.2 us (31%)
  other arithmetic  18 us (29%)
  starting transfers between devices  9.62 us (16%)
  matrix products  8.92 us (14%)
  local copies, waits for them, and re-layouts  4.13 us (7%)
  between operations  1.58 us (3%)
    convert_element_type x1, other arithmetic, local(): sin_table = sin_f.astype(jnp.bfloat16)  16.3 us
    ppermute x3, waiting for transfers between devices, butterfly_sum(): x = x + lax.ppermute(x, axis, [(i, i ^ step) for i in range(n)])  11.1 us
    ppermute x2, waiting for transfers between devices, halving_scatter(): held = keep + lax.ppermute(send, axis, [(i, i ^ step) for i in range(n)])  8.1 us
    ppermute x3, starting transfers between devices, butterfly_sum(): x = x + lax.ppermute(x, axis, [(i, i ^ step) for i in range(n)])  7.77 us
    dot_general x1, matrix products, local(): field = jnp.dot(cos_side, cos_table, preferred_element_type=jnp.float32)  4 us
    dot_general x1, matrix products, local(): lax.dot_general(charge_live, cos_table, tensor_product, preferred_element...  1.97 us
    dot_general x1, matrix products, local(): lax.dot_general(charge_live, sin_table, tensor_product, preferred_element...  1.95 us
    ppermute x2, starting transfers between devices, halving_scatter(): held = keep + lax.ppermute(send, axis, [(i, i ^ step) for i in range(n)])  1.85 us
  transfers between devices with their start and end apart: 5, of which 5 were waited for; matrix products, arithmetic and copies ran while one was open for 0% of the time, Pallas kernels for 0%

profile of v3, /device:TPU:0, one launch (start us, length us, event | category | flops | bytes accessed | tf_op | source)
XLA Modules:
  0.0 61.5 jit_solution(12808147213106428891)
XLA Ops:
  0.6 0.7 %convert_element_type.14 = f32[3,512]{1,0:T(4,128)S(1)} convert(s32[3,512]{1,0:T(4,128)} %param.7) | non-fusion elementwise | flops 1536 | bytes 12288 | tf_op jit(solution)/shard_map/convert_element_type | solution.py:103
  1.4 1.1 %fusion.32 = (f32[1,6144]{1,0:T(1,128)S(1)}, f32[1,6144]{1,0:T(1,128)S(1)}, f32[1,6144]{1,0:T(1,128)S(1)}) fusion(f32[3,6144]{1,0:T(4,128)} %param.5), kind=kLoop, calls=%fused_computation.72 | loop fusion | bytes 147456 | tf_op jit(solution)/shard_map/slice | solution.py:105
  2.5 0.0 copy-start.2
  2.5 16.3 %multiply_convert_fusion = (bf16[512,6144]{1,0:T(8,128)(2,1)S(1)}, bf16[512,6144]{1,0:T(8,128)(2,1)S(1)}) fusion(f32[6144]{0:T(1024)S(1)} %bitcast.53, f32[512]{0:T(512)S(1)} %bitcast.63, f32[6144]{0:T(1024)S(1)} %bitcast.54, f32[512]{0:T(512)S(1)} %bitcast.64, f32[6144]{0:T(1024)S(1)} %bitcast.52, f32[512]{0:T(512)S(1)} %bitcast.65), kind=kLoop, calls=%fused_computation | loop fusion | flops 122683392 | bytes 12662784 | tf_op jit(solution)/shard_map/convert_element_type | solution.py:111
  18.8 0.0 copy-start
  18.8 0.0 copy-start.1
  19.5 0.0 copy-done.2
  19.5 0.0 copy-start.3
  19.5 2.0 %convolution_bitcast_fusion = f32[1,32,512]{2,1,0:T(8,128)S(1)} fusion(bf16[512,6144]{1,0:T(8,128)(2,1)S(1)} %get-tuple-element.5, bf16[32,6144]{1,0:T(8,128)(2,1)S(1)} %copy-done.2, pred[6144]{0:T(1024)(128)(4,1)S(1)} %iota_compare_fusion), kind=kOutput, calls=%fused_computation.14 | convolution fusion | flops 201523200 | bytes 6756352 | tf_op jit(solution)/shard_map/dot_general | solution.py:117
  21.5 2.0 %convolution_bitcast_fusion.1 = f32[1,32,512]{2,1,0:T(8,128)S(1)} fusion(bf16[512,6144]{1,0:T(8,128)(2,1)S(1)} %get-tuple-element.4, bf16[32,6144]{1,0:T(8,128)(2,1)S(1)} %copy-done.2, pred[6144]{0:T(1024)(128)(4,1)S(1)} %iota_compare_fusion), kind=kOutput, calls=%fused_computation.15 | convolution fusion | flops 201523200 | bytes 6756352 | tf_op jit(solution)/shard_map/dot_general | solution.py:114
  23.5 0.0 copy-done
  23.5 0.0 copy-done.1
  23.5 3.0 %collective-permute-start = (f32[2,32,512]{2,1,0:T(8,128)S(1)}, f32[2,32,512]{2,1,0:T(8,128)S(1)}, u32[]{:S(2)}, u32[]{:S(2)}) collective-permute-start(f32[2,32,512]{2,1,0:T(8,128)S(1)} %pad_maximum_fusion.1), channel_id=1, source_target_pairs={{0,4},{4,0},{8,12},{12,8},{16,20},{20,16},{24,28},{28,24},{1,5},{5... | collective-permute-start | bytes 393224 | tf_op jit(solution)/shard_map/ppermute | solution.py:72
  26.5 3.5 %collective-permute-done = f32[2,32,512]{2,1,0:T(8,128)S(1)} collective-permute-done((f32[2,32,512]{2,1,0:T(8,128)S(1)}, f32[2,32,512]{2,1,0:T(8,128)S(1)}, u32[]{:S(2)}, u32[]{:S(2)}) %collective-permute-start) | collective-permute-done | bytes 131104 | tf_op jit(solution)/shard_map/ppermute | solution.py:72
  30.1 1.9 %collective-permute-start.1 = (f32[2,32,512]{2,1,0:T(8,128)S(1)}, f32[2,32,512]{2,1,0:T(8,128)S(1)}, u32[]{:S(2)}, u32[]{:S(2)}) collective-permute-start(f32[2,32,512]{2,1,0:T(8,128)S(1)} %fusion.28), channel_id=1, source_target_pairs={{0,8},{4,12},{8,0},{12,4},{16,24},{20,28},{24,16},{28,20},{1,9},{5... | collective-permute-start | bytes 393224 | tf_op jit(solution)/shard_map/ppermute | solution.py:72
  31.9 3.2 %collective-permute-done.1 = f32[2,32,512]{2,1,0:T(8,128)S(1)} collective-permute-done((f32[2,32,512]{2,1,0:T(8,128)S(1)}, f32[2,32,512]{2,1,0:T(8,128)S(1)}, u32[]{:S(2)}, u32[]{:S(2)}) %collective-permute-start.1) | collective-permute-done | bytes 131104 | tf_op jit(solution)/shard_map/ppermute | solution.py:72
  35.1 2.9 %collective-permute-start.2 = (f32[2,32,512]{2,1,0:T(8,128)S(1)}, f32[2,32,512]{2,1,0:T(8,128)S(1)}, u32[]{:S(2)}, u32[]{:S(2)}) collective-permute-start(f32[2,32,512]{2,1,0:T(8,128)S(1)} %fusion.37), channel_id=1, source_target_pairs={{0,16},{4,20},{8,24},{12,28},{16,0},{20,4},{24,8},{28,12},{1,17},{... | collective-permute-start | bytes 393224 | tf_op jit(solution)/shard_map/ppermute | solution.py:72
  38.0 0.0 copy-done.3
  38.0 4.5 %collective-permute-done.2 = f32[2,32,512]{2,1,0:T(8,128)S(1)} collective-permute-done((f32[2,32,512]{2,1,0:T(8,128)S(1)}, f32[2,32,512]{2,1,0:T(8,128)S(1)}, u32[]{:S(2)}, u32[]{:S(2)}) %collective-permute-start.2) | collective-permute-done | bytes 131104 | tf_op jit(solution)/shard_map/ppermute | solution.py:72
  42.5 0.1 multiply_convert_fusion.3
  42.6 0.0 slice-start
  42.6 0.0 slice-start.1
  42.6 4.0 %fusion.7 = f32[128,6144]{1,0:T(8,128)S(1)} fusion(bf16[512,6144]{1,0:T(8,128)(2,1)} %copy-done.1, bf16[32,512]{1,0:T(8,128)(2,1)S(1)} %get-tuple-element.41, bf16[32,512]{1,0:T(8,128)(2,1)S(1)} %get-tuple-element.40, bf16[32,512]{1,0:T(8,128)(2,1)S(1)} %get-tuple-element.42, bf16[32,512]{1,0:T(8,128)(2,1)S(1)} %get-tuple-element.25), kind=kOutput, calls=%fused_computation.29 | convolution fusion | flops 805830656 | bytes 9568256 | tf_op jit(solution)/shard_map/dot_general | solution.py:124
  46.6 0.0 slice-done
  46.7 0.6 %slice-done.1 = s8[2097152]{0:T(1024)(128)(4,1)S(1)} async-done(((s8[6291456]{0:T(1024)(128)(4,1)}), s8[2097152]{0:T(1024)(128)(4,1)S(1)}, s32[]{:S(2)}) %slice-start.1) | async-done | bytes 2097176
  47.3 1.0 %convolution_add_fusion = f32[128,6144]{1,0:T(8,128)S(1)} fusion(f32[128,6144]{1,0:T(8,128)S(1)} %fusion.7, bf16[512,6144]{1,0:T(8,128)(2,1)S(1)} %bitcast.51, bf16[32,512]{1,0:T(8,128)(2,1)S(1)} %get-tuple-element.24, bf16[32,512]{1,0:T(8,128)(2,1)S(1)} %get-tuple-element.23, bf16[32,512]{1,0:T(8,128)(2,1)S(1)} %get-tuple-element.11, ...), kind=kOutput, calls=%fused_computation.10 | convolution fusion | flops 806617088 | bytes 12713984 | tf_op jit(solution)/shard_map/dot_general | solution.py:125
  48.3 0.4 fusion.3
  48.7 0.7 %concatenate.22 = f32[32,2,2,1536]{3,2,1,0:T(2,128)S(1)} reshape(f32[32,6144]{1,0:T(8,128)S(1)} %get-tuple-element.15) | data formatting | bytes 1572864 | tf_op jit(solution)/shard_map/concatenate | solution.py:132
  49.4 0.3 copy.8
  49.8 0.1 pad_maximum_fusion
  50.0 0.1 select_bitcast_fusion
  50.0 0.1 collective-permute-start.3
  50.1 1.8 %collective-permute-done.3 = f32[35,2,1536]{2,0,1:T(8,128)S(1)} collective-permute-done((f32[35,2,1536]{2,0,1:T(8,128)S(1)}, f32[35,2,1536]{2,0,1:T(8,128)S(1)}, u32[]{:S(2)}, u32[]{:S(2)}) %collective-permute-start.3) | collective-permute-done | bytes 430112 | tf_op jit(solution)/shard_map/ppermute | solution.py:89
  52.0 0.1 fusion.6
  52.1 1.8 %collective-permute-start.4 = (f32[35,1,1536]{2,0,1:T(8,128)S(1)}, f32[35,1,1536]{2,0,1:T(8,128)S(1)}, u32[]{:S(2)}, u32[]{:S(2)}) collective-permute-start(f32[35,1,1536]{2,0,1:T(8,128)S(1)} %select_bitcast_fusion.1), channel_id=1, source_target_pairs={{0,2},{1,3},{2,0},{3,1},{4,6},{5,7},{6,4},{7,5},{8,10},{9,11},{10,... | collective-permute-start | bytes 645128 | tf_op jit(solution)/shard_map/ppermute | solution.py:89
  53.8 6.3 %collective-permute-done.4 = f32[35,1,1536]{2,0,1:T(8,128)S(1)} collective-permute-done((f32[35,1,1536]{2,0,1:T(8,128)S(1)}, f32[35,1,1536]{2,0,1:T(8,128)S(1)}, u32[]{:S(2)}, u32[]{:S(2)}) %collective-permute-start.4) | collective-permute-done | bytes 215072 | tf_op jit(solution)/shard_map/ppermute | solution.py:89
  60.1 0.1 bitcast_add_fusion.1
  60.2 0.7 %slice_bitcast_fusion = f32[32,1536]{1,0:T(8,128)} fusion(f32[35,1,1536]{2,0,1:T(8,128)S(1)} %bitcast_add_fusion.1), kind=kLoop, calls=%fused_computation.27 | loop fusion | bytes 393216 | tf_op jit(solution)/shard_map/slice | solution.py:134
  60.9 0.6 slice_bitcast_fusion.3
  (16 shorter events, 0.3 us)
Async XLA Ops:
  2.5 17.0 %copy-start.2 = (bf16[32,6144]{1,0:T(8,128)(2,1)S(1)}, bf16[32,6144]{1,0:T(8,128)(2,1)}, u32[]{:S(2)}) copy-start(bf16[32,6144]{1,0:T(8,128)(2,1)} %param.6) | copy-start | bytes 1179652
  18.8 4.7 %copy-start = (bf16[512,6144]{1,0:T(8,128)(2,1)}, bf16[512,6144]{1,0:T(8,128)(2,1)S(1)}, u32[]{:S(2)}) copy-start(bf16[512,6144]{1,0:T(8,128)(2,1)S(1)} %get-tuple-element.5) | copy-start | bytes 18874372
  18.8 4.7 %copy-start.1 = (bf16[512,6144]{1,0:T(8,128)(2,1)}, bf16[512,6144]{1,0:T(8,128)(2,1)S(1)}, u32[]{:S(2)}) copy-start(bf16[512,6144]{1,0:T(8,128)(2,1)S(1)} %get-tuple-element.4) | copy-start | bytes 18874372
  19.5 18.5 %copy-start.3 = (f32[32]{0:T(128)S(1)}, f32[32]{0:T(128)}, u32[]{:S(2)}) copy-start(f32[32]{0:T(128)} %param.9) | copy-start | bytes 388
  23.5 6.5 %collective-permute-start = (f32[2,32,512]{2,1,0:T(8,128)S(1)}, f32[2,32,512]{2,1,0:T(8,128)S(1)}, u32[]{:S(2)}, u32[]{:S(2)}) collective-permute-start(f32[2,32,512]{2,1,0:T(8,128)S(1)} %pad_maximum_fusion.1), channel_id=1, source_target_pairs={{0,4},{4,0},{8,12},{12,8},{16,20},{20,16},{24,28},{28,24},{1,5},{5... | collective-permute-start | bytes 393224 | tf_op jit(solution)/shard_map/ppermute | solution.py:72
  30.1 5.0 %collective-permute-start.1 = (f32[2,32,512]{2,1,0:T(8,128)S(1)}, f32[2,32,512]{2,1,0:T(8,128)S(1)}, u32[]{:S(2)}, u32[]{:S(2)}) collective-permute-start(f32[2,32,512]{2,1,0:T(8,128)S(1)} %fusion.28), channel_id=1, source_target_pairs={{0,8},{4,12},{8,0},{12,4},{16,24},{20,28},{24,16},{28,20},{1,9},{5... | collective-permute-start | bytes 393224 | tf_op jit(solution)/shard_map/ppermute | solution.py:72
  35.1 7.3 %collective-permute-start.2 = (f32[2,32,512]{2,1,0:T(8,128)S(1)}, f32[2,32,512]{2,1,0:T(8,128)S(1)}, u32[]{:S(2)}, u32[]{:S(2)}) collective-permute-start(f32[2,32,512]{2,1,0:T(8,128)S(1)} %fusion.37), channel_id=1, source_target_pairs={{0,16},{4,20},{8,24},{12,28},{16,0},{20,4},{24,8},{28,12},{1,17},{... | collective-permute-start | bytes 393224 | tf_op jit(solution)/shard_map/ppermute | solution.py:72
  42.6 4.1 %slice-start = ((s8[6291456]{0:T(1024)(128)(4,1)}), s8[4194304]{0:T(1024)(128)(4,1)S(1)}, s32[]{:S(2)}) async-start(s8[6291456]{0:T(1024)(128)(4,1)} %bitcast.50), calls=%async_computation | async-start | bytes 8388608
  42.6 4.6 %slice-start.1 = ((s8[6291456]{0:T(1024)(128)(4,1)}), s8[2097152]{0:T(1024)(128)(4,1)S(1)}, s32[]{:S(2)}) async-start(s8[6291456]{0:T(1024)(128)(4,1)} %bitcast.50), calls=%async_computation.1 | async-start | bytes 4194304
  50.0 1.9 %collective-permute-start.3 = (f32[35,2,1536]{2,0,1:T(8,128)S(1)}, f32[35,2,1536]{2,0,1:T(8,128)S(1)}, u32[]{:S(2)}, u32[]{:S(2)}) collective-permute-start(f32[35,2,1536]{2,0,1:T(8,128)S(1)} %select_bitcast_fusion), channel_id=1, source_target_pairs={{0,1},{1,0},{2,3},{3,2},{4,5},{5,4},{6,7},{7,6},{8,9},{9,8},{10,11... | collective-permute-start | bytes 1290248 | tf_op jit(solution)/shard_map/ppermute | solution.py:89
  52.1 8.1 %collective-permute-start.4 = (f32[35,1,1536]{2,0,1:T(8,128)S(1)}, f32[35,1,1536]{2,0,1:T(8,128)S(1)}, u32[]{:S(2)}, u32[]{:S(2)}) collective-permute-start(f32[35,1,1536]{2,0,1:T(8,128)S(1)} %select_bitcast_fusion.1), channel_id=1, source_target_pairs={{0,2},{1,3},{2,0},{3,1},{4,6},{5,7},{6,4},{7,5},{8,10},{9,11},{10,... | collective-permute-start | bytes 645128 | tf_op jit(solution)/shard_map/ppermute | solution.py:89

commit v4 on v3

--- a/solution.py
+++ b/solution.py
@@ -74,21 +74,18 @@
     return x
 
 
-def halving_scatter(x, axis, n):
-    rows_all = x.shape[1]
-    rows = rows_all // n
+def halving_scatter(held, axis, n):
     me = lax.axis_index(axis)
-    held = x.reshape(x.shape[0], n, rows)
     step = 1
     while step < n:
-        m = held.shape[1]
-        pairs = held.reshape(held.shape[0], m // 2, 2, rows)
+        m = held.shape[0]
+        pairs = held.reshape(m // 2, 2, *held.shape[1:])
         bit = (me // step) % 2
-        keep = jnp.where(bit == 0, pairs[:, :, 0], pairs[:, :, 1])
-        send = jnp.where(bit == 0, pairs[:, :, 1], pairs[:, :, 0])
+        keep = jnp.where(bit == 0, pairs[:, 0], pairs[:, 1])
+        send = jnp.where(bit == 0, pairs[:, 1], pairs[:, 0])
         held = keep + lax.ppermute(send, axis, [(i, i ^ step) for i in range(n)])
         step *= 2
-    return held.reshape(held.shape[0], rows)
+    return held[0]
 
 
 def make_local(n_dom, n_ka):
@@ -107,22 +104,19 @@
             + cartesian_mode_vector[2][:, None] * cell_coordinates_frac[2][None, :]
         )
         cos_f, sin_f = turns_cos_sin(t)
-        cos_table = cos_f.astype(jnp.bfloat16)
-        sin_table = sin_f.astype(jnp.bfloat16)
-        cos_table, sin_table = lax.optimization_barrier((cos_table, sin_table))
+        table = jnp.concatenate([cos_f, sin_f], 0).astype(jnp.bfloat16)
+        table = lax.optimization_barrier(table)
+        n_k = cartesian_mode_vector.shape[1]
         tensor_product = (((1,), (1,)), ((), ()))
-        s_cos = lax.dot_general(
-            charge_live, cos_table, tensor_product, preferred_element_type=jnp.float32
+        s_both = lax.dot_general(
+            charge_live, table, tensor_product, preferred_element_type=jnp.float32
         )
-        s_sin = lax.dot_general(
-            charge_live, sin_table, tensor_product, preferred_element_type=jnp.float32
+        s_both = butterfly_sum(s_both.reshape(channels, 2, n_k), "dom", n_dom)
+        cos_side, sin_side = reciprocal_filter_weight(
+            s_both[:, 0], s_both[:, 1], cartesian_mode_vector, gaussian_spread, atoms_total
         )
-        s_both = butterfly_sum(jnp.stack([s_cos, s_sin], 0), "dom", n_dom)
-        cos_side, sin_side = reciprocal_filter_weight(
-            s_both[0], s_both[1], cartesian_mode_vector, gaussian_spread, atoms_total
-        )
-        field = jnp.dot(cos_side, cos_table, preferred_element_type=jnp.float32)
-        field = field + jnp.dot(sin_side, sin_table, preferred_element_type=jnp.float32)
+        sides = jnp.concatenate([cos_side, sin_side], 1)
+        field = jnp.dot(sides, table, preferred_element_type=jnp.float32)
         charge_f = charge_live.astype(jnp.float32)
         head = jnp.where(live[None, :], field[:channels], 0.0)
         force_rows = [
@@ -130,7 +124,9 @@
             for d in range(3)
         ]
         partial = jnp.concatenate([head] + force_rows, 0)
-        own = halving_scatter(partial, "ka", n_ka)
+        rows = n_local // n_ka
+        blocks = jnp.stack([partial[:, b * rows : (b + 1) * rows] for b in range(n_ka)], 0)
+        own = halving_scatter(blocks, "ka", n_ka)
         return (own[:channels], own[channels:])
 
     return local

time: 61.7 us -> 66.8 us (1.083)
  local copies, waits for them, and re-layouts: 4.13 us -> 6.49 us
  matrix products: 8.92 us -> 10.4 us
  other arithmetic: 18 us -> 19.3 us
    another operation x3 -> x4, other arithmetic: 0.14 us -> 16.5 us
    convert_element_type x1 -> x0, other arithmetic: 16.3 us -> none  [local(): sin_table = sin_f.astype(jnp.bfloat16)]
    unnamed x12 -> x6, local copies, waits for them, and re-layouts: 0.66 us -> 3.78 us
    dot_general x4 -> x2, matrix products: 8.92 us -> 10.4 us  [the longest x1 6.58 us: local(): field = jnp.dot(sides, table, preferred_element_type=jnp.float32)]
    concatenate x0 -> x1, other arithmetic: none -> 1.12 us  [local(): table = jnp.concatenate([cos_f, sin_f], 0).astype(jnp.bfloat16)]
    concatenate x8 -> x0, local copies, waits for them, and re-layouts: 1.05 us -> none  [local(): partial = jnp.concatenate([head] + force_rows, 0)]
where the time goes in v4:
time: 66.8 us; the launch traced here: 66.6 us
  other arithmetic  19.3 us (29%)
  waiting for transfers between devices  19.2 us (29%)
  matrix products  10.4 us (16%)
  starting transfers between devices  9.62 us (14%)
  local copies, waits for them, and re-layouts  6.49 us (10%)
  between operations  1.55 us (2%)
    another operation x3, other arithmetic  16.4 us
    ppermute x3, waiting for transfers between devices, butterfly_sum(): x = x + lax.ppermute(x, axis, [(i, i ^ step) for i in range(n)])  11.1 us
    ppermute x2, waiting for transfers between devices, halving_scatter(): held = keep + lax.ppermute(send, axis, [(i, i ^ step) for i in range(n)])  8.1 us
    ppermute x3, starting transfers between devices, butterfly_sum(): x = x + lax.ppermute(x, axis, [(i, i ^ step) for i in range(n)])  7.77 us
    dot_general x1, matrix products, local(): field = jnp.dot(sides, table, preferred_element_type=jnp.float32)  6.58 us
    dot_general x1, matrix products, local(): lax.dot_general(charge_live, table, tensor_product, preferred_element_typ...  3.8 us
    unnamed x6, local copies, waits for them, and re-layouts  3.78 us
    ppermute x2, starting transfers between devices, halving_scatter(): held = keep + lax.ppermute(send, axis, [(i, i ^ step) for i in range(n)])  1.85 us
  transfers between devices with their start and end apart: 5, of which 5 were waited for; matrix products, arithmetic and copies ran while one was open for 0% of the time, Pallas kernels for 0%

profile of v4, /device:TPU:0, one launch (start us, length us, event | category | flops | bytes accessed | tf_op | source)
XLA Modules:
  0.0 66.6 jit_solution(16397573284745261975)
XLA Ops:
  0.6 0.7 %convert_element_type.4 = f32[3,512]{1,0:T(4,128)S(1)} convert(s32[3,512]{1,0:T(4,128)} %param.7) | non-fusion elementwise | flops 1536 | bytes 12288 | tf_op jit(solution)/shard_map/convert_element_type | solution.py:100
  1.4 1.1 %fusion.31 = (f32[1,6144]{1,0:T(1,128)S(1)}, f32[1,6144]{1,0:T(1,128)S(1)}, f32[1,6144]{1,0:T(1,128)S(1)}) fusion(f32[3,6144]{1,0:T(4,128)} %param.5), kind=kLoop, calls=%fused_computation.76 | loop fusion | bytes 147456 | tf_op jit(solution)/shard_map/slice | solution.py:102
  2.5 16.3 %subtract_convert_fusion = (bf16[512,6144]{1,0:T(8,128)(2,1)S(1)}, bf16[512,6144]{1,0:T(8,128)(2,1)S(1)}) fusion(f32[6144]{0:T(1024)S(1)} %bitcast.72, f32[512]{0:T(512)S(1)} %bitcast.82, f32[6144]{0:T(1024)S(1)} %bitcast.73, f32[512]{0:T(512)S(1)} %bitcast.83, f32[6144]{0:T(1024)S(1)} %bitcast.71, f32[512]{0:T(512)S(1)} %bitcast.84), kind=kLoop, calls=%fused_computation.2 | loop fusion | flops 122683392 | bytes 12662784 | tf_op jit(solution)/shard_map/convert.8
  18.8 0.0 copy-start.1
  18.8 1.1 %pad_maximum_fusion = bf16[1024,6144]{1,0:T(8,128)(2,1)S(1)} fusion(bf16[512,6144]{1,0:T(8,128)(2,1)S(1)} %get-tuple-element.22, bf16[512,6144]{1,0:T(8,128)(2,1)S(1)} %get-tuple-element.21), kind=kLoop, calls=%fused_computation | loop fusion | flops 25165824 | bytes 25165824 | tf_op jit(solution)/shard_map/concatenate | solution.py:107
  19.9 0.0 copy-start
  19.9 0.0 copy-start.2
  20.7 3.8 %copy-done = bf16[1024,6144]{1,0:T(8,128)(2,1)} copy-done((bf16[1024,6144]{1,0:T(8,128)(2,1)}, bf16[1024,6144]{1,0:T(8,128)(2,1)S(1)}, u32[]{:S(2)}) %copy-start) | copy-done | bytes 12582936
  24.5 0.0 copy-done.1
  24.5 3.8 %fusion.23 = f32[32,1024]{1,0:T(8,128)S(1)} fusion(bf16[1024,6144]{1,0:T(8,128)(2,1)S(1)} %pad_maximum_fusion, bf16[32,6144]{1,0:T(8,128)(2,1)S(1)} %copy-done.1, pred[6144]{0:T(1024)(128)(4,1)S(1)} %iota_compare_fusion), kind=kOutput, calls=%fused_computation.48 | convolution fusion | flops 402849792 | bytes 13113344 | tf_op jit(solution)/shard_map/dot_general | solution.py:111
  28.3 0.1 reshape.72
  28.4 3.0 %collective-permute-start = (f32[32,2,512]{2,1,0:T(2,128)S(1)}, f32[32,2,512]{2,1,0:T(2,128)S(1)}, u32[]{:S(2)}, u32[]{:S(2)}) collective-permute-start(f32[32,2,512]{2,1,0:T(2,128)S(1)} %reshape.72), channel_id=1, source_target_pairs={{0,4},{4,0},{8,12},{12,8},{16,20},{20,16},{24,28},{28,24},{1,5},{5... | collective-permute-start | bytes 393224 | tf_op jit(solution)/shard_map/ppermute | solution.py:72
  31.4 3.5 %collective-permute-done = f32[32,2,512]{2,1,0:T(2,128)S(1)} collective-permute-done((f32[32,2,512]{2,1,0:T(2,128)S(1)}, f32[32,2,512]{2,1,0:T(2,128)S(1)}, u32[]{:S(2)}, u32[]{:S(2)}) %collective-permute-start) | collective-permute-done | bytes 131104 | tf_op jit(solution)/shard_map/ppermute | solution.py:72
  34.9 0.1 add.138
  35.0 1.9 %collective-permute-start.1 = (f32[32,2,512]{2,1,0:T(2,128)S(1)}, f32[32,2,512]{2,1,0:T(2,128)S(1)}, u32[]{:S(2)}, u32[]{:S(2)}) collective-permute-start(f32[32,2,512]{2,1,0:T(2,128)S(1)} %add.138), channel_id=1, source_target_pairs={{0,8},{4,12},{8,0},{12,4},{16,24},{20,28},{24,16},{28,20},{1,9},{5... | collective-permute-start | bytes 393224 | tf_op jit(solution)/shard_map/ppermute | solution.py:72
  36.9 3.2 %collective-permute-done.1 = f32[32,2,512]{2,1,0:T(2,128)S(1)} collective-permute-done((f32[32,2,512]{2,1,0:T(2,128)S(1)}, f32[32,2,512]{2,1,0:T(2,128)S(1)}, u32[]{:S(2)}, u32[]{:S(2)}) %collective-permute-start.1) | collective-permute-done | bytes 131104 | tf_op jit(solution)/shard_map/ppermute | solution.py:72
  40.0 0.1 add.139
  40.1 2.9 %collective-permute-start.2 = (f32[32,2,512]{2,1,0:T(2,128)S(1)}, f32[32,2,512]{2,1,0:T(2,128)S(1)}, u32[]{:S(2)}, u32[]{:S(2)}) collective-permute-start(f32[32,2,512]{2,1,0:T(2,128)S(1)} %add.139), channel_id=1, source_target_pairs={{0,16},{4,20},{8,24},{12,28},{16,0},{20,4},{24,8},{28,12},{1,17},{... | collective-permute-start | bytes 393224 | tf_op jit(solution)/shard_map/ppermute | solution.py:72
  43.0 0.0 copy-done.2
  43.0 4.5 %collective-permute-done.2 = f32[32,2,512]{2,1,0:T(2,128)S(1)} collective-permute-done((f32[32,2,512]{2,1,0:T(2,128)S(1)}, f32[32,2,512]{2,1,0:T(2,128)S(1)}, u32[]{:S(2)}, u32[]{:S(2)}) %collective-permute-start.2) | collective-permute-done | bytes 131104 | tf_op jit(solution)/shard_map/ppermute | solution.py:72
  47.4 0.1 add.140
  47.5 0.1 fusion.30
  47.6 0.1 multiply_convert_fusion.6
  47.8 6.6 %fusion.7 = f32[128,6144]{1,0:T(8,128)S(1)} fusion(bf16[1024,6144]{1,0:T(8,128)(2,1)} %copy-done, bf16[32,512]{1,0:T(8,128)(2,1)S(1)} %get-tuple-element.28, bf16[32,512]{1,0:T(8,128)(2,1)S(1)} %get-tuple-element.27, bf16[32,512]{1,0:T(8,128)(2,1)S(1)} %get-tuple-element.26, bf16[32,512]{1,0:T(8,128)(2,1)S(1)} %get-tuple-element.42, ...), kind=kOutput, calls=%fused_computation.26 | convolution fusion | flops 1612709888 | bytes 15990784 | tf_op jit(solution)/shard_map/dot_general | solution.py:119
  54.4 0.5 fusion.3
  54.8 0.1 pad_maximum_fusion.1
  54.9 0.1 slice_bitcast_fusion.5
  55.0 0.1 pad_maximum_fusion.2
  55.1 0.1 select_bitcast_fusion
  55.1 0.1 collective-permute-start.3
  55.2 1.8 %collective-permute-done.3 = f32[2,35,1536]{2,1,0:T(8,128)S(1)} collective-permute-done((f32[2,35,1536]{2,1,0:T(8,128)S(1)}, f32[2,35,1536]{2,1,0:T(8,128)S(1)}, u32[]{:S(2)}, u32[]{:S(2)}) %collective-permute-start.3) | collective-permute-done | bytes 430112 | tf_op jit(solution)/shard_map/ppermute | solution.py:86
  57.1 0.1 fusion.6
  57.2 1.8 %collective-permute-start.4 = (f32[1,35,1536]{2,1,0:T(8,128)S(1)}, f32[1,35,1536]{2,1,0:T(8,128)S(1)}, u32[]{:S(2)}, u32[]{:S(2)}) collective-permute-start(f32[1,35,1536]{2,1,0:T(8,128)S(1)} %select_bitcast_fusion.1), channel_id=1, source_target_pairs={{0,2},{1,3},{2,0},{3,1},{4,6},{5,7},{6,4},{7,5},{8,10},{9,11},{10,... | collective-permute-start | bytes 645128 | tf_op jit(solution)/shard_map/ppermute | solution.py:86
  59.0 6.3 %collective-permute-done.4 = f32[1,35,1536]{2,1,0:T(8,128)S(1)} collective-permute-done((f32[1,35,1536]{2,1,0:T(8,128)S(1)}, f32[1,35,1536]{2,1,0:T(8,128)S(1)}, u32[]{:S(2)}, u32[]{:S(2)}) %collective-permute-start.4) | collective-permute-done | bytes 215072 | tf_op jit(solution)/shard_map/ppermute | solution.py:86
  65.2 0.1 bitcast_add_fusion.1
  65.3 0.7 %slice_bitcast_fusion.6 = f32[32,1536]{1,0:T(8,128)} fusion(f32[1,35,1536]{2,1,0:T(8,128)S(1)} %bitcast_add_fusion.1), kind=kLoop, calls=%fused_computation.49 | loop fusion | bytes 393216 | tf_op jit(solution)/shard_map/slice | solution.py:130
  66.0 0.6 slice_bitcast_fusion.7
  (5 shorter events, 0.1 us)
Async XLA Ops:
  18.8 5.7 %copy-start.1 = (bf16[32,6144]{1,0:T(8,128)(2,1)S(1)}, bf16[32,6144]{1,0:T(8,128)(2,1)}, u32[]{:S(2)}) copy-start(bf16[32,6144]{1,0:T(8,128)(2,1)} %param.6) | copy-start | bytes 1179652
  19.9 4.5 %copy-start = (bf16[1024,6144]{1,0:T(8,128)(2,1)}, bf16[1024,6144]{1,0:T(8,128)(2,1)S(1)}, u32[]{:S(2)}) copy-start(bf16[1024,6144]{1,0:T(8,128)(2,1)S(1)} %pad_maximum_fusion) | copy-start | bytes 37748740
  19.9 23.0 %copy-start.2 = (f32[32]{0:T(128)S(1)}, f32[32]{0:T(128)}, u32[]{:S(2)}) copy-start(f32[32]{0:T(128)} %param.9) | copy-start | bytes 388
  28.4 6.5 %collective-permute-start = (f32[32,2,512]{2,1,0:T(2,128)S(1)}, f32[32,2,512]{2,1,0:T(2,128)S(1)}, u32[]{:S(2)}, u32[]{:S(2)}) collective-permute-start(f32[32,2,512]{2,1,0:T(2,128)S(1)} %reshape.72), channel_id=1, source_target_pairs={{0,4},{4,0},{8,12},{12,8},{16,20},{20,16},{24,28},{28,24},{1,5},{5... | collective-permute-start | bytes 393224 | tf_op jit(solution)/shard_map/ppermute | solution.py:72
  35.0 5.0 %collective-permute-start.1 = (f32[32,2,512]{2,1,0:T(2,128)S(1)}, f32[32,2,512]{2,1,0:T(2,128)S(1)}, u32[]{:S(2)}, u32[]{:S(2)}) collective-permute-start(f32[32,2,512]{2,1,0:T(2,128)S(1)} %add.138), channel_id=1, source_target_pairs={{0,8},{4,12},{8,0},{12,4},{16,24},{20,28},{24,16},{28,20},{1,9},{5... | collective-permute-start | bytes 393224 | tf_op jit(solution)/shard_map/ppermute | solution.py:72
  40.1 7.3 %collective-permute-start.2 = (f32[32,2,512]{2,1,0:T(2,128)S(1)}, f32[32,2,512]{2,1,0:T(2,128)S(1)}, u32[]{:S(2)}, u32[]{:S(2)}) collective-permute-start(f32[32,2,512]{2,1,0:T(2,128)S(1)} %add.139), channel_id=1, source_target_pairs={{0,16},{4,20},{8,24},{12,28},{16,0},{20,4},{24,8},{28,12},{1,17},{... | collective-permute-start | bytes 393224 | tf_op jit(solution)/shard_map/ppermute | solution.py:72
  55.1 1.9 %collective-permute-start.3 = (f32[2,35,1536]{2,1,0:T(8,128)S(1)}, f32[2,35,1536]{2,1,0:T(8,128)S(1)}, u32[]{:S(2)}, u32[]{:S(2)}) collective-permute-start(f32[2,35,1536]{2,1,0:T(8,128)S(1)} %select_bitcast_fusion), channel_id=1, source_target_pairs={{0,1},{1,0},{2,3},{3,2},{4,5},{5,4},{6,7},{7,6},{8,9},{9,8},{10,11... | collective-permute-start | bytes 1290248 | tf_op jit(solution)/shard_map/ppermute | solution.py:86
  57.2 8.1 %collective-permute-start.4 = (f32[1,35,1536]{2,1,0:T(8,128)S(1)}, f32[1,35,1536]{2,1,0:T(8,128)S(1)}, u32[]{:S(2)}, u32[]{:S(2)}) collective-permute-start(f32[1,35,1536]{2,1,0:T(8,128)S(1)} %select_bitcast_fusion.1), channel_id=1, source_target_pairs={{0,2},{1,3},{2,0},{3,1},{4,6},{5,7},{6,4},{7,5},{8,10},{9,11},{10,... | collective-permute-start | bytes 645128 | tf_op jit(solution)/shard_map/ppermute | solution.py:86

commit v5 on v3

--- a/solution.py
+++ b/solution.py
@@ -74,21 +74,18 @@
     return x
 
 
-def halving_scatter(x, axis, n):
-    rows_all = x.shape[1]
-    rows = rows_all // n
+def halving_scatter(held, axis, n):
     me = lax.axis_index(axis)
-    held = x.reshape(x.shape[0], n, rows)
     step = 1
     while step < n:
-        m = held.shape[1]
-        pairs = held.reshape(held.shape[0], m // 2, 2, rows)
+        m = held.shape[0]
+        pairs = held.reshape(m // 2, 2, *held.shape[1:])
         bit = (me // step) % 2
-        keep = jnp.where(bit == 0, pairs[:, :, 0], pairs[:, :, 1])
-        send = jnp.where(bit == 0, pairs[:, :, 1], pairs[:, :, 0])
+        keep = jnp.where(bit == 0, pairs[:, 0], pairs[:, 1])
+        send = jnp.where(bit == 0, pairs[:, 1], pairs[:, 0])
         held = keep + lax.ppermute(send, axis, [(i, i ^ step) for i in range(n)])
         step *= 2
-    return held.reshape(held.shape[0], rows)
+    return held[0]
 
 
 def make_local(n_dom, n_ka):
@@ -130,7 +127,9 @@
             for d in range(3)
         ]
         partial = jnp.concatenate([head] + force_rows, 0)
-        own = halving_scatter(partial, "ka", n_ka)
+        rows = n_local // n_ka
+        blocks = jnp.stack([partial[:, b * rows : (b + 1) * rows] for b in range(n_ka)], 0)
+        own = halving_scatter(blocks, "ka", n_ka)
         return (own[:channels], own[channels:])
 
     return local

time: 61.7 us -> 60.7 us (0.984)
  local copies, waits for them, and re-layouts: 4.13 us -> 3.14 us
    concatenate x8 -> x0, local copies, waits for them, and re-layouts: 1.05 us -> none  [local(): partial = jnp.concatenate([head] + force_rows, 0)]
where the time goes in v5:
time: 60.7 us; the launch traced here: 60.5 us
  waiting for transfers between devices  19.2 us (32%)
  other arithmetic  18.1 us (30%)
  starting transfers between devices  9.62 us (16%)
  matrix products  8.92 us (15%)
  local copies, waits for them, and re-layouts  3.14 us (5%)
  between operations  1.53 us (3%)
    convert_element_type x1, other arithmetic, local(): sin_table = sin_f.astype(jnp.bfloat16)  16.3 us
    ppermute x3, waiting for transfers between devices, butterfly_sum(): x = x + lax.ppermute(x, axis, [(i, i ^ step) for i in range(n)])  11.1 us
    ppermute x2, waiting for transfers between devices, halving_scatter(): held = keep + lax.ppermute(send, axis, [(i, i ^ step) for i in range(n)])  8.1 us
    ppermute x3, starting transfers between devices, butterfly_sum(): x = x + lax.ppermute(x, axis, [(i, i ^ step) for i in range(n)])  7.77 us
    dot_general x1, matrix products, local(): field = jnp.dot(cos_side, cos_table, preferred_element_type=jnp.float32)  4 us
    dot_general x1, matrix products, local(): lax.dot_general(charge_live, cos_table, tensor_product, preferred_element...  1.97 us
    dot_general x1, matrix products, local(): lax.dot_general(charge_live, sin_table, tensor_product, preferred_element...  1.95 us
    ppermute x2, starting transfers between devices, halving_scatter(): held = keep + lax.ppermute(send, axis, [(i, i ^ step) for i in range(n)])  1.85 us
  transfers between devices with their start and end apart: 5, of which 5 were waited for; matrix products, arithmetic and copies ran while one was open for 0% of the time, Pallas kernels for 0%

profile of v5, /device:TPU:0, one launch (start us, length us, event | category | flops | bytes accessed | tf_op | source)
XLA Modules:
  0.0 60.5 jit_solution(5211523724215271063)
XLA Ops:
  0.6 0.7 %convert_element_type.14 = f32[3,512]{1,0:T(4,128)S(1)} convert(s32[3,512]{1,0:T(4,128)} %param.7) | non-fusion elementwise | flops 1536 | bytes 12288 | tf_op jit(solution)/shard_map/convert_element_type | solution.py:100
  1.4 1.1 %fusion.32 = (f32[1,6144]{1,0:T(1,128)S(1)}, f32[1,6144]{1,0:T(1,128)S(1)}, f32[1,6144]{1,0:T(1,128)S(1)}) fusion(f32[3,6144]{1,0:T(4,128)} %param.5), kind=kLoop, calls=%fused_computation.79 | loop fusion | bytes 147456 | tf_op jit(solution)/shard_map/slice | solution.py:102
  2.5 0.0 copy-start.2
  2.5 16.3 %multiply_convert_fusion = (bf16[512,6144]{1,0:T(8,128)(2,1)S(1)}, bf16[512,6144]{1,0:T(8,128)(2,1)S(1)}) fusion(f32[6144]{0:T(1024)S(1)} %bitcast.82, f32[512]{0:T(512)S(1)} %bitcast.92, f32[6144]{0:T(1024)S(1)} %bitcast.83, f32[512]{0:T(512)S(1)} %bitcast.93, f32[6144]{0:T(1024)S(1)} %bitcast.81, f32[512]{0:T(512)S(1)} %bitcast.94), kind=kLoop, calls=%fused_computation | loop fusion | flops 122683392 | bytes 12662784 | tf_op jit(solution)/shard_map/convert_element_type | solution.py:108
  18.8 0.0 copy-start
  18.8 0.0 copy-start.1
  19.5 0.0 copy-done.2
  19.5 0.0 copy-start.3
  19.5 2.0 %convolution_bitcast_fusion = f32[1,32,512]{2,1,0:T(8,128)S(1)} fusion(bf16[512,6144]{1,0:T(8,128)(2,1)S(1)} %get-tuple-element.5, bf16[32,6144]{1,0:T(8,128)(2,1)S(1)} %copy-done.2, pred[6144]{0:T(1024)(128)(4,1)S(1)} %iota_compare_fusion), kind=kOutput, calls=%fused_computation.14 | convolution fusion | flops 201523200 | bytes 6756352 | tf_op jit(solution)/shard_map/dot_general | solution.py:114
  21.5 2.0 %convolution_bitcast_fusion.1 = f32[1,32,512]{2,1,0:T(8,128)S(1)} fusion(bf16[512,6144]{1,0:T(8,128)(2,1)S(1)} %get-tuple-element.4, bf16[32,6144]{1,0:T(8,128)(2,1)S(1)} %copy-done.2, pred[6144]{0:T(1024)(128)(4,1)S(1)} %iota_compare_fusion), kind=kOutput, calls=%fused_computation.15 | convolution fusion | flops 201523200 | bytes 6756352 | tf_op jit(solution)/shard_map/dot_general | solution.py:111
  23.5 0.0 copy-done
  23.5 0.0 copy-done.1
  23.5 3.0 %collective-permute-start = (f32[2,32,512]{2,1,0:T(8,128)S(1)}, f32[2,32,512]{2,1,0:T(8,128)S(1)}, u32[]{:S(2)}, u32[]{:S(2)}) collective-permute-start(f32[2,32,512]{2,1,0:T(8,128)S(1)} %pad_maximum_fusion.2), channel_id=1, source_target_pairs={{0,4},{4,0},{8,12},{12,8},{16,20},{20,16},{24,28},{28,24},{1,5},{5... | collective-permute-start | bytes 393224 | tf_op jit(solution)/shard_map/ppermute | solution.py:72
  26.5 3.5 %collective-permute-done = f32[2,32,512]{2,1,0:T(8,128)S(1)} collective-permute-done((f32[2,32,512]{2,1,0:T(8,128)S(1)}, f32[2,32,512]{2,1,0:T(8,128)S(1)}, u32[]{:S(2)}, u32[]{:S(2)}) %collective-permute-start) | collective-permute-done | bytes 131104 | tf_op jit(solution)/shard_map/ppermute | solution.py:72
  30.1 1.9 %collective-permute-start.1 = (f32[2,32,512]{2,1,0:T(8,128)S(1)}, f32[2,32,512]{2,1,0:T(8,128)S(1)}, u32[]{:S(2)}, u32[]{:S(2)}) collective-permute-start(f32[2,32,512]{2,1,0:T(8,128)S(1)} %fusion.28), channel_id=1, source_target_pairs={{0,8},{4,12},{8,0},{12,4},{16,24},{20,28},{24,16},{28,20},{1,9},{5... | collective-permute-start | bytes 393224 | tf_op jit(solution)/shard_map/ppermute | solution.py:72
  31.9 3.2 %collective-permute-done.1 = f32[2,32,512]{2,1,0:T(8,128)S(1)} collective-permute-done((f32[2,32,512]{2,1,0:T(8,128)S(1)}, f32[2,32,512]{2,1,0:T(8,128)S(1)}, u32[]{:S(2)}, u32[]{:S(2)}) %collective-permute-start.1) | collective-permute-done | bytes 131104 | tf_op jit(solution)/shard_map/ppermute | solution.py:72
  35.1 2.9 %collective-permute-start.2 = (f32[2,32,512]{2,1,0:T(8,128)S(1)}, f32[2,32,512]{2,1,0:T(8,128)S(1)}, u32[]{:S(2)}, u32[]{:S(2)}) collective-permute-start(f32[2,32,512]{2,1,0:T(8,128)S(1)} %fusion.37), channel_id=1, source_target_pairs={{0,16},{4,20},{8,24},{12,28},{16,0},{20,4},{24,8},{28,12},{1,17},{... | collective-permute-start | bytes 393224 | tf_op jit(solution)/shard_map/ppermute | solution.py:72
  38.0 0.0 copy-done.3
  38.0 4.5 %collective-permute-done.2 = f32[2,32,512]{2,1,0:T(8,128)S(1)} collective-permute-done((f32[2,32,512]{2,1,0:T(8,128)S(1)}, f32[2,32,512]{2,1,0:T(8,128)S(1)}, u32[]{:S(2)}, u32[]{:S(2)}) %collective-permute-start.2) | collective-permute-done | bytes 131104 | tf_op jit(solution)/shard_map/ppermute | solution.py:72
  42.5 0.1 multiply_convert_fusion.3
  42.6 0.0 slice-start
  42.6 0.0 slice-start.1
  42.6 4.0 %fusion.7 = f32[128,6144]{1,0:T(8,128)S(1)} fusion(bf16[512,6144]{1,0:T(8,128)(2,1)} %copy-done.1, bf16[32,512]{1,0:T(8,128)(2,1)S(1)} %get-tuple-element.45, bf16[32,512]{1,0:T(8,128)(2,1)S(1)} %get-tuple-element.44, bf16[32,512]{1,0:T(8,128)(2,1)S(1)} %get-tuple-element.46, bf16[32,512]{1,0:T(8,128)(2,1)S(1)} %get-tuple-element.29), kind=kOutput, calls=%fused_computation.36 | convolution fusion | flops 805830656 | bytes 9568256 | tf_op jit(solution)/shard_map/dot_general | solution.py:121
  46.6 0.0 slice-done
  46.7 0.6 %slice-done.1 = s8[2097152]{0:T(1024)(128)(4,1)S(1)} async-done(((s8[6291456]{0:T(1024)(128)(4,1)}), s8[2097152]{0:T(1024)(128)(4,1)S(1)}, s32[]{:S(2)}) %slice-start.1) | async-done | bytes 2097176
  47.3 1.0 %convolution_add_fusion = f32[128,6144]{1,0:T(8,128)S(1)} fusion(f32[128,6144]{1,0:T(8,128)S(1)} %fusion.7, bf16[512,6144]{1,0:T(8,128)(2,1)S(1)} %bitcast.75, bf16[32,512]{1,0:T(8,128)(2,1)S(1)} %get-tuple-element.28, bf16[32,512]{1,0:T(8,128)(2,1)S(1)} %get-tuple-element.27, bf16[32,512]{1,0:T(8,128)(2,1)S(1)} %get-tuple-element.11, ...), kind=kOutput, calls=%fused_computation.10 | convolution fusion | flops 806617088 | bytes 12713984 | tf_op jit(solution)/shard_map/dot_general | solution.py:122
  48.3 0.4 fusion.3
  48.7 0.1 pad_maximum_fusion
  48.8 0.1 slice_bitcast_fusion.5
  48.9 0.1 pad_maximum_fusion.1
  49.0 0.1 select_bitcast_fusion
  49.1 0.1 collective-permute-start.3
  49.2 1.8 %collective-permute-done.3 = f32[2,35,1536]{2,1,0:T(8,128)S(1)} collective-permute-done((f32[2,35,1536]{2,1,0:T(8,128)S(1)}, f32[2,35,1536]{2,1,0:T(8,128)S(1)}, u32[]{:S(2)}, u32[]{:S(2)}) %collective-permute-start.3) | collective-permute-done | bytes 430112 | tf_op jit(solution)/shard_map/ppermute | solution.py:86
  51.0 0.1 fusion.6
  51.1 1.8 %collective-permute-start.4 = (f32[1,35,1536]{2,1,0:T(8,128)S(1)}, f32[1,35,1536]{2,1,0:T(8,128)S(1)}, u32[]{:S(2)}, u32[]{:S(2)}) collective-permute-start(f32[1,35,1536]{2,1,0:T(8,128)S(1)} %select_bitcast_fusion.1), channel_id=1, source_target_pairs={{0,2},{1,3},{2,0},{3,1},{4,6},{5,7},{6,4},{7,5},{8,10},{9,11},{10,... | collective-permute-start | bytes 645128 | tf_op jit(solution)/shard_map/ppermute | solution.py:86
  52.9 6.3 %collective-permute-done.4 = f32[1,35,1536]{2,1,0:T(8,128)S(1)} collective-permute-done((f32[1,35,1536]{2,1,0:T(8,128)S(1)}, f32[1,35,1536]{2,1,0:T(8,128)S(1)}, u32[]{:S(2)}, u32[]{:S(2)}) %collective-permute-start.4) | collective-permute-done | bytes 215072 | tf_op jit(solution)/shard_map/ppermute | solution.py:86
  59.2 0.1 bitcast_add_fusion.1
  59.2 0.7 %slice_bitcast_fusion.6 = f32[32,1536]{1,0:T(8,128)} fusion(f32[1,35,1536]{2,1,0:T(8,128)S(1)} %bitcast_add_fusion.1), kind=kLoop, calls=%fused_computation.34 | loop fusion | bytes 393216 | tf_op jit(solution)/shard_map/slice | solution.py:133
  59.9 0.6 %slice_bitcast_fusion.9 = f32[3,1536]{1,0:T(4,128)} fusion(f32[1,35,1536]{2,1,0:T(8,128)S(1)} %bitcast_add_fusion.1), kind=kLoop, calls=%fused_computation.62 | loop fusion | bytes 36864 | tf_op jit(solution)/shard_map/slice | solution.py:133
  (10 shorter events, 0.2 us)
Async XLA Ops:
  2.5 17.0 %copy-start.2 = (bf16[32,6144]{1,0:T(8,128)(2,1)S(1)}, bf16[32,6144]{1,0:T(8,128)(2,1)}, u32[]{:S(2)}) copy-start(bf16[32,6144]{1,0:T(8,128)(2,1)} %param.6) | copy-start | bytes 1179652
  18.8 4.7 %copy-start = (bf16[512,6144]{1,0:T(8,128)(2,1)}, bf16[512,6144]{1,0:T(8,128)(2,1)S(1)}, u32[]{:S(2)}) copy-start(bf16[512,6144]{1,0:T(8,128)(2,1)S(1)} %get-tuple-element.5) | copy-start | bytes 18874372
  18.8 4.7 %copy-start.1 = (bf16[512,6144]{1,0:T(8,128)(2,1)}, bf16[512,6144]{1,0:T(8,128)(2,1)S(1)}, u32[]{:S(2)}) copy-start(bf16[512,6144]{1,0:T(8,128)(2,1)S(1)} %get-tuple-element.4) | copy-start | bytes 18874372
  19.5 18.5 %copy-start.3 = (f32[32]{0:T(128)S(1)}, f32[32]{0:T(128)}, u32[]{:S(2)}) copy-start(f32[32]{0:T(128)} %param.9) | copy-start | bytes 388
  23.5 6.5 %collective-permute-start = (f32[2,32,512]{2,1,0:T(8,128)S(1)}, f32[2,32,512]{2,1,0:T(8,128)S(1)}, u32[]{:S(2)}, u32[]{:S(2)}) collective-permute-start(f32[2,32,512]{2,1,0:T(8,128)S(1)} %pad_maximum_fusion.2), channel_id=1, source_target_pairs={{0,4},{4,0},{8,12},{12,8},{16,20},{20,16},{24,28},{28,24},{1,5},{5... | collective-permute-start | bytes 393224 | tf_op jit(solution)/shard_map/ppermute | solution.py:72
  30.1 5.0 %collective-permute-start.1 = (f32[2,32,512]{2,1,0:T(8,128)S(1)}, f32[2,32,512]{2,1,0:T(8,128)S(1)}, u32[]{:S(2)}, u32[]{:S(2)}) collective-permute-start(f32[2,32,512]{2,1,0:T(8,128)S(1)} %fusion.28), channel_id=1, source_target_pairs={{0,8},{4,12},{8,0},{12,4},{16,24},{20,28},{24,16},{28,20},{1,9},{5... | collective-permute-start | bytes 393224 | tf_op jit(solution)/shard_map/ppermute | solution.py:72
  35.1 7.3 %collective-permute-start.2 = (f32[2,32,512]{2,1,0:T(8,128)S(1)}, f32[2,32,512]{2,1,0:T(8,128)S(1)}, u32[]{:S(2)}, u32[]{:S(2)}) collective-permute-start(f32[2,32,512]{2,1,0:T(8,128)S(1)} %fusion.37), channel_id=1, source_target_pairs={{0,16},{4,20},{8,24},{12,28},{16,0},{20,4},{24,8},{28,12},{1,17},{... | collective-permute-start | bytes 393224 | tf_op jit(solution)/shard_map/ppermute | solution.py:72
  42.6 4.1 %slice-start = ((s8[6291456]{0:T(1024)(128)(4,1)}), s8[4194304]{0:T(1024)(128)(4,1)S(1)}, s32[]{:S(2)}) async-start(s8[6291456]{0:T(1024)(128)(4,1)} %bitcast.74), calls=%async_computation | async-start | bytes 8388608
  42.6 4.6 %slice-start.1 = ((s8[6291456]{0:T(1024)(128)(4,1)}), s8[2097152]{0:T(1024)(128)(4,1)S(1)}, s32[]{:S(2)}) async-start(s8[6291456]{0:T(1024)(128)(4,1)} %bitcast.74), calls=%async_computation.1 | async-start | bytes 4194304
  49.1 1.9 %collective-permute-start.3 = (f32[2,35,1536]{2,1,0:T(8,128)S(1)}, f32[2,35,1536]{2,1,0:T(8,128)S(1)}, u32[]{:S(2)}, u32[]{:S(2)}) collective-permute-start(f32[2,35,1536]{2,1,0:T(8,128)S(1)} %select_bitcast_fusion), channel_id=1, source_target_pairs={{0,1},{1,0},{2,3},{3,2},{4,5},{5,4},{6,7},{7,6},{8,9},{9,8},{10,11... | collective-permute-start | bytes 1290248 | tf_op jit(solution)/shard_map/ppermute | solution.py:86
  51.1 8.1 %collective-permute-start.4 = (f32[1,35,1536]{2,1,0:T(8,128)S(1)}, f32[1,35,1536]{2,1,0:T(8,128)S(1)}, u32[]{:S(2)}, u32[]{:S(2)}) collective-permute-start(f32[1,35,1536]{2,1,0:T(8,128)S(1)} %select_bitcast_fusion.1), channel_id=1, source_target_pairs={{0,2},{1,3},{2,0},{3,1},{4,6},{5,7},{6,4},{7,5},{8,10},{9,11},{10,... | collective-permute-start | bytes 645128 | tf_op jit(solution)/shard_map/ppermute | solution.py:86

commit v6 on v5

--- a/solution.py
+++ b/solution.py
@@ -8,8 +8,10 @@
 two_pi = 6.283185307179586
 box_length = 125.0
 
-_SIN_C = [(-1) ** n * math.pi ** (2 * n + 1) / float(math.factorial(2 * n + 1)) for n in range(6)]
-_COS_C = [(-1) ** n * math.pi ** (2 * n) / float(math.factorial(2 * n)) for n in range(7)]
+_SIN_C = [3.1415926399240375, -5.167710053300693, 2.5500768575243145, -0.5982866957251158,
+          0.0776479208030991]
+_COS_C = [0.9999999525693762, -4.934792730768449, 4.058409142115622, -1.3318612751935888,
+          0.2196570817648336]
 
 
 def turns_cos_sin(t):

time: 60.7 us -> 58.3 us (0.960)
  other arithmetic: 18.1 us -> 15.6 us
    convert_element_type x1, other arithmetic: 16.3 us -> 13.8 us  [local(): sin_table = sin_f.astype(jnp.bfloat16)]
where the time goes in v6:
time: 58.3 us; the launch traced here: 58 us
  waiting for transfers between devices  19.2 us (33%)
  other arithmetic  15.6 us (27%)
  starting transfers between devices  9.62 us (17%)
  matrix products  8.92 us (15%)
  local copies, waits for them, and re-layouts  3.14 us (5%)
  between operations  1.53 us (3%)
    convert_element_type x1, other arithmetic, local(): sin_table = sin_f.astype(jnp.bfloat16)  13.8 us
    ppermute x3, waiting for transfers between devices, butterfly_sum(): x = x + lax.ppermute(x, axis, [(i, i ^ step) for i in range(n)])  11.1 us
    ppermute x2, waiting for transfers between devices, halving_scatter(): held = keep + lax.ppermute(send, axis, [(i, i ^ step) for i in range(n)])  8.1 us
    ppermute x3, starting transfers between devices, butterfly_sum(): x = x + lax.ppermute(x, axis, [(i, i ^ step) for i in range(n)])  7.77 us
    dot_general x1, matrix products, local(): field = jnp.dot(cos_side, cos_table, preferred_element_type=jnp.float32)  4 us
    dot_general x1, matrix products, local(): lax.dot_general(charge_live, cos_table, tensor_product, preferred_element...  1.97 us
    dot_general x1, matrix products, local(): lax.dot_general(charge_live, sin_table, tensor_product, preferred_element...  1.95 us
    ppermute x2, starting transfers between devices, halving_scatter(): held = keep + lax.ppermute(send, axis, [(i, i ^ step) for i in range(n)])  1.85 us
  transfers between devices with their start and end apart: 5, of which 5 were waited for; matrix products, arithmetic and copies ran while one was open for 0% of the time, Pallas kernels for 0%

profile of v6, /device:TPU:0, one launch (start us, length us, event | category | flops | bytes accessed | tf_op | source)
XLA Modules:
  0.0 58.0 jit_solution(12189577112090013175)
XLA Ops:
  0.6 0.7 %convert_element_type.14 = f32[3,512]{1,0:T(4,128)S(1)} convert(s32[3,512]{1,0:T(4,128)} %param.7) | non-fusion elementwise | flops 1536 | bytes 12288 | tf_op jit(solution)/shard_map/convert_element_type | solution.py:102
  1.4 1.1 %fusion.31 = (f32[1,6144]{1,0:T(1,128)S(1)}, f32[1,6144]{1,0:T(1,128)S(1)}, f32[1,6144]{1,0:T(1,128)S(1)}) fusion(f32[3,6144]{1,0:T(4,128)} %param.5), kind=kLoop, calls=%fused_computation.77 | loop fusion | bytes 147456 | tf_op jit(solution)/shard_map/slice | solution.py:104
  2.5 0.0 copy-start.2
  2.5 13.8 %multiply_convert_fusion = (bf16[512,6144]{1,0:T(8,128)(2,1)S(1)}, bf16[512,6144]{1,0:T(8,128)(2,1)S(1)}) fusion(f32[6144]{0:T(1024)S(1)} %bitcast.82, f32[512]{0:T(512)S(1)} %bitcast.92, f32[6144]{0:T(1024)S(1)} %bitcast.83, f32[512]{0:T(512)S(1)} %bitcast.93, f32[6144]{0:T(1024)S(1)} %bitcast.81, f32[512]{0:T(512)S(1)} %bitcast.94), kind=kLoop, calls=%fused_computation | loop fusion | flops 103809024 | bytes 12662784 | tf_op jit(solution)/shard_map/convert_element_type | solution.py:110
  16.3 0.0 copy-start
  16.3 0.0 copy-start.1
  17.0 0.0 copy-done.2
  17.0 0.0 copy-start.3
  17.1 2.0 %convolution_bitcast_fusion = f32[1,32,512]{2,1,0:T(8,128)S(1)} fusion(bf16[512,6144]{1,0:T(8,128)(2,1)S(1)} %get-tuple-element.5, bf16[32,6144]{1,0:T(8,128)(2,1)S(1)} %copy-done.2, pred[6144]{0:T(1024)(128)(4,1)S(1)} %iota_compare_fusion), kind=kOutput, calls=%fused_computation.12 | convolution fusion | flops 201523200 | bytes 6756352 | tf_op jit(solution)/shard_map/dot_general | solution.py:116
  19.0 2.0 %convolution_bitcast_fusion.1 = f32[1,32,512]{2,1,0:T(8,128)S(1)} fusion(bf16[512,6144]{1,0:T(8,128)(2,1)S(1)} %get-tuple-element.4, bf16[32,6144]{1,0:T(8,128)(2,1)S(1)} %copy-done.2, pred[6144]{0:T(1024)(128)(4,1)S(1)} %iota_compare_fusion), kind=kOutput, calls=%fused_computation.13 | convolution fusion | flops 201523200 | bytes 6756352 | tf_op jit(solution)/shard_map/dot_general | solution.py:113
  21.0 0.0 copy-done
  21.0 0.0 copy-done.1
  21.0 3.0 %collective-permute-start = (f32[2,32,512]{2,1,0:T(8,128)S(1)}, f32[2,32,512]{2,1,0:T(8,128)S(1)}, u32[]{:S(2)}, u32[]{:S(2)}) collective-permute-start(f32[2,32,512]{2,1,0:T(8,128)S(1)} %pad_maximum_fusion.2), channel_id=1, source_target_pairs={{0,4},{4,0},{8,12},{12,8},{16,20},{20,16},{24,28},{28,24},{1,5},{5... | collective-permute-start | bytes 393224 | tf_op jit(solution)/shard_map/ppermute | solution.py:74
  24.1 3.5 %collective-permute-done = f32[2,32,512]{2,1,0:T(8,128)S(1)} collective-permute-done((f32[2,32,512]{2,1,0:T(8,128)S(1)}, f32[2,32,512]{2,1,0:T(8,128)S(1)}, u32[]{:S(2)}, u32[]{:S(2)}) %collective-permute-start) | collective-permute-done | bytes 131104 | tf_op jit(solution)/shard_map/ppermute | solution.py:74
  27.6 1.9 %collective-permute-start.1 = (f32[2,32,512]{2,1,0:T(8,128)S(1)}, f32[2,32,512]{2,1,0:T(8,128)S(1)}, u32[]{:S(2)}, u32[]{:S(2)}) collective-permute-start(f32[2,32,512]{2,1,0:T(8,128)S(1)} %fusion.27), channel_id=1, source_target_pairs={{0,8},{4,12},{8,0},{12,4},{16,24},{20,28},{24,16},{28,20},{1,9},{5... | collective-permute-start | bytes 393224 | tf_op jit(solution)/shard_map/ppermute | solution.py:74
  29.4 3.2 %collective-permute-done.1 = f32[2,32,512]{2,1,0:T(8,128)S(1)} collective-permute-done((f32[2,32,512]{2,1,0:T(8,128)S(1)}, f32[2,32,512]{2,1,0:T(8,128)S(1)}, u32[]{:S(2)}, u32[]{:S(2)}) %collective-permute-start.1) | collective-permute-done | bytes 131104 | tf_op jit(solution)/shard_map/ppermute | solution.py:74
  32.6 2.9 %collective-permute-start.2 = (f32[2,32,512]{2,1,0:T(8,128)S(1)}, f32[2,32,512]{2,1,0:T(8,128)S(1)}, u32[]{:S(2)}, u32[]{:S(2)}) collective-permute-start(f32[2,32,512]{2,1,0:T(8,128)S(1)} %fusion.36), channel_id=1, source_target_pairs={{0,16},{4,20},{8,24},{12,28},{16,0},{20,4},{24,8},{28,12},{1,17},{... | collective-permute-start | bytes 393224 | tf_op jit(solution)/shard_map/ppermute | solution.py:74
  35.5 0.0 copy-done.3
  35.5 4.5 %collective-permute-done.2 = f32[2,32,512]{2,1,0:T(8,128)S(1)} collective-permute-done((f32[2,32,512]{2,1,0:T(8,128)S(1)}, f32[2,32,512]{2,1,0:T(8,128)S(1)}, u32[]{:S(2)}, u32[]{:S(2)}) %collective-permute-start.2) | collective-permute-done | bytes 131104 | tf_op jit(solution)/shard_map/ppermute | solution.py:74
  40.0 0.1 multiply_convert_fusion.3
  40.1 0.0 slice-start
  40.1 0.0 slice-start.1
  40.2 4.0 %fusion.6 = f32[128,6144]{1,0:T(8,128)S(1)} fusion(bf16[512,6144]{1,0:T(8,128)(2,1)} %copy-done.1, bf16[32,512]{1,0:T(8,128)(2,1)S(1)} %get-tuple-element.45, bf16[32,512]{1,0:T(8,128)(2,1)S(1)} %get-tuple-element.44, bf16[32,512]{1,0:T(8,128)(2,1)S(1)} %get-tuple-element.46, bf16[32,512]{1,0:T(8,128)(2,1)S(1)} %get-tuple-element.29), kind=kOutput, calls=%fused_computation.34 | convolution fusion | flops 805830656 | bytes 9568256 | tf_op jit(solution)/shard_map/dot_general | solution.py:123
  44.2 0.0 slice-done
  44.2 0.6 %slice-done.1 = s8[2097152]{0:T(1024)(128)(4,1)S(1)} async-done(((s8[6291456]{0:T(1024)(128)(4,1)}), s8[2097152]{0:T(1024)(128)(4,1)S(1)}, s32[]{:S(2)}) %slice-start.1) | async-done | bytes 2097176
  44.8 1.0 %convolution_add_fusion = f32[128,6144]{1,0:T(8,128)S(1)} fusion(f32[128,6144]{1,0:T(8,128)S(1)} %fusion.6, bf16[512,6144]{1,0:T(8,128)(2,1)S(1)} %bitcast.75, bf16[32,512]{1,0:T(8,128)(2,1)S(1)} %get-tuple-element.28, bf16[32,512]{1,0:T(8,128)(2,1)S(1)} %get-tuple-element.27, bf16[32,512]{1,0:T(8,128)(2,1)S(1)} %get-tuple-element.11, ...), kind=kOutput, calls=%fused_computation.8 | convolution fusion | flops 806617088 | bytes 12713984 | tf_op jit(solution)/shard_map/dot_general | solution.py:124
  45.8 0.4 fusion.2
  46.3 0.1 pad_maximum_fusion
  46.4 0.1 slice_bitcast_fusion.5
  46.4 0.1 pad_maximum_fusion.1
  46.5 0.1 select_bitcast_fusion
  46.6 0.1 collective-permute-start.3
  46.7 1.8 %collective-permute-done.3 = f32[2,35,1536]{2,1,0:T(8,128)S(1)} collective-permute-done((f32[2,35,1536]{2,1,0:T(8,128)S(1)}, f32[2,35,1536]{2,1,0:T(8,128)S(1)}, u32[]{:S(2)}, u32[]{:S(2)}) %collective-permute-start.3) | collective-permute-done | bytes 430112 | tf_op jit(solution)/shard_map/ppermute | solution.py:88
  48.5 0.1 fusion.5
  48.6 1.8 %collective-permute-start.4 = (f32[1,35,1536]{2,1,0:T(8,128)S(1)}, f32[1,35,1536]{2,1,0:T(8,128)S(1)}, u32[]{:S(2)}, u32[]{:S(2)}) collective-permute-start(f32[1,35,1536]{2,1,0:T(8,128)S(1)} %select_bitcast_fusion.1), channel_id=1, source_target_pairs={{0,2},{1,3},{2,0},{3,1},{4,6},{5,7},{6,4},{7,5},{8,10},{9,11},{10,... | collective-permute-start | bytes 645128 | tf_op jit(solution)/shard_map/ppermute | solution.py:88
  50.4 6.3 %collective-permute-done.4 = f32[1,35,1536]{2,1,0:T(8,128)S(1)} collective-permute-done((f32[1,35,1536]{2,1,0:T(8,128)S(1)}, f32[1,35,1536]{2,1,0:T(8,128)S(1)}, u32[]{:S(2)}, u32[]{:S(2)}) %collective-permute-start.4) | collective-permute-done | bytes 215072 | tf_op jit(solution)/shard_map/ppermute | solution.py:88
  56.7 0.1 bitcast_add_fusion.1
  56.7 0.7 %slice_bitcast_fusion.6 = f32[32,1536]{1,0:T(8,128)} fusion(f32[1,35,1536]{2,1,0:T(8,128)S(1)} %bitcast_add_fusion.1), kind=kLoop, calls=%fused_computation.32 | loop fusion | bytes 393216 | tf_op jit(solution)/shard_map/slice | solution.py:135
  57.4 0.6 %slice_bitcast_fusion.9 = f32[3,1536]{1,0:T(4,128)} fusion(f32[1,35,1536]{2,1,0:T(8,128)S(1)} %bitcast_add_fusion.1), kind=kLoop, calls=%fused_computation.60 | loop fusion | bytes 36864 | tf_op jit(solution)/shard_map/slice | solution.py:135
  (10 shorter events, 0.2 us)
Async XLA Ops:
  2.5 14.6 %copy-start.2 = (bf16[32,6144]{1,0:T(8,128)(2,1)S(1)}, bf16[32,6144]{1,0:T(8,128)(2,1)}, u32[]{:S(2)}) copy-start(bf16[32,6144]{1,0:T(8,128)(2,1)} %param.6) | copy-start | bytes 1179652
  16.3 4.7 %copy-start = (bf16[512,6144]{1,0:T(8,128)(2,1)}, bf16[512,6144]{1,0:T(8,128)(2,1)S(1)}, u32[]{:S(2)}) copy-start(bf16[512,6144]{1,0:T(8,128)(2,1)S(1)} %get-tuple-element.5) | copy-start | bytes 18874372
  16.3 4.7 %copy-start.1 = (bf16[512,6144]{1,0:T(8,128)(2,1)}, bf16[512,6144]{1,0:T(8,128)(2,1)S(1)}, u32[]{:S(2)}) copy-start(bf16[512,6144]{1,0:T(8,128)(2,1)S(1)} %get-tuple-element.4) | copy-start | bytes 18874372
  17.0 18.5 %copy-start.3 = (f32[32]{0:T(128)S(1)}, f32[32]{0:T(128)}, u32[]{:S(2)}) copy-start(f32[32]{0:T(128)} %param.9) | copy-start | bytes 388
  21.0 6.5 %collective-permute-start = (f32[2,32,512]{2,1,0:T(8,128)S(1)}, f32[2,32,512]{2,1,0:T(8,128)S(1)}, u32[]{:S(2)}, u32[]{:S(2)}) collective-permute-start(f32[2,32,512]{2,1,0:T(8,128)S(1)} %pad_maximum_fusion.2), channel_id=1, source_target_pairs={{0,4},{4,0},{8,12},{12,8},{16,20},{20,16},{24,28},{28,24},{1,5},{5... | collective-permute-start | bytes 393224 | tf_op jit(solution)/shard_map/ppermute | solution.py:74
  27.6 5.0 %collective-permute-start.1 = (f32[2,32,512]{2,1,0:T(8,128)S(1)}, f32[2,32,512]{2,1,0:T(8,128)S(1)}, u32[]{:S(2)}, u32[]{:S(2)}) collective-permute-start(f32[2,32,512]{2,1,0:T(8,128)S(1)} %fusion.27), channel_id=1, source_target_pairs={{0,8},{4,12},{8,0},{12,4},{16,24},{20,28},{24,16},{28,20},{1,9},{5... | collective-permute-start | bytes 393224 | tf_op jit(solution)/shard_map/ppermute | solution.py:74
  32.6 7.3 %collective-permute-start.2 = (f32[2,32,512]{2,1,0:T(8,128)S(1)}, f32[2,32,512]{2,1,0:T(8,128)S(1)}, u32[]{:S(2)}, u32[]{:S(2)}) collective-permute-start(f32[2,32,512]{2,1,0:T(8,128)S(1)} %fusion.36), channel_id=1, source_target_pairs={{0,16},{4,20},{8,24},{12,28},{16,0},{20,4},{24,8},{28,12},{1,17},{... | collective-permute-start | bytes 393224 | tf_op jit(solution)/shard_map/ppermute | solution.py:74
  40.1 4.1 %slice-start = ((s8[6291456]{0:T(1024)(128)(4,1)}), s8[4194304]{0:T(1024)(128)(4,1)S(1)}, s32[]{:S(2)}) async-start(s8[6291456]{0:T(1024)(128)(4,1)} %bitcast.74), calls=%async_computation | async-start | bytes 8388608
  40.1 4.6 %slice-start.1 = ((s8[6291456]{0:T(1024)(128)(4,1)}), s8[2097152]{0:T(1024)(128)(4,1)S(1)}, s32[]{:S(2)}) async-start(s8[6291456]{0:T(1024)(128)(4,1)} %bitcast.74), calls=%async_computation.1 | async-start | bytes 4194304
  46.6 1.9 %collective-permute-start.3 = (f32[2,35,1536]{2,1,0:T(8,128)S(1)}, f32[2,35,1536]{2,1,0:T(8,128)S(1)}, u32[]{:S(2)}, u32[]{:S(2)}) collective-permute-start(f32[2,35,1536]{2,1,0:T(8,128)S(1)} %select_bitcast_fusion), channel_id=1, source_target_pairs={{0,1},{1,0},{2,3},{3,2},{4,5},{5,4},{6,7},{7,6},{8,9},{9,8},{10,11... | collective-permute-start | bytes 1290248 | tf_op jit(solution)/shard_map/ppermute | solution.py:88
  48.6 8.1 %collective-permute-start.4 = (f32[1,35,1536]{2,1,0:T(8,128)S(1)}, f32[1,35,1536]{2,1,0:T(8,128)S(1)}, u32[]{:S(2)}, u32[]{:S(2)}) collective-permute-start(f32[1,35,1536]{2,1,0:T(8,128)S(1)} %select_bitcast_fusion.1), channel_id=1, source_target_pairs={{0,2},{1,3},{2,0},{3,1},{4,6},{5,7},{6,4},{7,5},{8,10},{9,11},{10,... | collective-permute-start | bytes 645128 | tf_op jit(solution)/shard_map/ppermute | solution.py:88

commit v7 on v6

--- a/solution.py
+++ b/solution.py
@@ -12,20 +12,21 @@
           0.0776479208030991]
 _COS_C = [0.9999999525693762, -4.934792730768449, 4.058409142115622, -1.3318612751935888,
           0.2196570817648336]
+_ROOT2 = math.sqrt(2.0)
 
 
 def turns_cos_sin(t):
     r = t - jnp.floor(t + 0.5)
     r2 = r * r
-    s = jnp.float32(_SIN_C[-1])
+    s = jnp.float32(_SIN_C[-1] * _ROOT2)
     for coef in _SIN_C[-2::-1]:
-        s = s * r2 + jnp.float32(coef)
+        s = s * r2 + jnp.float32(coef * _ROOT2)
     s = s * r
-    c = jnp.float32(_COS_C[-1])
+    c = jnp.float32(_COS_C[-1] * _ROOT2)
     for coef in _COS_C[-2::-1]:
-        c = c * r2 + jnp.float32(coef)
-    cos_out = 1.0 - 2.0 * (s * s)
-    sin_out = 2.0 * (s * c)
+        c = c * r2 + jnp.float32(coef * _ROOT2)
+    cos_out = 1.0 - s * s
+    sin_out = s * c
     return cos_out, sin_out
 
 

time: 58.3 us -> 57.4 us (0.985)
  other arithmetic: 15.6 us -> 14.8 us
    convert_element_type x1, other arithmetic: 13.8 us -> 13 us  [local(): sin_table = sin_f.astype(jnp.bfloat16)]
where the time goes in v7:
time: 57.4 us; the launch traced here: 57.2 us
  waiting for transfers between devices  19.2 us (33%)
  other arithmetic  14.8 us (26%)
  starting transfers between devices  9.62 us (17%)
  matrix products  8.92 us (16%)
  local copies, waits for them, and re-layouts  3.14 us (5%)
  between operations  1.53 us (3%)
    convert_element_type x1, other arithmetic, local(): sin_table = sin_f.astype(jnp.bfloat16)  13 us
    ppermute x3, waiting for transfers between devices, butterfly_sum(): x = x + lax.ppermute(x, axis, [(i, i ^ step) for i in range(n)])  11.1 us
    ppermute x2, waiting for transfers between devices, halving_scatter(): held = keep + lax.ppermute(send, axis, [(i, i ^ step) for i in range(n)])  8.1 us
    ppermute x3, starting transfers between devices, butterfly_sum(): x = x + lax.ppermute(x, axis, [(i, i ^ step) for i in range(n)])  7.77 us
    dot_general x1, matrix products, local(): field = jnp.dot(cos_side, cos_table, preferred_element_type=jnp.float32)  4 us
    dot_general x1, matrix products, local(): lax.dot_general(charge_live, cos_table, tensor_product, preferred_element...  1.97 us
    dot_general x1, matrix products, local(): lax.dot_general(charge_live, sin_table, tensor_product, preferred_element...  1.95 us
    ppermute x2, starting transfers between devices, halving_scatter(): held = keep + lax.ppermute(send, axis, [(i, i ^ step) for i in range(n)])  1.85 us
  transfers between devices with their start and end apart: 5, of which 5 were waited for; matrix products, arithmetic and copies ran while one was open for 0% of the time, Pallas kernels for 0%

profile of v7, /device:TPU:0, one launch (start us, length us, event | category | flops | bytes accessed | tf_op | source)
XLA Modules:
  0.0 57.2 jit_solution(12232831345807673532)
XLA Ops:
  0.6 0.7 %convert_element_type.14 = f32[3,512]{1,0:T(4,128)S(1)} convert(s32[3,512]{1,0:T(4,128)} %param.7) | non-fusion elementwise | flops 1536 | bytes 12288 | tf_op jit(solution)/shard_map/convert_element_type | solution.py:103
  1.4 1.1 %fusion.31 = (f32[1,6144]{1,0:T(1,128)S(1)}, f32[1,6144]{1,0:T(1,128)S(1)}, f32[1,6144]{1,0:T(1,128)S(1)}) fusion(f32[3,6144]{1,0:T(4,128)} %param.5), kind=kLoop, calls=%fused_computation.77 | loop fusion | bytes 147456 | tf_op jit(solution)/shard_map/slice | solution.py:105
  2.5 0.0 copy-start.2
  2.5 13.0 %multiply_convert_fusion = (bf16[512,6144]{1,0:T(8,128)(2,1)S(1)}, bf16[512,6144]{1,0:T(8,128)(2,1)S(1)}) fusion(f32[6144]{0:T(1024)S(1)} %bitcast.82, f32[512]{0:T(512)S(1)} %bitcast.92, f32[6144]{0:T(1024)S(1)} %bitcast.83, f32[512]{0:T(512)S(1)} %bitcast.93, f32[6144]{0:T(1024)S(1)} %bitcast.81, f32[512]{0:T(512)S(1)} %bitcast.94), kind=kLoop, calls=%fused_computation | loop fusion | flops 97517568 | bytes 12662784 | tf_op jit(solution)/shard_map/convert_element_type | solution.py:111
  15.5 0.0 copy-start
  15.5 0.0 copy-start.1
  16.2 0.0 copy-done.2
  16.2 0.0 copy-start.3
  16.2 2.0 %convolution_bitcast_fusion = f32[1,32,512]{2,1,0:T(8,128)S(1)} fusion(bf16[512,6144]{1,0:T(8,128)(2,1)S(1)} %get-tuple-element.5, bf16[32,6144]{1,0:T(8,128)(2,1)S(1)} %copy-done.2, pred[6144]{0:T(1024)(128)(4,1)S(1)} %iota_compare_fusion), kind=kOutput, calls=%fused_computation.12 | convolution fusion | flops 201523200 | bytes 6756352 | tf_op jit(solution)/shard_map/dot_general | solution.py:117
  18.2 2.0 %convolution_bitcast_fusion.1 = f32[1,32,512]{2,1,0:T(8,128)S(1)} fusion(bf16[512,6144]{1,0:T(8,128)(2,1)S(1)} %get-tuple-element.4, bf16[32,6144]{1,0:T(8,128)(2,1)S(1)} %copy-done.2, pred[6144]{0:T(1024)(128)(4,1)S(1)} %iota_compare_fusion), kind=kOutput, calls=%fused_computation.13 | convolution fusion | flops 201523200 | bytes 6756352 | tf_op jit(solution)/shard_map/dot_general | solution.py:114
  20.2 0.0 copy-done
  20.2 0.0 copy-done.1
  20.2 3.0 %collective-permute-start = (f32[2,32,512]{2,1,0:T(8,128)S(1)}, f32[2,32,512]{2,1,0:T(8,128)S(1)}, u32[]{:S(2)}, u32[]{:S(2)}) collective-permute-start(f32[2,32,512]{2,1,0:T(8,128)S(1)} %pad_maximum_fusion.2), channel_id=1, source_target_pairs={{0,4},{4,0},{8,12},{12,8},{16,20},{20,16},{24,28},{28,24},{1,5},{5... | collective-permute-start | bytes 393224 | tf_op jit(solution)/shard_map/ppermute | solution.py:75
  23.2 3.5 %collective-permute-done = f32[2,32,512]{2,1,0:T(8,128)S(1)} collective-permute-done((f32[2,32,512]{2,1,0:T(8,128)S(1)}, f32[2,32,512]{2,1,0:T(8,128)S(1)}, u32[]{:S(2)}, u32[]{:S(2)}) %collective-permute-start) | collective-permute-done | bytes 131104 | tf_op jit(solution)/shard_map/ppermute | solution.py:75
  26.8 1.9 %collective-permute-start.1 = (f32[2,32,512]{2,1,0:T(8,128)S(1)}, f32[2,32,512]{2,1,0:T(8,128)S(1)}, u32[]{:S(2)}, u32[]{:S(2)}) collective-permute-start(f32[2,32,512]{2,1,0:T(8,128)S(1)} %fusion.27), channel_id=1, source_target_pairs={{0,8},{4,12},{8,0},{12,4},{16,24},{20,28},{24,16},{28,20},{1,9},{5... | collective-permute-start | bytes 393224 | tf_op jit(solution)/shard_map/ppermute | solution.py:75
  28.6 3.2 %collective-permute-done.1 = f32[2,32,512]{2,1,0:T(8,128)S(1)} collective-permute-done((f32[2,32,512]{2,1,0:T(8,128)S(1)}, f32[2,32,512]{2,1,0:T(8,128)S(1)}, u32[]{:S(2)}, u32[]{:S(2)}) %collective-permute-start.1) | collective-permute-done | bytes 131104 | tf_op jit(solution)/shard_map/ppermute | solution.py:75
  31.8 2.9 %collective-permute-start.2 = (f32[2,32,512]{2,1,0:T(8,128)S(1)}, f32[2,32,512]{2,1,0:T(8,128)S(1)}, u32[]{:S(2)}, u32[]{:S(2)}) collective-permute-start(f32[2,32,512]{2,1,0:T(8,128)S(1)} %fusion.36), channel_id=1, source_target_pairs={{0,16},{4,20},{8,24},{12,28},{16,0},{20,4},{24,8},{28,12},{1,17},{... | collective-permute-start | bytes 393224 | tf_op jit(solution)/shard_map/ppermute | solution.py:75
  34.7 0.0 copy-done.3
  34.7 4.5 %collective-permute-done.2 = f32[2,32,512]{2,1,0:T(8,128)S(1)} collective-permute-done((f32[2,32,512]{2,1,0:T(8,128)S(1)}, f32[2,32,512]{2,1,0:T(8,128)S(1)}, u32[]{:S(2)}, u32[]{:S(2)}) %collective-permute-start.2) | collective-permute-done | bytes 131104 | tf_op jit(solution)/shard_map/ppermute | solution.py:75
  39.2 0.1 multiply_convert_fusion.3
  39.3 0.0 slice-start
  39.3 0.0 slice-start.1
  39.3 4.0 %fusion.6 = f32[128,6144]{1,0:T(8,128)S(1)} fusion(bf16[512,6144]{1,0:T(8,128)(2,1)} %copy-done.1, bf16[32,512]{1,0:T(8,128)(2,1)S(1)} %get-tuple-element.45, bf16[32,512]{1,0:T(8,128)(2,1)S(1)} %get-tuple-element.44, bf16[32,512]{1,0:T(8,128)(2,1)S(1)} %get-tuple-element.46, bf16[32,512]{1,0:T(8,128)(2,1)S(1)} %get-tuple-element.29), kind=kOutput, calls=%fused_computation.34 | convolution fusion | flops 805830656 | bytes 9568256 | tf_op jit(solution)/shard_map/dot_general | solution.py:124
  43.4 0.0 slice-done
  43.4 0.6 %slice-done.1 = s8[2097152]{0:T(1024)(128)(4,1)S(1)} async-done(((s8[6291456]{0:T(1024)(128)(4,1)}), s8[2097152]{0:T(1024)(128)(4,1)S(1)}, s32[]{:S(2)}) %slice-start.1) | async-done | bytes 2097176
  44.0 1.0 %convolution_add_fusion = f32[128,6144]{1,0:T(8,128)S(1)} fusion(f32[128,6144]{1,0:T(8,128)S(1)} %fusion.6, bf16[512,6144]{1,0:T(8,128)(2,1)S(1)} %bitcast.75, bf16[32,512]{1,0:T(8,128)(2,1)S(1)} %get-tuple-element.28, bf16[32,512]{1,0:T(8,128)(2,1)S(1)} %get-tuple-element.27, bf16[32,512]{1,0:T(8,128)(2,1)S(1)} %get-tuple-element.11, ...), kind=kOutput, calls=%fused_computation.8 | convolution fusion | flops 806617088 | bytes 12713984 | tf_op jit(solution)/shard_map/dot_general | solution.py:125
  45.0 0.4 fusion.2
  45.4 0.1 pad_maximum_fusion
  45.6 0.1 slice_bitcast_fusion.5
  45.6 0.1 pad_maximum_fusion.1
  45.7 0.1 select_bitcast_fusion
  45.8 0.1 collective-permute-start.3
  45.9 1.8 %collective-permute-done.3 = f32[2,35,1536]{2,1,0:T(8,128)S(1)} collective-permute-done((f32[2,35,1536]{2,1,0:T(8,128)S(1)}, f32[2,35,1536]{2,1,0:T(8,128)S(1)}, u32[]{:S(2)}, u32[]{:S(2)}) %collective-permute-start.3) | collective-permute-done | bytes 430112 | tf_op jit(solution)/shard_map/ppermute | solution.py:89
  47.7 0.1 fusion.5
  47.8 1.8 %collective-permute-start.4 = (f32[1,35,1536]{2,1,0:T(8,128)S(1)}, f32[1,35,1536]{2,1,0:T(8,128)S(1)}, u32[]{:S(2)}, u32[]{:S(2)}) collective-permute-start(f32[1,35,1536]{2,1,0:T(8,128)S(1)} %select_bitcast_fusion.1), channel_id=1, source_target_pairs={{0,2},{1,3},{2,0},{3,1},{4,6},{5,7},{6,4},{7,5},{8,10},{9,11},{10,... | collective-permute-start | bytes 645128 | tf_op jit(solution)/shard_map/ppermute | solution.py:89
  49.6 6.3 %collective-permute-done.4 = f32[1,35,1536]{2,1,0:T(8,128)S(1)} collective-permute-done((f32[1,35,1536]{2,1,0:T(8,128)S(1)}, f32[1,35,1536]{2,1,0:T(8,128)S(1)}, u32[]{:S(2)}, u32[]{:S(2)}) %collective-permute-start.4) | collective-permute-done | bytes 215072 | tf_op jit(solution)/shard_map/ppermute | solution.py:89
  55.9 0.1 bitcast_add_fusion.1
  55.9 0.7 %slice_bitcast_fusion.6 = f32[32,1536]{1,0:T(8,128)} fusion(f32[1,35,1536]{2,1,0:T(8,128)S(1)} %bitcast_add_fusion.1), kind=kLoop, calls=%fused_computation.32 | loop fusion | bytes 393216 | tf_op jit(solution)/shard_map/slice | solution.py:136
  56.6 0.6 %slice_bitcast_fusion.9 = f32[3,1536]{1,0:T(4,128)} fusion(f32[1,35,1536]{2,1,0:T(8,128)S(1)} %bitcast_add_fusion.1), kind=kLoop, calls=%fused_computation.60 | loop fusion | bytes 36864 | tf_op jit(solution)/shard_map/slice | solution.py:136
  (10 shorter events, 0.2 us)
Async XLA Ops:
  2.5 13.8 %copy-start.2 = (bf16[32,6144]{1,0:T(8,128)(2,1)S(1)}, bf16[32,6144]{1,0:T(8,128)(2,1)}, u32[]{:S(2)}) copy-start(bf16[32,6144]{1,0:T(8,128)(2,1)} %param.6) | copy-start | bytes 1179652
  15.5 4.7 %copy-start = (bf16[512,6144]{1,0:T(8,128)(2,1)}, bf16[512,6144]{1,0:T(8,128)(2,1)S(1)}, u32[]{:S(2)}) copy-start(bf16[512,6144]{1,0:T(8,128)(2,1)S(1)} %get-tuple-element.5) | copy-start | bytes 18874372
  15.5 4.7 %copy-start.1 = (bf16[512,6144]{1,0:T(8,128)(2,1)}, bf16[512,6144]{1,0:T(8,128)(2,1)S(1)}, u32[]{:S(2)}) copy-start(bf16[512,6144]{1,0:T(8,128)(2,1)S(1)} %get-tuple-element.4) | copy-start | bytes 18874372
  16.2 18.5 %copy-start.3 = (f32[32]{0:T(128)S(1)}, f32[32]{0:T(128)}, u32[]{:S(2)}) copy-start(f32[32]{0:T(128)} %param.9) | copy-start | bytes 388
  20.2 6.5 %collective-permute-start = (f32[2,32,512]{2,1,0:T(8,128)S(1)}, f32[2,32,512]{2,1,0:T(8,128)S(1)}, u32[]{:S(2)}, u32[]{:S(2)}) collective-permute-start(f32[2,32,512]{2,1,0:T(8,128)S(1)} %pad_maximum_fusion.2), channel_id=1, source_target_pairs={{0,4},{4,0},{8,12},{12,8},{16,20},{20,16},{24,28},{28,24},{1,5},{5... | collective-permute-start | bytes 393224 | tf_op jit(solution)/shard_map/ppermute | solution.py:75
  26.8 5.0 %collective-permute-start.1 = (f32[2,32,512]{2,1,0:T(8,128)S(1)}, f32[2,32,512]{2,1,0:T(8,128)S(1)}, u32[]{:S(2)}, u32[]{:S(2)}) collective-permute-start(f32[2,32,512]{2,1,0:T(8,128)S(1)} %fusion.27), channel_id=1, source_target_pairs={{0,8},{4,12},{8,0},{12,4},{16,24},{20,28},{24,16},{28,20},{1,9},{5... | collective-permute-start | bytes 393224 | tf_op jit(solution)/shard_map/ppermute | solution.py:75
  31.8 7.3 %collective-permute-start.2 = (f32[2,32,512]{2,1,0:T(8,128)S(1)}, f32[2,32,512]{2,1,0:T(8,128)S(1)}, u32[]{:S(2)}, u32[]{:S(2)}) collective-permute-start(f32[2,32,512]{2,1,0:T(8,128)S(1)} %fusion.36), channel_id=1, source_target_pairs={{0,16},{4,20},{8,24},{12,28},{16,0},{20,4},{24,8},{28,12},{1,17},{... | collective-permute-start | bytes 393224 | tf_op jit(solution)/shard_map/ppermute | solution.py:75
  39.3 4.1 %slice-start = ((s8[6291456]{0:T(1024)(128)(4,1)}), s8[4194304]{0:T(1024)(128)(4,1)S(1)}, s32[]{:S(2)}) async-start(s8[6291456]{0:T(1024)(128)(4,1)} %bitcast.74), calls=%async_computation | async-start | bytes 8388608
  39.3 4.6 %slice-start.1 = ((s8[6291456]{0:T(1024)(128)(4,1)}), s8[2097152]{0:T(1024)(128)(4,1)S(1)}, s32[]{:S(2)}) async-start(s8[6291456]{0:T(1024)(128)(4,1)} %bitcast.74), calls=%async_computation.1 | async-start | bytes 4194304
  45.8 1.9 %collective-permute-start.3 = (f32[2,35,1536]{2,1,0:T(8,128)S(1)}, f32[2,35,1536]{2,1,0:T(8,128)S(1)}, u32[]{:S(2)}, u32[]{:S(2)}) collective-permute-start(f32[2,35,1536]{2,1,0:T(8,128)S(1)} %select_bitcast_fusion), channel_id=1, source_target_pairs={{0,1},{1,0},{2,3},{3,2},{4,5},{5,4},{6,7},{7,6},{8,9},{9,8},{10,11... | collective-permute-start | bytes 1290248 | tf_op jit(solution)/shard_map/ppermute | solution.py:89
  47.8 8.1 %collective-permute-start.4 = (f32[1,35,1536]{2,1,0:T(8,128)S(1)}, f32[1,35,1536]{2,1,0:T(8,128)S(1)}, u32[]{:S(2)}, u32[]{:S(2)}) collective-permute-start(f32[1,35,1536]{2,1,0:T(8,128)S(1)} %select_bitcast_fusion.1), channel_id=1, source_target_pairs={{0,2},{1,3},{2,0},{3,1},{4,6},{5,7},{6,4},{7,5},{8,10},{9,11},{10,... | collective-permute-start | bytes 645128 | tf_op jit(solution)/shard_map/ppermute | solution.py:89

commit v8 on v7

--- a/solution.py
+++ b/solution.py
@@ -86,7 +86,12 @@
         bit = (me // step) % 2
         keep = jnp.where(bit == 0, pairs[:, 0], pairs[:, 1])
         send = jnp.where(bit == 0, pairs[:, 1], pairs[:, 0])
-        held = keep + lax.ppermute(send, axis, [(i, i ^ step) for i in range(n)])
+        pairs_list = [(i, i ^ step) for i in range(n)]
+        if step >= 2:
+            recv = lax.ppermute(send.astype(jnp.bfloat16), axis, pairs_list).astype(jnp.float32)
+        else:
+            recv = lax.ppermute(send, axis, pairs_list)
+        held = keep + recv
         step *= 2
     return held[0]
 

time: 57.4 us -> 54.8 us (0.955)
  waiting for transfers between devices: 19.2 us -> 16.6 us
    ppermute x2, waiting for transfers between devices: 8.1 us -> 5.47 us  [the longest x1 3.65 us: halving_scatter(): lax.ppermute(send.astype(jnp.bfloat16), axis, pairs_list)]
where the time goes in v8:
time: 54.8 us; the launch traced here: 54.6 us
  waiting for transfers between devices  16.6 us (30%)
  other arithmetic  14.8 us (27%)
  starting transfers between devices  9.62 us (18%)
  matrix products  8.92 us (16%)
  local copies, waits for them, and re-layouts  3.14 us (6%)
  between operations  1.53 us (3%)
    convert_element_type x1, other arithmetic, local(): sin_table = sin_f.astype(jnp.bfloat16)  13 us
    ppermute x3, waiting for transfers between devices, butterfly_sum(): x = x + lax.ppermute(x, axis, [(i, i ^ step) for i in range(n)])  11.1 us
    ppermute x3, starting transfers between devices, butterfly_sum(): x = x + lax.ppermute(x, axis, [(i, i ^ step) for i in range(n)])  7.77 us
    dot_general x1, matrix products, local(): field = jnp.dot(cos_side, cos_table, preferred_element_type=jnp.float32)  4 us
    ppermute x1, waiting for transfers between devices, halving_scatter(): lax.ppermute(send.astype(jnp.bfloat16), axis, pairs_list)  3.65 us
    dot_general x1, matrix products, local(): lax.dot_general(charge_live, cos_table, tensor_product, preferred_element...  1.97 us
    dot_general x1, matrix products, local(): lax.dot_general(charge_live, sin_table, tensor_product, preferred_element...  1.95 us
    ppermute x1, waiting for transfers between devices, halving_scatter(): recv = lax.ppermute(send, axis, pairs_list)  1.82 us
  transfers between devices with their start and end apart: 5, of which 5 were waited for; matrix products, arithmetic and copies ran while one was open for 0% of the time, Pallas kernels for 0%

profile of v8, /device:TPU:0, one launch (start us, length us, event | category | flops | bytes accessed | tf_op | source)
XLA Modules:
  0.0 54.6 jit_solution(17942654359229257082)
XLA Ops:
  0.6 0.7 %convert_element_type.31 = f32[3,512]{1,0:T(4,128)S(1)} convert(s32[3,512]{1,0:T(4,128)} %param.7) | non-fusion elementwise | flops 1536 | bytes 12288 | tf_op jit(solution)/shard_map/convert_element_type | solution.py:108
  1.4 1.1 %fusion.32 = (f32[1,6144]{1,0:T(1,128)S(1)}, f32[1,6144]{1,0:T(1,128)S(1)}, f32[1,6144]{1,0:T(1,128)S(1)}) fusion(f32[3,6144]{1,0:T(4,128)} %param.5), kind=kLoop, calls=%fused_computation.78 | loop fusion | bytes 147456 | tf_op jit(solution)/shard_map/slice | solution.py:110
  2.5 0.0 copy-start.2
  2.5 13.0 %multiply_convert_fusion = (bf16[512,6144]{1,0:T(8,128)(2,1)S(1)}, bf16[512,6144]{1,0:T(8,128)(2,1)S(1)}) fusion(f32[6144]{0:T(1024)S(1)} %bitcast.82, f32[512]{0:T(512)S(1)} %bitcast.92, f32[6144]{0:T(1024)S(1)} %bitcast.83, f32[512]{0:T(512)S(1)} %bitcast.93, f32[6144]{0:T(1024)S(1)} %bitcast.81, f32[512]{0:T(512)S(1)} %bitcast.94), kind=kLoop, calls=%fused_computation | loop fusion | flops 97517568 | bytes 12662784 | tf_op jit(solution)/shard_map/convert_element_type | solution.py:116
  15.5 0.0 copy-start
  15.5 0.0 copy-start.1
  16.2 0.0 copy-done.2
  16.2 0.0 copy-start.3
  16.2 2.0 %convolution_bitcast_fusion = f32[1,32,512]{2,1,0:T(8,128)S(1)} fusion(bf16[512,6144]{1,0:T(8,128)(2,1)S(1)} %get-tuple-element.5, bf16[32,6144]{1,0:T(8,128)(2,1)S(1)} %copy-done.2, pred[6144]{0:T(1024)(128)(4,1)S(1)} %iota_compare_fusion), kind=kOutput, calls=%fused_computation.12 | convolution fusion | flops 201523200 | bytes 6756352 | tf_op jit(solution)/shard_map/dot_general | solution.py:122
  18.2 2.0 %convolution_bitcast_fusion.1 = f32[1,32,512]{2,1,0:T(8,128)S(1)} fusion(bf16[512,6144]{1,0:T(8,128)(2,1)S(1)} %get-tuple-element.4, bf16[32,6144]{1,0:T(8,128)(2,1)S(1)} %copy-done.2, pred[6144]{0:T(1024)(128)(4,1)S(1)} %iota_compare_fusion), kind=kOutput, calls=%fused_computation.13 | convolution fusion | flops 201523200 | bytes 6756352 | tf_op jit(solution)/shard_map/dot_general | solution.py:119
  20.2 0.0 copy-done
  20.2 0.0 copy-done.1
  20.2 3.0 %collective-permute-start = (f32[2,32,512]{2,1,0:T(8,128)S(1)}, f32[2,32,512]{2,1,0:T(8,128)S(1)}, u32[]{:S(2)}, u32[]{:S(2)}) collective-permute-start(f32[2,32,512]{2,1,0:T(8,128)S(1)} %pad_maximum_fusion.2), channel_id=1, source_target_pairs={{0,4},{4,0},{8,12},{12,8},{16,20},{20,16},{24,28},{28,24},{1,5},{5... | collective-permute-start | bytes 393224 | tf_op jit(solution)/shard_map/ppermute | solution.py:75
  23.2 3.5 %collective-permute-done = f32[2,32,512]{2,1,0:T(8,128)S(1)} collective-permute-done((f32[2,32,512]{2,1,0:T(8,128)S(1)}, f32[2,32,512]{2,1,0:T(8,128)S(1)}, u32[]{:S(2)}, u32[]{:S(2)}) %collective-permute-start) | collective-permute-done | bytes 131104 | tf_op jit(solution)/shard_map/ppermute | solution.py:75
  26.8 1.9 %collective-permute-start.1 = (f32[2,32,512]{2,1,0:T(8,128)S(1)}, f32[2,32,512]{2,1,0:T(8,128)S(1)}, u32[]{:S(2)}, u32[]{:S(2)}) collective-permute-start(f32[2,32,512]{2,1,0:T(8,128)S(1)} %fusion.28), channel_id=1, source_target_pairs={{0,8},{4,12},{8,0},{12,4},{16,24},{20,28},{24,16},{28,20},{1,9},{5... | collective-permute-start | bytes 393224 | tf_op jit(solution)/shard_map/ppermute | solution.py:75
  28.6 3.2 %collective-permute-done.1 = f32[2,32,512]{2,1,0:T(8,128)S(1)} collective-permute-done((f32[2,32,512]{2,1,0:T(8,128)S(1)}, f32[2,32,512]{2,1,0:T(8,128)S(1)}, u32[]{:S(2)}, u32[]{:S(2)}) %collective-permute-start.1) | collective-permute-done | bytes 131104 | tf_op jit(solution)/shard_map/ppermute | solution.py:75
  31.8 2.9 %collective-permute-start.2 = (f32[2,32,512]{2,1,0:T(8,128)S(1)}, f32[2,32,512]{2,1,0:T(8,128)S(1)}, u32[]{:S(2)}, u32[]{:S(2)}) collective-permute-start(f32[2,32,512]{2,1,0:T(8,128)S(1)} %fusion.37), channel_id=1, source_target_pairs={{0,16},{4,20},{8,24},{12,28},{16,0},{20,4},{24,8},{28,12},{1,17},{... | collective-permute-start | bytes 393224 | tf_op jit(solution)/shard_map/ppermute | solution.py:75
  34.7 0.0 copy-done.3
  34.7 4.5 %collective-permute-done.2 = f32[2,32,512]{2,1,0:T(8,128)S(1)} collective-permute-done((f32[2,32,512]{2,1,0:T(8,128)S(1)}, f32[2,32,512]{2,1,0:T(8,128)S(1)}, u32[]{:S(2)}, u32[]{:S(2)}) %collective-permute-start.2) | collective-permute-done | bytes 131104 | tf_op jit(solution)/shard_map/ppermute | solution.py:75
  39.2 0.1 multiply_convert_fusion.3
  39.3 0.0 slice-start
  39.3 0.0 slice-start.1
  39.3 4.0 %fusion.6 = f32[128,6144]{1,0:T(8,128)S(1)} fusion(bf16[512,6144]{1,0:T(8,128)(2,1)} %copy-done.1, bf16[32,512]{1,0:T(8,128)(2,1)S(1)} %get-tuple-element.45, bf16[32,512]{1,0:T(8,128)(2,1)S(1)} %get-tuple-element.44, bf16[32,512]{1,0:T(8,128)(2,1)S(1)} %get-tuple-element.46, bf16[32,512]{1,0:T(8,128)(2,1)S(1)} %get-tuple-element.29), kind=kOutput, calls=%fused_computation.34 | convolution fusion | flops 805830656 | bytes 9568256 | tf_op jit(solution)/shard_map/dot_general | solution.py:129
  43.4 0.0 slice-done
  43.4 0.6 %slice-done.1 = s8[2097152]{0:T(1024)(128)(4,1)S(1)} async-done(((s8[6291456]{0:T(1024)(128)(4,1)}), s8[2097152]{0:T(1024)(128)(4,1)S(1)}, s32[]{:S(2)}) %slice-start.1) | async-done | bytes 2097176
  44.0 1.0 %convolution_add_fusion = f32[128,6144]{1,0:T(8,128)S(1)} fusion(f32[128,6144]{1,0:T(8,128)S(1)} %fusion.6, bf16[512,6144]{1,0:T(8,128)(2,1)S(1)} %bitcast.75, bf16[32,512]{1,0:T(8,128)(2,1)S(1)} %get-tuple-element.28, bf16[32,512]{1,0:T(8,128)(2,1)S(1)} %get-tuple-element.27, bf16[32,512]{1,0:T(8,128)(2,1)S(1)} %get-tuple-element.11, ...), kind=kOutput, calls=%fused_computation.8 | convolution fusion | flops 806617088 | bytes 12713984 | tf_op jit(solution)/shard_map/dot_general | solution.py:130
  45.0 0.4 fusion.2
  45.4 0.1 pad_maximum_fusion
  45.6 0.1 slice_bitcast_fusion.5
  45.6 0.1 pad_maximum_fusion.1
  45.7 0.1 select_bitcast_fusion
  45.8 0.1 collective-permute-start.3
  45.9 1.8 %collective-permute-done.3 = f32[2,35,1536]{2,1,0:T(8,128)S(1)} collective-permute-done((f32[2,35,1536]{2,1,0:T(8,128)S(1)}, f32[2,35,1536]{2,1,0:T(8,128)S(1)}, u32[]{:S(2)}, u32[]{:S(2)}) %collective-permute-start.3) | collective-permute-done | bytes 430112 | tf_op jit(solution)/shard_map/ppermute | solution.py:93
  47.7 0.1 fusion.5
  47.8 1.8 %collective-permute-start.4 = (bf16[1,35,1536]{2,1,0:T(8,128)(2,1)S(1)}, bf16[1,35,1536]{2,1,0:T(8,128)(2,1)S(1)}, u32[]{:S(2)}, u32[]{:S(2)}) collective-permute-start(bf16[1,35,1536]{2,1,0:T(8,128)(2,1)S(1)} %fusion.21), channel_id=1, source_target_pairs={{0,2},{1,3},{2,0},{3,1},{4,6},{5,7},{6,4},{7,5},{8,10},{9,11},{10,... | collective-permute-start | bytes 322568 | tf_op jit(solution)/shard_map/ppermute | solution.py:91
  49.6 3.7 %collective-permute-done.4 = bf16[1,35,1536]{2,1,0:T(8,128)(2,1)S(1)} collective-permute-done((bf16[1,35,1536]{2,1,0:T(8,128)(2,1)S(1)}, bf16[1,35,1536]{2,1,0:T(8,128)(2,1)S(1)}, u32[]{:S(2)}, u32[]{:S(2)}) %collective-permute-start.4) | collective-permute-done | bytes 107552 | tf_op jit(solution)/shard_map/ppermute | solution.py:91
  53.3 0.7 %slice_bitcast_fusion.6 = f32[32,1536]{1,0:T(8,128)} fusion(f32[1,35,1536]{2,1,0:T(8,128)S(1)} %bitcast_add_fusion.1), kind=kLoop, calls=%fused_computation.32 | loop fusion | bytes 393216 | tf_op jit(solution)/shard_map/slice | solution.py:141
  54.0 0.6 %slice_bitcast_fusion.9 = f32[3,1536]{1,0:T(4,128)} fusion(f32[1,35,1536]{2,1,0:T(8,128)S(1)} %bitcast_add_fusion.1), kind=kLoop, calls=%fused_computation.61 | loop fusion | bytes 36864 | tf_op jit(solution)/shard_map/slice | solution.py:141
  (11 shorter events, 0.2 us)
Async XLA Ops:
  2.5 13.8 %copy-start.2 = (bf16[32,6144]{1,0:T(8,128)(2,1)S(1)}, bf16[32,6144]{1,0:T(8,128)(2,1)}, u32[]{:S(2)}) copy-start(bf16[32,6144]{1,0:T(8,128)(2,1)} %param.6) | copy-start | bytes 1179652
  15.5 4.7 %copy-start = (bf16[512,6144]{1,0:T(8,128)(2,1)}, bf16[512,6144]{1,0:T(8,128)(2,1)S(1)}, u32[]{:S(2)}) copy-start(bf16[512,6144]{1,0:T(8,128)(2,1)S(1)} %get-tuple-element.5) | copy-start | bytes 18874372
  15.5 4.7 %copy-start.1 = (bf16[512,6144]{1,0:T(8,128)(2,1)}, bf16[512,6144]{1,0:T(8,128)(2,1)S(1)}, u32[]{:S(2)}) copy-start(bf16[512,6144]{1,0:T(8,128)(2,1)S(1)} %get-tuple-element.4) | copy-start | bytes 18874372
  16.2 18.5 %copy-start.3 = (f32[32]{0:T(128)S(1)}, f32[32]{0:T(128)}, u32[]{:S(2)}) copy-start(f32[32]{0:T(128)} %param.9) | copy-start | bytes 388
  20.2 6.5 %collective-permute-start = (f32[2,32,512]{2,1,0:T(8,128)S(1)}, f32[2,32,512]{2,1,0:T(8,128)S(1)}, u32[]{:S(2)}, u32[]{:S(2)}) collective-permute-start(f32[2,32,512]{2,1,0:T(8,128)S(1)} %pad_maximum_fusion.2), channel_id=1, source_target_pairs={{0,4},{4,0},{8,12},{12,8},{16,20},{20,16},{24,28},{28,24},{1,5},{5... | collective-permute-start | bytes 393224 | tf_op jit(solution)/shard_map/ppermute | solution.py:75
  26.8 5.0 %collective-permute-start.1 = (f32[2,32,512]{2,1,0:T(8,128)S(1)}, f32[2,32,512]{2,1,0:T(8,128)S(1)}, u32[]{:S(2)}, u32[]{:S(2)}) collective-permute-start(f32[2,32,512]{2,1,0:T(8,128)S(1)} %fusion.28), channel_id=1, source_target_pairs={{0,8},{4,12},{8,0},{12,4},{16,24},{20,28},{24,16},{28,20},{1,9},{5... | collective-permute-start | bytes 393224 | tf_op jit(solution)/shard_map/ppermute | solution.py:75
  31.8 7.3 %collective-permute-start.2 = (f32[2,32,512]{2,1,0:T(8,128)S(1)}, f32[2,32,512]{2,1,0:T(8,128)S(1)}, u32[]{:S(2)}, u32[]{:S(2)}) collective-permute-start(f32[2,32,512]{2,1,0:T(8,128)S(1)} %fusion.37), channel_id=1, source_target_pairs={{0,16},{4,20},{8,24},{12,28},{16,0},{20,4},{24,8},{28,12},{1,17},{... | collective-permute-start | bytes 393224 | tf_op jit(solution)/shard_map/ppermute | solution.py:75
  39.3 4.1 %slice-start = ((s8[6291456]{0:T(1024)(128)(4,1)}), s8[4194304]{0:T(1024)(128)(4,1)S(1)}, s32[]{:S(2)}) async-start(s8[6291456]{0:T(1024)(128)(4,1)} %bitcast.74), calls=%async_computation | async-start | bytes 8388608
  39.3 4.6 %slice-start.1 = ((s8[6291456]{0:T(1024)(128)(4,1)}), s8[2097152]{0:T(1024)(128)(4,1)S(1)}, s32[]{:S(2)}) async-start(s8[6291456]{0:T(1024)(128)(4,1)} %bitcast.74), calls=%async_computation.1 | async-start | bytes 4194304
  45.8 1.9 %collective-permute-start.3 = (f32[2,35,1536]{2,1,0:T(8,128)S(1)}, f32[2,35,1536]{2,1,0:T(8,128)S(1)}, u32[]{:S(2)}, u32[]{:S(2)}) collective-permute-start(f32[2,35,1536]{2,1,0:T(8,128)S(1)} %select_bitcast_fusion), channel_id=1, source_target_pairs={{0,1},{1,0},{2,3},{3,2},{4,5},{5,4},{6,7},{7,6},{8,9},{9,8},{10,11... | collective-permute-start | bytes 1290248 | tf_op jit(solution)/shard_map/ppermute | solution.py:93
  47.8 5.4 %collective-permute-start.4 = (bf16[1,35,1536]{2,1,0:T(8,128)(2,1)S(1)}, bf16[1,35,1536]{2,1,0:T(8,128)(2,1)S(1)}, u32[]{:S(2)}, u32[]{:S(2)}) collective-permute-start(bf16[1,35,1536]{2,1,0:T(8,128)(2,1)S(1)} %fusion.21), channel_id=1, source_target_pairs={{0,2},{1,3},{2,0},{3,1},{4,6},{5,7},{6,4},{7,5},{8,10},{9,11},{10,... | collective-permute-start | bytes 322568 | tf_op jit(solution)/shard_map/ppermute | solution.py:91

commit v9 on v8

--- a/solution.py
+++ b/solution.py
@@ -70,10 +70,10 @@
 
 
 def butterfly_sum(x, axis, n):
-    step = 1
-    while step < n:
+    step = n // 2
+    while step >= 1:
         x = x + lax.ppermute(x, axis, [(i, i ^ step) for i in range(n)])
-        step *= 2
+        step //= 2
     return x
 
 

time: 54.8 us -> 56.4 us (1.029)
  waiting for transfers between devices: 16.6 us -> 19.6 us
  starting transfers between devices: 9.62 us -> 8.2 us
    ppermute x3, waiting for transfers between devices: 11.1 us -> 13.9 us  [butterfly_sum(): x = x + lax.ppermute(x, axis, [(i, i ^ step) for i in range(n)])]
    ppermute x3, starting transfers between devices: 7.77 us -> 6.52 us  [butterfly_sum(): x = x + lax.ppermute(x, axis, [(i, i ^ step) for i in range(n)])]
where the time goes in v9:
time: 56.4 us; the launch traced here: 56.2 us
  waiting for transfers between devices  19.6 us (35%)
  other arithmetic  14.8 us (26%)
  matrix products  8.92 us (16%)
  starting transfers between devices  8.2 us (15%)
  local copies, waits for them, and re-layouts  3.14 us (6%)
  between operations  1.53 us (3%)
    ppermute x3, waiting for transfers between devices, butterfly_sum(): x = x + lax.ppermute(x, axis, [(i, i ^ step) for i in range(n)])  13.9 us
    convert_element_type x1, other arithmetic, local(): sin_table = sin_f.astype(jnp.bfloat16)  13 us
    ppermute x3, starting transfers between devices, butterfly_sum(): x = x + lax.ppermute(x, axis, [(i, i ^ step) for i in range(n)])  6.52 us
    dot_general x1, matrix products, local(): field = jnp.dot(cos_side, cos_table, preferred_element_type=jnp.float32)  4 us
    ppermute x1, waiting for transfers between devices, halving_scatter(): lax.ppermute(send.astype(jnp.bfloat16), axis, pairs_list)  3.82 us
    dot_general x1, matrix products, local(): lax.dot_general(charge_live, cos_table, tensor_product, preferred_element...  1.97 us
    dot_general x1, matrix products, local(): lax.dot_general(charge_live, sin_table, tensor_product, preferred_element...  1.95 us
    ppermute x1, waiting for transfers between devices, halving_scatter(): recv = lax.ppermute(send, axis, pairs_list)  1.82 us
  transfers between devices with their start and end apart: 5, of which 5 were waited for; matrix products, arithmetic and copies ran while one was open for 0% of the time, Pallas kernels for 0%

profile of v9, /device:TPU:0, one launch (start us, length us, event | category | flops | bytes accessed | tf_op | source)
XLA Modules:
  0.0 56.2 jit_solution(14579141954130922903)
XLA Ops:
  0.6 0.7 %convert_element_type.31 = f32[3,512]{1,0:T(4,128)S(1)} convert(s32[3,512]{1,0:T(4,128)} %param.7) | non-fusion elementwise | flops 1536 | bytes 12288 | tf_op jit(solution)/shard_map/convert_element_type | solution.py:108
  1.4 1.1 %fusion.32 = (f32[1,6144]{1,0:T(1,128)S(1)}, f32[1,6144]{1,0:T(1,128)S(1)}, f32[1,6144]{1,0:T(1,128)S(1)}) fusion(f32[3,6144]{1,0:T(4,128)} %param.5), kind=kLoop, calls=%fused_computation.78 | loop fusion | bytes 147456 | tf_op jit(solution)/shard_map/slice | solution.py:110
  2.5 0.0 copy-start.2
  2.5 13.0 %multiply_convert_fusion = (bf16[512,6144]{1,0:T(8,128)(2,1)S(1)}, bf16[512,6144]{1,0:T(8,128)(2,1)S(1)}) fusion(f32[6144]{0:T(1024)S(1)} %bitcast.82, f32[512]{0:T(512)S(1)} %bitcast.92, f32[6144]{0:T(1024)S(1)} %bitcast.83, f32[512]{0:T(512)S(1)} %bitcast.93, f32[6144]{0:T(1024)S(1)} %bitcast.81, f32[512]{0:T(512)S(1)} %bitcast.94), kind=kLoop, calls=%fused_computation | loop fusion | flops 97517568 | bytes 12662784 | tf_op jit(solution)/shard_map/convert_element_type | solution.py:116
  15.5 0.0 copy-start
  15.5 0.0 copy-start.1
  16.2 0.0 copy-done.2
  16.2 0.0 copy-start.3
  16.2 2.0 %convolution_bitcast_fusion = f32[1,32,512]{2,1,0:T(8,128)S(1)} fusion(bf16[512,6144]{1,0:T(8,128)(2,1)S(1)} %get-tuple-element.5, bf16[32,6144]{1,0:T(8,128)(2,1)S(1)} %copy-done.2, pred[6144]{0:T(1024)(128)(4,1)S(1)} %iota_compare_fusion), kind=kOutput, calls=%fused_computation.12 | convolution fusion | flops 201523200 | bytes 6756352 | tf_op jit(solution)/shard_map/dot_general | solution.py:122
  18.2 2.0 %convolution_bitcast_fusion.1 = f32[1,32,512]{2,1,0:T(8,128)S(1)} fusion(bf16[512,6144]{1,0:T(8,128)(2,1)S(1)} %get-tuple-element.4, bf16[32,6144]{1,0:T(8,128)(2,1)S(1)} %copy-done.2, pred[6144]{0:T(1024)(128)(4,1)S(1)} %iota_compare_fusion), kind=kOutput, calls=%fused_computation.13 | convolution fusion | flops 201523200 | bytes 6756352 | tf_op jit(solution)/shard_map/dot_general | solution.py:119
  20.2 0.0 copy-done
  20.2 0.0 copy-done.1
  20.2 4.1 %collective-permute-start = (f32[2,32,512]{2,1,0:T(8,128)S(1)}, f32[2,32,512]{2,1,0:T(8,128)S(1)}, u32[]{:S(2)}, u32[]{:S(2)}) collective-permute-start(f32[2,32,512]{2,1,0:T(8,128)S(1)} %pad_maximum_fusion.2), channel_id=1, source_target_pairs={{0,16},{4,20},{8,24},{12,28},{16,0},{20,4},{24,8},{28,12},{1,17},{... | collective-permute-start | bytes 393224 | tf_op jit(solution)/shard_map/ppermute | solution.py:75
  24.3 6.3 %collective-permute-done = f32[2,32,512]{2,1,0:T(8,128)S(1)} collective-permute-done((f32[2,32,512]{2,1,0:T(8,128)S(1)}, f32[2,32,512]{2,1,0:T(8,128)S(1)}, u32[]{:S(2)}, u32[]{:S(2)}) %collective-permute-start) | collective-permute-done | bytes 131104 | tf_op jit(solution)/shard_map/ppermute | solution.py:75
  30.6 0.8 %collective-permute-start.1 = (f32[2,32,512]{2,1,0:T(8,128)S(1)}, f32[2,32,512]{2,1,0:T(8,128)S(1)}, u32[]{:S(2)}, u32[]{:S(2)}) collective-permute-start(f32[2,32,512]{2,1,0:T(8,128)S(1)} %fusion.28), channel_id=1, source_target_pairs={{0,8},{4,12},{8,0},{12,4},{16,24},{20,28},{24,16},{28,20},{1,9},{5... | collective-permute-start | bytes 393224 | tf_op jit(solution)/shard_map/ppermute | solution.py:75
  31.4 4.2 %collective-permute-done.1 = f32[2,32,512]{2,1,0:T(8,128)S(1)} collective-permute-done((f32[2,32,512]{2,1,0:T(8,128)S(1)}, f32[2,32,512]{2,1,0:T(8,128)S(1)}, u32[]{:S(2)}, u32[]{:S(2)}) %collective-permute-start.1) | collective-permute-done | bytes 131104 | tf_op jit(solution)/shard_map/ppermute | solution.py:75
  35.7 1.6 %collective-permute-start.2 = (f32[2,32,512]{2,1,0:T(8,128)S(1)}, f32[2,32,512]{2,1,0:T(8,128)S(1)}, u32[]{:S(2)}, u32[]{:S(2)}) collective-permute-start(f32[2,32,512]{2,1,0:T(8,128)S(1)} %fusion.37), channel_id=1, source_target_pairs={{0,4},{4,0},{8,12},{12,8},{16,20},{20,16},{24,28},{28,24},{1,5},{5... | collective-permute-start | bytes 393224 | tf_op jit(solution)/shard_map/ppermute | solution.py:75
  37.3 0.0 copy-done.3
  37.3 3.4 %collective-permute-done.2 = f32[2,32,512]{2,1,0:T(8,128)S(1)} collective-permute-done((f32[2,32,512]{2,1,0:T(8,128)S(1)}, f32[2,32,512]{2,1,0:T(8,128)S(1)}, u32[]{:S(2)}, u32[]{:S(2)}) %collective-permute-start.2) | collective-permute-done | bytes 131104 | tf_op jit(solution)/shard_map/ppermute | solution.py:75
  40.8 0.1 multiply_convert_fusion.3
  40.9 0.0 slice-start
  40.9 0.0 slice-start.1
  40.9 4.0 %fusion.6 = f32[128,6144]{1,0:T(8,128)S(1)} fusion(bf16[512,6144]{1,0:T(8,128)(2,1)} %copy-done.1, bf16[32,512]{1,0:T(8,128)(2,1)S(1)} %get-tuple-element.45, bf16[32,512]{1,0:T(8,128)(2,1)S(1)} %get-tuple-element.44, bf16[32,512]{1,0:T(8,128)(2,1)S(1)} %get-tuple-element.46, bf16[32,512]{1,0:T(8,128)(2,1)S(1)} %get-tuple-element.29), kind=kOutput, calls=%fused_computation.34 | convolution fusion | flops 805830656 | bytes 9568256 | tf_op jit(solution)/shard_map/dot_general | solution.py:129
  44.9 0.0 slice-done
  44.9 0.6 %slice-done.1 = s8[2097152]{0:T(1024)(128)(4,1)S(1)} async-done(((s8[6291456]{0:T(1024)(128)(4,1)}), s8[2097152]{0:T(1024)(128)(4,1)S(1)}, s32[]{:S(2)}) %slice-start.1) | async-done | bytes 2097176
  45.6 1.0 %convolution_add_fusion = f32[128,6144]{1,0:T(8,128)S(1)} fusion(f32[128,6144]{1,0:T(8,128)S(1)} %fusion.6, bf16[512,6144]{1,0:T(8,128)(2,1)S(1)} %bitcast.75, bf16[32,512]{1,0:T(8,128)(2,1)S(1)} %get-tuple-element.28, bf16[32,512]{1,0:T(8,128)(2,1)S(1)} %get-tuple-element.27, bf16[32,512]{1,0:T(8,128)(2,1)S(1)} %get-tuple-element.11, ...), kind=kOutput, calls=%fused_computation.8 | convolution fusion | flops 806617088 | bytes 12713984 | tf_op jit(solution)/shard_map/dot_general | solution.py:130
  46.6 0.4 fusion.2
  47.0 0.1 pad_maximum_fusion
  47.1 0.1 slice_bitcast_fusion.5
  47.2 0.1 pad_maximum_fusion.1
  47.3 0.1 select_bitcast_fusion
  47.3 0.1 collective-permute-start.3
  47.5 1.8 %collective-permute-done.3 = f32[2,35,1536]{2,1,0:T(8,128)S(1)} collective-permute-done((f32[2,35,1536]{2,1,0:T(8,128)S(1)}, f32[2,35,1536]{2,1,0:T(8,128)S(1)}, u32[]{:S(2)}, u32[]{:S(2)}) %collective-permute-start.3) | collective-permute-done | bytes 430112 | tf_op jit(solution)/shard_map/ppermute | solution.py:93
  49.3 0.1 fusion.5
  49.4 1.6 %collective-permute-start.4 = (bf16[1,35,1536]{2,1,0:T(8,128)(2,1)S(1)}, bf16[1,35,1536]{2,1,0:T(8,128)(2,1)S(1)}, u32[]{:S(2)}, u32[]{:S(2)}) collective-permute-start(bf16[1,35,1536]{2,1,0:T(8,128)(2,1)S(1)} %fusion.21), channel_id=1, source_target_pairs={{0,2},{1,3},{2,0},{3,1},{4,6},{5,7},{6,4},{7,5},{8,10},{9,11},{10,... | collective-permute-start | bytes 322568 | tf_op jit(solution)/shard_map/ppermute | solution.py:91
  51.0 3.8 %collective-permute-done.4 = bf16[1,35,1536]{2,1,0:T(8,128)(2,1)S(1)} collective-permute-done((bf16[1,35,1536]{2,1,0:T(8,128)(2,1)S(1)}, bf16[1,35,1536]{2,1,0:T(8,128)(2,1)S(1)}, u32[]{:S(2)}, u32[]{:S(2)}) %collective-permute-start.4) | collective-permute-done | bytes 107552 | tf_op jit(solution)/shard_map/ppermute | solution.py:91
  54.9 0.7 %slice_bitcast_fusion.6 = f32[32,1536]{1,0:T(8,128)} fusion(f32[1,35,1536]{2,1,0:T(8,128)S(1)} %bitcast_add_fusion.1), kind=kLoop, calls=%fused_computation.32 | loop fusion | bytes 393216 | tf_op jit(solution)/shard_map/slice | solution.py:141
  55.6 0.6 %slice_bitcast_fusion.9 = f32[3,1536]{1,0:T(4,128)} fusion(f32[1,35,1536]{2,1,0:T(8,128)S(1)} %bitcast_add_fusion.1), kind=kLoop, calls=%fused_computation.61 | loop fusion | bytes 36864 | tf_op jit(solution)/shard_map/slice | solution.py:141
  (11 shorter events, 0.2 us)
Async XLA Ops:
  2.5 13.8 %copy-start.2 = (bf16[32,6144]{1,0:T(8,128)(2,1)S(1)}, bf16[32,6144]{1,0:T(8,128)(2,1)}, u32[]{:S(2)}) copy-start(bf16[32,6144]{1,0:T(8,128)(2,1)} %param.6) | copy-start | bytes 1179652
  15.5 4.7 %copy-start = (bf16[512,6144]{1,0:T(8,128)(2,1)}, bf16[512,6144]{1,0:T(8,128)(2,1)S(1)}, u32[]{:S(2)}) copy-start(bf16[512,6144]{1,0:T(8,128)(2,1)S(1)} %get-tuple-element.5) | copy-start | bytes 18874372
  15.5 4.7 %copy-start.1 = (bf16[512,6144]{1,0:T(8,128)(2,1)}, bf16[512,6144]{1,0:T(8,128)(2,1)S(1)}, u32[]{:S(2)}) copy-start(bf16[512,6144]{1,0:T(8,128)(2,1)S(1)} %get-tuple-element.4) | copy-start | bytes 18874372
  16.2 21.1 %copy-start.3 = (f32[32]{0:T(128)S(1)}, f32[32]{0:T(128)}, u32[]{:S(2)}) copy-start(f32[32]{0:T(128)} %param.9) | copy-start | bytes 388
  20.2 10.4 %collective-permute-start = (f32[2,32,512]{2,1,0:T(8,128)S(1)}, f32[2,32,512]{2,1,0:T(8,128)S(1)}, u32[]{:S(2)}, u32[]{:S(2)}) collective-permute-start(f32[2,32,512]{2,1,0:T(8,128)S(1)} %pad_maximum_fusion.2), channel_id=1, source_target_pairs={{0,16},{4,20},{8,24},{12,28},{16,0},{20,4},{24,8},{28,12},{1,17},{... | collective-permute-start | bytes 393224 | tf_op jit(solution)/shard_map/ppermute | solution.py:75
  30.6 5.0 %collective-permute-start.1 = (f32[2,32,512]{2,1,0:T(8,128)S(1)}, f32[2,32,512]{2,1,0:T(8,128)S(1)}, u32[]{:S(2)}, u32[]{:S(2)}) collective-permute-start(f32[2,32,512]{2,1,0:T(8,128)S(1)} %fusion.28), channel_id=1, source_target_pairs={{0,8},{4,12},{8,0},{12,4},{16,24},{20,28},{24,16},{28,20},{1,9},{5... | collective-permute-start | bytes 393224 | tf_op jit(solution)/shard_map/ppermute | solution.py:75
  35.7 5.0 %collective-permute-start.2 = (f32[2,32,512]{2,1,0:T(8,128)S(1)}, f32[2,32,512]{2,1,0:T(8,128)S(1)}, u32[]{:S(2)}, u32[]{:S(2)}) collective-permute-start(f32[2,32,512]{2,1,0:T(8,128)S(1)} %fusion.37), channel_id=1, source_target_pairs={{0,4},{4,0},{8,12},{12,8},{16,20},{20,16},{24,28},{28,24},{1,5},{5... | collective-permute-start | bytes 393224 | tf_op jit(solution)/shard_map/ppermute | solution.py:75
  40.9 4.1 %slice-start = ((s8[6291456]{0:T(1024)(128)(4,1)}), s8[4194304]{0:T(1024)(128)(4,1)S(1)}, s32[]{:S(2)}) async-start(s8[6291456]{0:T(1024)(128)(4,1)} %bitcast.74), calls=%async_computation | async-start | bytes 8388608
  40.9 4.6 %slice-start.1 = ((s8[6291456]{0:T(1024)(128)(4,1)}), s8[2097152]{0:T(1024)(128)(4,1)S(1)}, s32[]{:S(2)}) async-start(s8[6291456]{0:T(1024)(128)(4,1)} %bitcast.74), calls=%async_computation.1 | async-start | bytes 4194304
  47.3 1.9 %collective-permute-start.3 = (f32[2,35,1536]{2,1,0:T(8,128)S(1)}, f32[2,35,1536]{2,1,0:T(8,128)S(1)}, u32[]{:S(2)}, u32[]{:S(2)}) collective-permute-start(f32[2,35,1536]{2,1,0:T(8,128)S(1)} %select_bitcast_fusion), channel_id=1, source_target_pairs={{0,1},{1,0},{2,3},{3,2},{4,5},{5,4},{6,7},{7,6},{8,9},{9,8},{10,11... | collective-permute-start | bytes 1290248 | tf_op jit(solution)/shard_map/ppermute | solution.py:93
  49.4 5.4 %collective-permute-start.4 = (bf16[1,35,1536]{2,1,0:T(8,128)(2,1)S(1)}, bf16[1,35,1536]{2,1,0:T(8,128)(2,1)S(1)}, u32[]{:S(2)}, u32[]{:S(2)}) collective-permute-start(bf16[1,35,1536]{2,1,0:T(8,128)(2,1)S(1)} %fusion.21), channel_id=1, source_target_pairs={{0,2},{1,3},{2,0},{3,1},{4,6},{5,7},{6,4},{7,5},{8,10},{9,11},{10,... | collective-permute-start | bytes 322568 | tf_op jit(solution)/shard_map/ppermute | solution.py:91

commit v10 on v8

--- a/solution.py
+++ b/solution.py
@@ -3,6 +3,7 @@
 import jax
 import jax.numpy as jnp
 from jax import lax
+from jax.experimental import pallas as pl
 from jax.sharding import PartitionSpec as P
 
 two_pi = 6.283185307179586
@@ -28,6 +29,38 @@
     cos_out = 1.0 - s * s
     sin_out = s * c
     return cos_out, sin_out
+
+
+def field_kernel(cs_ref, ss_ref, ct_ref, st_ref, q_ref, live_ref, out_ref):
+    field = jnp.dot(cs_ref[...], ct_ref[...], preferred_element_type=jnp.float32)
+    field = field + jnp.dot(ss_ref[...], st_ref[...], preferred_element_type=jnp.float32)
+    channels = q_ref.shape[0]
+    live = live_ref[...] > 0.0
+    out_ref[0, :channels, :] = jnp.where(live, field[:channels], 0.0)
+    q = q_ref[...].astype(jnp.float32)
+    for d in range(3):
+        rows = field[channels * (1 + d) : channels * (2 + d)]
+        out_ref[0, channels + d : channels + d + 1, :] = jnp.sum(q * rows, 0, keepdims=True)
+
+
+def field_blocks(cos_side, sin_side, cos_table, sin_table, charge_live, live_f, n_blocks):
+    n_side, n_k = cos_side.shape
+    channels, n_at = charge_live.shape
+    rows = n_at // n_blocks
+    return pl.pallas_call(
+        field_kernel,
+        grid=(n_blocks,),
+        in_specs=[
+            pl.BlockSpec((n_side, n_k), lambda b: (0, 0)),
+            pl.BlockSpec((n_side, n_k), lambda b: (0, 0)),
+            pl.BlockSpec((n_k, rows), lambda b: (0, b)),
+            pl.BlockSpec((n_k, rows), lambda b: (0, b)),
+            pl.BlockSpec((channels, rows), lambda b: (0, b)),
+            pl.BlockSpec((1, rows), lambda b: (0, b)),
+        ],
+        out_specs=pl.BlockSpec((1, channels + 3, rows), lambda b: (b, 0, 0)),
+        out_shape=jax.ShapeDtypeStruct((n_blocks, channels + 3, rows), jnp.float32),
+    )(cos_side, sin_side, cos_table, sin_table, charge_live, live_f)
 
 
 def reciprocal_filter_weight(s_cos, s_sin, cartesian_mode_vector, gaussian_spread, atoms_total):
@@ -126,17 +159,10 @@
         cos_side, sin_side = reciprocal_filter_weight(
             s_both[0], s_both[1], cartesian_mode_vector, gaussian_spread, atoms_total
         )
-        field = jnp.dot(cos_side, cos_table, preferred_element_type=jnp.float32)
-        field = field + jnp.dot(sin_side, sin_table, preferred_element_type=jnp.float32)
-        charge_f = charge_live.astype(jnp.float32)
-        head = jnp.where(live[None, :], field[:channels], 0.0)
-        force_rows = [
-            jnp.sum(charge_f * field[channels * (1 + d) : channels * (2 + d)], 0, keepdims=True)
-            for d in range(3)
-        ]
-        partial = jnp.concatenate([head] + force_rows, 0)
-        rows = n_local // n_ka
-        blocks = jnp.stack([partial[:, b * rows : (b + 1) * rows] for b in range(n_ka)], 0)
+        blocks = field_blocks(
+            cos_side, sin_side, cos_table, sin_table, charge_live,
+            live.astype(jnp.float32)[None, :], n_ka,
+        )
         own = halving_scatter(blocks, "ka", n_ka)
         return (own[:channels], own[channels:])
 

time: 54.8 us -> 59.8 us (1.091)
  Pallas kernels: 0 us -> 7.53 us
  matrix products: 8.92 us -> 3.99 us
  other arithmetic: 14.8 us -> 18.5 us
  local copies, waits for them, and re-layouts: 3.14 us -> 2.45 us
  waiting for transfers between devices: 16.6 us -> 16 us
    pallas_call x0 -> x1, Pallas kernels: none -> 7.53 us  [field_blocks(): pl.pallas_call(field_kernel, grid=(n_blocks,), in_specs=[pl.BlockSpec((n_...]
    dot_general x2 -> x0, matrix products: 5 us -> none  [the longest x1 4 us: local(): field = jnp.dot(cos_side, cos_table, preferred_element_type=jnp.float32)]
    concatenate x1 -> x2, other arithmetic: 0.11 us -> 1.34 us  [the longest x1 0.68 us: reciprocal_filter_weight(): jnp.concatenate([partial_second_term, scale * cartesian_mode_vector[0] *...]
    reshape x1, other arithmetic: 0.07 us -> 1.26 us  [halving_scatter(): pairs = held.reshape(m // 2, 2, *held.shape[1:])]
    select_n x1, other arithmetic: 0.06 us -> 1.23 us  [halving_scatter(): send = jnp.where(bit == 0, pairs[:, 1], pairs[:, 0])]
    ppermute x3, waiting for transfers between devices: 11.1 us -> 10.5 us  [butterfly_sum(): x = x + lax.ppermute(x, axis, [(i, i ^ step) for i in range(n)])]
    convert_element_type x0 -> x1, other arithmetic: none -> 0.63 us  [local(): live.astype(jnp.float32)[None, :]]
    unnamed x12 -> x10, local copies, waits for them, and re-layouts: 0.66 us -> 0.03 us
  transfers between devices with their start and end apart: 5 -> 5, of which waited for: 5 -> 5; matrix products, arithmetic and copies ran while one was open for 0% -> 1% of each run, Pallas kernels for 0% -> 0%
where the time goes in v10:
time: 59.8 us; the launch traced here: 59.6 us
  other arithmetic  18.5 us (31%)
  waiting for transfers between devices  16 us (27%)
  starting transfers between devices  9.61 us (16%)
  Pallas kernels  7.53 us (13%)
  matrix products  3.99 us (7%)
  local copies, waits for them, and re-layouts  2.45 us (4%)
  between operations  1.49 us (2%)
    convert_element_type x1, other arithmetic, local(): sin_table = sin_f.astype(jnp.bfloat16)  13 us
    ppermute x3, waiting for transfers between devices, butterfly_sum(): x = x + lax.ppermute(x, axis, [(i, i ^ step) for i in range(n)])  10.5 us
    ppermute x3, starting transfers between devices, butterfly_sum(): x = x + lax.ppermute(x, axis, [(i, i ^ step) for i in range(n)])  7.77 us
    pallas_call x1, Pallas kernels, field_blocks(): pl.pallas_call(field_kernel, grid=(n_blocks,), in_specs=[pl.BlockSpec((n_...  7.53 us
    ppermute x1, waiting for transfers between devices, halving_scatter(): lax.ppermute(send.astype(jnp.bfloat16), axis, pairs_list)  3.65 us
    dot_general x1, matrix products, local(): lax.dot_general(charge_live, sin_table, tensor_product, preferred_element...  2 us
    dot_general x1, matrix products, local(): lax.dot_general(charge_live, cos_table, tensor_product, preferred_element...  1.99 us
    ppermute x1, waiting for transfers between devices, halving_scatter(): recv = lax.ppermute(send, axis, pairs_list)  1.82 us
  transfers between devices with their start and end apart: 5, of which 5 were waited for; matrix products, arithmetic and copies ran while one was open for 1% of the time, Pallas kernels for 0%

profile of v10, /device:TPU:0, one launch (start us, length us, event | category | flops | bytes accessed | tf_op | source)
XLA Modules:
  0.0 59.6 jit_solution(12988597142304660335)
XLA Ops:
  0.6 0.7 %convert_element_type.38 = f32[3,512]{1,0:T(4,128)S(1)} convert(s32[3,512]{1,0:T(4,128)} %param.7) | non-fusion elementwise | flops 1536 | bytes 12288 | tf_op jit(solution)/shard_map/convert_element_type | solution.py:141
  1.4 1.1 %fusion.10 = (f32[1,6144]{1,0:T(1,128)S(1)}, f32[1,6144]{1,0:T(1,128)S(1)}, f32[1,6144]{1,0:T(1,128)S(1)}) fusion(f32[3,6144]{1,0:T(4,128)} %param.5), kind=kLoop, calls=%fused_computation.48 | loop fusion | bytes 147456 | tf_op jit(solution)/shard_map/slice | solution.py:143
  2.5 0.0 copy-start.3
  2.5 13.0 %multiply_convert_fusion = (bf16[512,6144]{1,0:T(8,128)(2,1)S(1)}, bf16[512,6144]{1,0:T(8,128)(2,1)S(1)}) fusion(f32[6144]{0:T(1024)S(1)} %bitcast.67, f32[512]{0:T(512)S(1)} %bitcast.77, f32[6144]{0:T(1024)S(1)} %bitcast.68, f32[512]{0:T(512)S(1)} %bitcast.78, f32[6144]{0:T(1024)S(1)} %bitcast.66, f32[512]{0:T(512)S(1)} %bitcast.79), kind=kLoop, calls=%fused_computation | loop fusion | flops 97517568 | bytes 12662784 | tf_op jit(solution)/shard_map/convert_element_type | solution.py:149
  15.5 0.0 copy-start
  15.5 0.0 copy-start.1
  16.2 0.0 copy-done.3
  16.3 0.0 copy-start.2
  16.3 0.0 copy-start.4
  16.3 2.0 %convolution_bitcast_fusion.1 = f32[1,32,512]{2,1,0:T(8,128)S(1)} fusion(bf16[32,6144]{1,0:T(8,128)(2,1)S(1)} %broadcast_select_fusion.q_ref, bf16[512,6144]{1,0:T(8,128)(2,1)S(1)} %get-tuple-element.4.ct_ref), kind=kOutput, calls=%fused_computation.9 | convolution fusion | flops 201326592 | bytes 6750208 | tf_op jit(solution)/shard_map/dot_general | solution.py:152
  18.3 2.0 %convolution_bitcast_fusion = f32[1,32,512]{2,1,0:T(8,128)S(1)} fusion(bf16[32,6144]{1,0:T(8,128)(2,1)S(1)} %broadcast_select_fusion.q_ref, bf16[512,6144]{1,0:T(8,128)(2,1)S(1)} %get-tuple-element.5.st_ref), kind=kOutput, calls=%fused_computation.8 | convolution fusion | flops 201326592 | bytes 6750208 | tf_op jit(solution)/shard_map/dot_general | solution.py:155
  20.3 0.0 copy-done
  20.3 0.0 copy-done.1
  20.3 0.0 copy-done.2
  20.4 3.0 %collective-permute-start = (f32[2,32,512]{2,1,0:T(8,128)S(1)}, f32[2,32,512]{2,1,0:T(8,128)S(1)}, u32[]{:S(2)}, u32[]{:S(2)}) collective-permute-start(f32[2,32,512]{2,1,0:T(8,128)S(1)} %pad_maximum_fusion), channel_id=1, source_target_pairs={{0,4},{4,0},{8,12},{12,8},{16,20},{20,16},{24,28},{28,24},{1,5},{5... | collective-permute-start | bytes 393224 | tf_op jit(solution)/shard_map/ppermute | solution.py:108
  23.4 3.5 %collective-permute-done = f32[2,32,512]{2,1,0:T(8,128)S(1)} collective-permute-done((f32[2,32,512]{2,1,0:T(8,128)S(1)}, f32[2,32,512]{2,1,0:T(8,128)S(1)}, u32[]{:S(2)}, u32[]{:S(2)}) %collective-permute-start) | collective-permute-done | bytes 131104 | tf_op jit(solution)/shard_map/ppermute | solution.py:108
  26.9 1.9 %collective-permute-start.1 = (f32[2,32,512]{2,1,0:T(8,128)S(1)}, f32[2,32,512]{2,1,0:T(8,128)S(1)}, u32[]{:S(2)}, u32[]{:S(2)}) collective-permute-start(f32[2,32,512]{2,1,0:T(8,128)S(1)} %fusion.6), channel_id=1, source_target_pairs={{0,8},{4,12},{8,0},{12,4},{16,24},{20,28},{24,16},{28,20},{1,9},{5... | collective-permute-start | bytes 393224 | tf_op jit(solution)/shard_map/ppermute | solution.py:108
  28.8 0.6 %compare_convert_fusion.live_ref = f32[1,6144]{1,0:T(1,128)} fusion(s32[]{:T(128)} %bitcast.63), kind=kLoop, calls=%fused_computation.23 | loop fusion | flops 12288 | bytes 24580 | tf_op jit(solution)/shard_map/convert_element_type | solution.py:164
  29.4 2.5 %collective-permute-done.1 = f32[2,32,512]{2,1,0:T(8,128)S(1)} collective-permute-done((f32[2,32,512]{2,1,0:T(8,128)S(1)}, f32[2,32,512]{2,1,0:T(8,128)S(1)}, u32[]{:S(2)}, u32[]{:S(2)}) %collective-permute-start.1) | collective-permute-done | bytes 131104 | tf_op jit(solution)/shard_map/ppermute | solution.py:108
  32.0 2.9 %collective-permute-start.2 = (f32[2,32,512]{2,1,0:T(8,128)S(1)}, f32[2,32,512]{2,1,0:T(8,128)S(1)}, u32[]{:S(2)}, u32[]{:S(2)}) collective-permute-start(f32[2,32,512]{2,1,0:T(8,128)S(1)} %fusion.15), channel_id=1, source_target_pairs={{0,16},{4,20},{8,24},{12,28},{16,0},{20,4},{24,8},{28,12},{1,17},{... | collective-permute-start | bytes 393224 | tf_op jit(solution)/shard_map/ppermute | solution.py:108
  34.9 0.0 copy-done.4
  34.9 4.5 %collective-permute-done.2 = f32[2,32,512]{2,1,0:T(8,128)S(1)} collective-permute-done((f32[2,32,512]{2,1,0:T(8,128)S(1)}, f32[2,32,512]{2,1,0:T(8,128)S(1)}, u32[]{:S(2)}, u32[]{:S(2)}) %collective-permute-start.2) | collective-permute-done | bytes 131104 | tf_op jit(solution)/shard_map/ppermute | solution.py:108
  39.3 0.1 multiply_convert_fusion.3
  39.5 0.7 %pad_maximum_fusion.2.ss_ref = bf16[128,512]{1,0:T(8,128)(2,1)} fusion(bf16[32,512]{1,0:T(8,128)(2,1)S(1)} %get-tuple-element.20, bf16[32,512]{1,0:T(8,128)(2,1)S(1)} %get-tuple-element.19, bf16[32,512]{1,0:T(8,128)(2,1)S(1)} %get-tuple-element.8, bf16[32,512]{1,0:T(8,128)(2,1)S(1)} %get-tuple-element.12), kind=kLoop, calls=%fused_computation.21 | loop fusion | flops 524288 | bytes 262144 | tf_op jit(solution)/shard_map/concatenate | solution.py:93
  40.2 0.7 %pad_maximum_fusion.1.cs_ref = bf16[128,512]{1,0:T(8,128)(2,1)} fusion(bf16[32,512]{1,0:T(8,128)(2,1)S(1)} %get-tuple-element.37, bf16[32,512]{1,0:T(8,128)(2,1)S(1)} %get-tuple-element.36, bf16[32,512]{1,0:T(8,128)(2,1)S(1)} %get-tuple-element.38, bf16[32,512]{1,0:T(8,128)(2,1)S(1)} %get-tuple-element.21), kind=kLoop, calls=%fused_computation.20 | loop fusion | flops 524288 | bytes 262144 | tf_op jit(solution)/shard_map/concatenate | solution.py:84
  40.8 7.5 %shard_map.68 = f32[4,35,1536]{2,1,0:T(8,128)} custom-call(bf16[128,512]{1,0:T(8,128)(2,1)} %pad_maximum_fusion.1.cs_ref, bf16[128,512]{1,0:T(8,128)(2,1)} %pad_maximum_fusion.2.ss_ref, bf16[512,6144]{1,0:T(8,128)(2,1)} %copy-done.1, bf16[512,6144]{1,0:T(8,128)(2,1)} %copy-done, bf16[32,6144]{1,0:T(8,128)(2,1)} %copy-done.2, ...), custom_call_target="tpu_custom_call" | custom-call | tf_op jit(solution)/shard_map/pallas_call | solution.py:50
  48.3 1.2 %select_bitcast_fusion = f32[2,35,1536]{2,1,0:T(8,128)S(1)} fusion(f32[2,2,35,1536]{3,2,1,0:T(8,128)} %bitcast.64, pred[]{:T(512)S(6)} %eq.12), kind=kLoop, calls=%fused_computation.14 | loop fusion | flops 107520 | bytes 1290241 | tf_op jit(solution)/shard_map/jit(_where)/select_n | solution.py:121
  49.6 0.1 collective-permute-start.3
  49.7 1.8 %collective-permute-done.3 = f32[2,35,1536]{2,1,0:T(8,128)S(1)} collective-permute-done((f32[2,35,1536]{2,1,0:T(8,128)S(1)}, f32[2,35,1536]{2,1,0:T(8,128)S(1)}, u32[]{:S(2)}, u32[]{:S(2)}) %collective-permute-start.3) | collective-permute-done | bytes 430112 | tf_op jit(solution)/shard_map/ppermute | solution.py:126
  51.5 1.3 %fusion.2 = f32[1,2,35,1536]{3,2,1,0:T(8,128)S(1)} fusion(f32[2,35,1536]{2,1,0:T(8,128)S(1)} %collective-permute-done.3, f32[2,2,35,1536]{3,2,1,0:T(8,128)} %bitcast.65, pred[]{:T(512)S(6)} %eq.12), kind=kLoop, calls=%fused_computation.13 | loop fusion | flops 215040 | bytes 1720321 | tf_op jit(solution)/shard_map/reshape | solution.py:118
  52.8 1.8 %collective-permute-start.4 = (bf16[1,35,1536]{2,1,0:T(8,128)(2,1)S(1)}, bf16[1,35,1536]{2,1,0:T(8,128)(2,1)S(1)}, u32[]{:S(2)}, u32[]{:S(2)}) collective-permute-start(bf16[1,35,1536]{2,1,0:T(8,128)(2,1)S(1)} %fusion.3), channel_id=1, source_target_pairs={{0,2},{1,3},{2,0},{3,1},{4,6},{5,7},{6,4},{7,5},{8,10},{9,11},{10,... | collective-permute-start | bytes 322568 | tf_op jit(solution)/shard_map/ppermute | solution.py:124
  54.6 3.7 %collective-permute-done.4 = bf16[1,35,1536]{2,1,0:T(8,128)(2,1)S(1)} collective-permute-done((bf16[1,35,1536]{2,1,0:T(8,128)(2,1)S(1)}, bf16[1,35,1536]{2,1,0:T(8,128)(2,1)S(1)}, u32[]{:S(2)}, u32[]{:S(2)}) %collective-permute-start.4) | collective-permute-done | bytes 107552 | tf_op jit(solution)/shard_map/ppermute | solution.py:124
  58.3 0.7 %slice_bitcast_fusion.2 = f32[32,1536]{1,0:T(8,128)} fusion(f32[1,35,1536]{2,1,0:T(8,128)S(1)} %bitcast_add_fusion.1), kind=kLoop, calls=%fused_computation.18 | loop fusion | bytes 393216 | tf_op jit(solution)/shard_map/slice | solution.py:167
  59.0 0.6 %slice_bitcast_fusion.5 = f32[3,1536]{1,0:T(4,128)} fusion(f32[1,35,1536]{2,1,0:T(8,128)S(1)} %bitcast_add_fusion.1), kind=kLoop, calls=%fused_computation.35 | loop fusion | bytes 36864 | tf_op jit(solution)/shard_map/slice | solution.py:167
  (11 shorter events, 0.3 us)
Async XLA Ops:
  2.5 13.8 %copy-start.3 = (bf16[32,6144]{1,0:T(8,128)(2,1)S(1)}, bf16[32,6144]{1,0:T(8,128)(2,1)}, u32[]{:S(2)}) copy-start(bf16[32,6144]{1,0:T(8,128)(2,1)} %param.6) | copy-start | bytes 1179652
  15.5 4.8 %copy-start = (bf16[512,6144]{1,0:T(8,128)(2,1)}, bf16[512,6144]{1,0:T(8,128)(2,1)S(1)}, u32[]{:S(2)}) copy-start(bf16[512,6144]{1,0:T(8,128)(2,1)S(1)} %get-tuple-element.5.st_ref) | copy-start | bytes 18874372
  15.5 4.8 %copy-start.1 = (bf16[512,6144]{1,0:T(8,128)(2,1)}, bf16[512,6144]{1,0:T(8,128)(2,1)S(1)}, u32[]{:S(2)}) copy-start(bf16[512,6144]{1,0:T(8,128)(2,1)S(1)} %get-tuple-element.4.ct_ref) | copy-start | bytes 18874372
  16.3 4.0 %copy-start.2 = (bf16[32,6144]{1,0:T(8,128)(2,1)}, bf16[32,6144]{1,0:T(8,128)(2,1)S(1)}, u32[]{:S(2)}) copy-start(bf16[32,6144]{1,0:T(8,128)(2,1)S(1)} %broadcast_select_fusion.q_ref) | copy-start | bytes 1179652
  16.3 18.6 %copy-start.4 = (f32[32]{0:T(128)S(1)}, f32[32]{0:T(128)}, u32[]{:S(2)}) copy-start(f32[32]{0:T(128)} %param.9) | copy-start | bytes 388
  20.4 6.5 %collective-permute-start = (f32[2,32,512]{2,1,0:T(8,128)S(1)}, f32[2,32,512]{2,1,0:T(8,128)S(1)}, u32[]{:S(2)}, u32[]{:S(2)}) collective-permute-start(f32[2,32,512]{2,1,0:T(8,128)S(1)} %pad_maximum_fusion), channel_id=1, source_target_pairs={{0,4},{4,0},{8,12},{12,8},{16,20},{20,16},{24,28},{28,24},{1,5},{5... | collective-permute-start | bytes 393224 | tf_op jit(solution)/shard_map/ppermute | solution.py:108
  26.9 5.0 %collective-permute-start.1 = (f32[2,32,512]{2,1,0:T(8,128)S(1)}, f32[2,32,512]{2,1,0:T(8,128)S(1)}, u32[]{:S(2)}, u32[]{:S(2)}) collective-permute-start(f32[2,32,512]{2,1,0:T(8,128)S(1)} %fusion.6), channel_id=1, source_target_pairs={{0,8},{4,12},{8,0},{12,4},{16,24},{20,28},{24,16},{28,20},{1,9},{5... | collective-permute-start | bytes 393224 | tf_op jit(solution)/shard_map/ppermute | solution.py:108
  32.0 7.3 %collective-permute-start.2 = (f32[2,32,512]{2,1,0:T(8,128)S(1)}, f32[2,32,512]{2,1,0:T(8,128)S(1)}, u32[]{:S(2)}, u32[]{:S(2)}) collective-permute-start(f32[2,32,512]{2,1,0:T(8,128)S(1)} %fusion.15), channel_id=1, source_target_pairs={{0,16},{4,20},{8,24},{12,28},{16,0},{20,4},{24,8},{28,12},{1,17},{... | collective-permute-start | bytes 393224 | tf_op jit(solution)/shard_map/ppermute | solution.py:108
  49.6 1.9 %collective-permute-start.3 = (f32[2,35,1536]{2,1,0:T(8,128)S(1)}, f32[2,35,1536]{2,1,0:T(8,128)S(1)}, u32[]{:S(2)}, u32[]{:S(2)}) collective-permute-start(f32[2,35,1536]{2,1,0:T(8,128)S(1)} %select_bitcast_fusion), channel_id=1, source_target_pairs={{0,1},{1,0},{2,3},{3,2},{4,5},{5,4},{6,7},{7,6},{8,9},{9,8},{10,11... | collective-permute-start | bytes 1290248 | tf_op jit(solution)/shard_map/ppermute | solution.py:126
  52.8 5.4 %collective-permute-start.4 = (bf16[1,35,1536]{2,1,0:T(8,128)(2,1)S(1)}, bf16[1,35,1536]{2,1,0:T(8,128)(2,1)S(1)}, u32[]{:S(2)}, u32[]{:S(2)}) collective-permute-start(bf16[1,35,1536]{2,1,0:T(8,128)(2,1)S(1)} %fusion.3), channel_id=1, source_target_pairs={{0,2},{1,3},{2,0},{3,1},{4,6},{5,7},{6,4},{7,5},{8,10},{9,11},{10,... | collective-permute-start | bytes 322568 | tf_op jit(solution)/shard_map/ppermute | solution.py:124

commit v11 on v8

--- a/solution.py
+++ b/solution.py
@@ -126,8 +126,10 @@
         cos_side, sin_side = reciprocal_filter_weight(
             s_both[0], s_both[1], cartesian_mode_vector, gaussian_spread, atoms_total
         )
-        field = jnp.dot(cos_side, cos_table, preferred_element_type=jnp.float32)
-        field = field + jnp.dot(sin_side, sin_table, preferred_element_type=jnp.float32)
+        field = lax.dot_general(
+            jnp.stack([cos_side, sin_side], 0), jnp.stack([cos_table, sin_table], 0),
+            (((0, 2), (0, 1)), ((), ())), preferred_element_type=jnp.float32,
+        )
         charge_f = charge_live.astype(jnp.float32)
         head = jnp.where(live[None, :], field[:channels], 0.0)
         force_rows = [

time: 54.8 us -> 55 us (level)
  matrix products: 8.92 us -> 9.74 us
  local copies, waits for them, and re-layouts: 3.14 us -> 2.52 us
    dot_general x2 -> x1, matrix products: 5 us -> 5.82 us  [local(): lax.dot_general(jnp.stack([cos_side, sin_side], 0), jnp.stack([cos_table,...]
    unnamed x12 -> x8, local copies, waits for them, and re-layouts: 0.66 us -> 0.03 us
where the time goes in v11:
time: 55 us; the launch traced here: 54.7 us
  waiting for transfers between devices  16.6 us (30%)
  other arithmetic  14.8 us (27%)
  matrix products  9.74 us (18%)
  starting transfers between devices  9.61 us (17%)
  local copies, waits for them, and re-layouts  2.52 us (5%)
  between operations  1.5 us (3%)
    convert_element_type x1, other arithmetic, local(): sin_table = sin_f.astype(jnp.bfloat16)  13 us
    ppermute x3, waiting for transfers between devices, butterfly_sum(): x = x + lax.ppermute(x, axis, [(i, i ^ step) for i in range(n)])  11.1 us
    ppermute x3, starting transfers between devices, butterfly_sum(): x = x + lax.ppermute(x, axis, [(i, i ^ step) for i in range(n)])  7.77 us
    dot_general x1, matrix products, local(): lax.dot_general(jnp.stack([cos_side, sin_side], 0), jnp.stack([cos_table,...  5.82 us
    ppermute x1, waiting for transfers between devices, halving_scatter(): lax.ppermute(send.astype(jnp.bfloat16), axis, pairs_list)  3.66 us
    dot_general x1, matrix products, local(): lax.dot_general(charge_live, cos_table, tensor_product, preferred_element...  1.97 us
    dot_general x1, matrix products, local(): lax.dot_general(charge_live, sin_table, tensor_product, preferred_element...  1.95 us
    ppermute x1, waiting for transfers between devices, halving_scatter(): recv = lax.ppermute(send, axis, pairs_list)  1.82 us
  transfers between devices with their start and end apart: 5, of which 5 were waited for; matrix products, arithmetic and copies ran while one was open for 0% of the time, Pallas kernels for 0%

profile of v11, /device:TPU:0, one launch (start us, length us, event | category | flops | bytes accessed | tf_op | source)
XLA Modules:
  0.0 54.7 jit_solution(7773492528378917626)
XLA Ops:
  0.6 0.7 %convert_element_type.45 = f32[3,512]{1,0:T(4,128)S(1)} convert(s32[3,512]{1,0:T(4,128)} %param.7) | non-fusion elementwise | flops 1536 | bytes 12288 | tf_op jit(solution)/shard_map/convert_element_type | solution.py:108
  1.4 1.1 %fusion.34 = (f32[1,6144]{1,0:T(1,128)S(1)}, f32[1,6144]{1,0:T(1,128)S(1)}, f32[1,6144]{1,0:T(1,128)S(1)}) fusion(f32[3,6144]{1,0:T(4,128)} %param.5), kind=kLoop, calls=%fused_computation.79 | loop fusion | bytes 147456 | tf_op jit(solution)/shard_map/slice | solution.py:110
  2.5 0.0 copy-start.2
  2.5 13.0 %multiply_convert_fusion = (bf16[512,6144]{1,0:T(8,128)(2,1)S(1)}, bf16[512,6144]{1,0:T(8,128)(2,1)S(1)}) fusion(f32[6144]{0:T(1024)S(1)} %bitcast.74, f32[512]{0:T(512)S(1)} %bitcast.84, f32[6144]{0:T(1024)S(1)} %bitcast.75, f32[512]{0:T(512)S(1)} %bitcast.85, f32[6144]{0:T(1024)S(1)} %bitcast.73, f32[512]{0:T(512)S(1)} %bitcast.86), kind=kLoop, calls=%fused_computation.4 | loop fusion | flops 97517568 | bytes 12662784 | tf_op jit(solution)/shard_map/convert_element_type | solution.py:116
  15.5 0.0 copy-start
  15.5 0.0 copy-start.1
  16.2 0.0 copy-done.2
  16.2 0.0 copy-start.3
  16.2 2.0 %convolution_bitcast_fusion = f32[1,32,512]{2,1,0:T(8,128)S(1)} fusion(bf16[512,6144]{1,0:T(8,128)(2,1)S(1)} %get-tuple-element.5, bf16[32,6144]{1,0:T(8,128)(2,1)S(1)} %copy-done.2, pred[6144]{0:T(1024)(128)(4,1)S(1)} %iota_compare_fusion), kind=kOutput, calls=%fused_computation.16 | convolution fusion | flops 201523200 | bytes 6756352 | tf_op jit(solution)/shard_map/dot_general | solution.py:122
  18.2 2.0 %convolution_bitcast_fusion.1 = f32[1,32,512]{2,1,0:T(8,128)S(1)} fusion(bf16[512,6144]{1,0:T(8,128)(2,1)S(1)} %get-tuple-element.4, bf16[32,6144]{1,0:T(8,128)(2,1)S(1)} %copy-done.2, pred[6144]{0:T(1024)(128)(4,1)S(1)} %iota_compare_fusion), kind=kOutput, calls=%fused_computation.17 | convolution fusion | flops 201523200 | bytes 6756352 | tf_op jit(solution)/shard_map/dot_general | solution.py:119
  20.2 0.0 copy-done
  20.2 0.0 copy-done.1
  20.2 3.0 %collective-permute-start = (f32[2,32,512]{2,1,0:T(8,128)S(1)}, f32[2,32,512]{2,1,0:T(8,128)S(1)}, u32[]{:S(2)}, u32[]{:S(2)}) collective-permute-start(f32[2,32,512]{2,1,0:T(8,128)S(1)} %pad_maximum_fusion.2), channel_id=1, source_target_pairs={{0,4},{4,0},{8,12},{12,8},{16,20},{20,16},{24,28},{28,24},{1,5},{5... | collective-permute-start | bytes 393224 | tf_op jit(solution)/shard_map/ppermute | solution.py:75
  23.2 3.5 %collective-permute-done = f32[2,32,512]{2,1,0:T(8,128)S(1)} collective-permute-done((f32[2,32,512]{2,1,0:T(8,128)S(1)}, f32[2,32,512]{2,1,0:T(8,128)S(1)}, u32[]{:S(2)}, u32[]{:S(2)}) %collective-permute-start) | collective-permute-done | bytes 131104 | tf_op jit(solution)/shard_map/ppermute | solution.py:75
  26.8 1.9 %collective-permute-start.1 = (f32[2,32,512]{2,1,0:T(8,128)S(1)}, f32[2,32,512]{2,1,0:T(8,128)S(1)}, u32[]{:S(2)}, u32[]{:S(2)}) collective-permute-start(f32[2,32,512]{2,1,0:T(8,128)S(1)} %fusion.32), channel_id=1, source_target_pairs={{0,8},{4,12},{8,0},{12,4},{16,24},{20,28},{24,16},{28,20},{1,9},{5... | collective-permute-start | bytes 393224 | tf_op jit(solution)/shard_map/ppermute | solution.py:75
  28.6 3.2 %collective-permute-done.1 = f32[2,32,512]{2,1,0:T(8,128)S(1)} collective-permute-done((f32[2,32,512]{2,1,0:T(8,128)S(1)}, f32[2,32,512]{2,1,0:T(8,128)S(1)}, u32[]{:S(2)}, u32[]{:S(2)}) %collective-permute-start.1) | collective-permute-done | bytes 131104 | tf_op jit(solution)/shard_map/ppermute | solution.py:75
  31.8 2.9 %collective-permute-start.2 = (f32[2,32,512]{2,1,0:T(8,128)S(1)}, f32[2,32,512]{2,1,0:T(8,128)S(1)}, u32[]{:S(2)}, u32[]{:S(2)}) collective-permute-start(f32[2,32,512]{2,1,0:T(8,128)S(1)} %fusion.37), channel_id=1, source_target_pairs={{0,16},{4,20},{8,24},{12,28},{16,0},{20,4},{24,8},{28,12},{1,17},{... | collective-permute-start | bytes 393224 | tf_op jit(solution)/shard_map/ppermute | solution.py:75
  34.7 0.0 copy-done.3
  34.7 4.5 %collective-permute-done.2 = f32[2,32,512]{2,1,0:T(8,128)S(1)} collective-permute-done((f32[2,32,512]{2,1,0:T(8,128)S(1)}, f32[2,32,512]{2,1,0:T(8,128)S(1)}, u32[]{:S(2)}, u32[]{:S(2)}) %collective-permute-start.2) | collective-permute-done | bytes 131104 | tf_op jit(solution)/shard_map/ppermute | solution.py:75
  39.2 0.1 multiply_convert_fusion.6
  39.3 5.8 %fusion.6 = f32[128,6144]{1,0:T(8,128)S(1)} fusion(bf16[1,512,6144]{2,1,0:T(8,128)(2,1)} %bitcast.66, bf16[1,512,6144]{2,1,0:T(8,128)(2,1)} %bitcast.67, bf16[1,32,512]{2,1,0:T(8,128)(2,1)S(1)} %get-tuple-element.32, bf16[1,32,512]{2,1,0:T(8,128)(2,1)S(1)} %get-tuple-element.31, bf16[1,32,512]{2,1,0:T(8,128)(2,1)S(1)} %get-tuple-element.30, ...), kind=kOutput, calls=%fused_computation.12 | convolution fusion | flops 1619001344 | bytes 15990784 | tf_op jit(solution)/shard_map/dot_general | solution.py:129
  45.2 0.5 fusion.9
  45.6 0.1 pad_maximum_fusion
  45.7 0.1 slice_bitcast_fusion.5
  45.8 0.1 pad_maximum_fusion.1
  45.9 0.1 select_bitcast_fusion
  45.9 0.1 collective-permute-start.3
  46.0 1.8 %collective-permute-done.3 = f32[2,35,1536]{2,1,0:T(8,128)S(1)} collective-permute-done((f32[2,35,1536]{2,1,0:T(8,128)S(1)}, f32[2,35,1536]{2,1,0:T(8,128)S(1)}, u32[]{:S(2)}, u32[]{:S(2)}) %collective-permute-start.3) | collective-permute-done | bytes 430112 | tf_op jit(solution)/shard_map/ppermute | solution.py:93
  47.9 0.1 fusion.12
  48.0 1.8 %collective-permute-start.4 = (bf16[1,35,1536]{2,1,0:T(8,128)(2,1)S(1)}, bf16[1,35,1536]{2,1,0:T(8,128)(2,1)S(1)}, u32[]{:S(2)}, u32[]{:S(2)}) collective-permute-start(bf16[1,35,1536]{2,1,0:T(8,128)(2,1)S(1)} %fusion.28), channel_id=1, source_target_pairs={{0,2},{1,3},{2,0},{3,1},{4,6},{5,7},{6,4},{7,5},{8,10},{9,11},{10,... | collective-permute-start | bytes 322568 | tf_op jit(solution)/shard_map/ppermute | solution.py:91
  49.7 3.7 %collective-permute-done.4 = bf16[1,35,1536]{2,1,0:T(8,128)(2,1)S(1)} collective-permute-done((bf16[1,35,1536]{2,1,0:T(8,128)(2,1)S(1)}, bf16[1,35,1536]{2,1,0:T(8,128)(2,1)S(1)}, u32[]{:S(2)}, u32[]{:S(2)}) %collective-permute-start.4) | collective-permute-done | bytes 107552 | tf_op jit(solution)/shard_map/ppermute | solution.py:91
  53.4 0.7 %slice_bitcast_fusion.6 = f32[32,1536]{1,0:T(8,128)} fusion(f32[1,35,1536]{2,1,0:T(8,128)S(1)} %bitcast_add_fusion.1), kind=kLoop, calls=%fused_computation.51 | loop fusion | bytes 393216 | tf_op jit(solution)/shard_map/slice | solution.py:143
  54.1 0.6 %slice_bitcast_fusion.7 = f32[3,1536]{1,0:T(4,128)} fusion(f32[1,35,1536]{2,1,0:T(8,128)S(1)} %bitcast_add_fusion.1), kind=kLoop, calls=%fused_computation.63 | loop fusion | bytes 36864 | tf_op jit(solution)/shard_map/slice | solution.py:143
  (10 shorter events, 0.2 us)
Async XLA Ops:
  2.5 13.8 %copy-start.2 = (bf16[32,6144]{1,0:T(8,128)(2,1)S(1)}, bf16[32,6144]{1,0:T(8,128)(2,1)}, u32[]{:S(2)}) copy-start(bf16[32,6144]{1,0:T(8,128)(2,1)} %param.6) | copy-start | bytes 1179652
  15.5 4.7 %copy-start = (bf16[512,6144]{1,0:T(8,128)(2,1)}, bf16[512,6144]{1,0:T(8,128)(2,1)S(1)}, u32[]{:S(2)}) copy-start(bf16[512,6144]{1,0:T(8,128)(2,1)S(1)} %get-tuple-element.5) | copy-start | bytes 18874372
  15.5 4.7 %copy-start.1 = (bf16[512,6144]{1,0:T(8,128)(2,1)}, bf16[512,6144]{1,0:T(8,128)(2,1)S(1)}, u32[]{:S(2)}) copy-start(bf16[512,6144]{1,0:T(8,128)(2,1)S(1)} %get-tuple-element.4) | copy-start | bytes 18874372
  16.2 18.5 %copy-start.3 = (f32[32]{0:T(128)S(1)}, f32[32]{0:T(128)}, u32[]{:S(2)}) copy-start(f32[32]{0:T(128)} %param.9) | copy-start | bytes 388
  20.2 6.5 %collective-permute-start = (f32[2,32,512]{2,1,0:T(8,128)S(1)}, f32[2,32,512]{2,1,0:T(8,128)S(1)}, u32[]{:S(2)}, u32[]{:S(2)}) collective-permute-start(f32[2,32,512]{2,1,0:T(8,128)S(1)} %pad_maximum_fusion.2), channel_id=1, source_target_pairs={{0,4},{4,0},{8,12},{12,8},{16,20},{20,16},{24,28},{28,24},{1,5},{5... | collective-permute-start | bytes 393224 | tf_op jit(solution)/shard_map/ppermute | solution.py:75
  26.8 5.0 %collective-permute-start.1 = (f32[2,32,512]{2,1,0:T(8,128)S(1)}, f32[2,32,512]{2,1,0:T(8,128)S(1)}, u32[]{:S(2)}, u32[]{:S(2)}) collective-permute-start(f32[2,32,512]{2,1,0:T(8,128)S(1)} %fusion.32), channel_id=1, source_target_pairs={{0,8},{4,12},{8,0},{12,4},{16,24},{20,28},{24,16},{28,20},{1,9},{5... | collective-permute-start | bytes 393224 | tf_op jit(solution)/shard_map/ppermute | solution.py:75
  31.8 7.3 %collective-permute-start.2 = (f32[2,32,512]{2,1,0:T(8,128)S(1)}, f32[2,32,512]{2,1,0:T(8,128)S(1)}, u32[]{:S(2)}, u32[]{:S(2)}) collective-permute-start(f32[2,32,512]{2,1,0:T(8,128)S(1)} %fusion.37), channel_id=1, source_target_pairs={{0,16},{4,20},{8,24},{12,28},{16,0},{20,4},{24,8},{28,12},{1,17},{... | collective-permute-start | bytes 393224 | tf_op jit(solution)/shard_map/ppermute | solution.py:75
  45.9 1.9 %collective-permute-start.3 = (f32[2,35,1536]{2,1,0:T(8,128)S(1)}, f32[2,35,1536]{2,1,0:T(8,128)S(1)}, u32[]{:S(2)}, u32[]{:S(2)}) collective-permute-start(f32[2,35,1536]{2,1,0:T(8,128)S(1)} %select_bitcast_fusion), channel_id=1, source_target_pairs={{0,1},{1,0},{2,3},{3,2},{4,5},{5,4},{6,7},{7,6},{8,9},{9,8},{10,11... | collective-permute-start | bytes 1290248 | tf_op jit(solution)/shard_map/ppermute | solution.py:93
  48.0 5.4 %collective-permute-start.4 = (bf16[1,35,1536]{2,1,0:T(8,128)(2,1)S(1)}, bf16[1,35,1536]{2,1,0:T(8,128)(2,1)S(1)}, u32[]{:S(2)}, u32[]{:S(2)}) collective-permute-start(bf16[1,35,1536]{2,1,0:T(8,128)(2,1)S(1)} %fusion.28), channel_id=1, source_target_pairs={{0,2},{1,3},{2,0},{3,1},{4,6},{5,7},{6,4},{7,5},{8,10},{9,11},{10,... | collective-permute-start | bytes 322568 | tf_op jit(solution)/shard_map/ppermute | solution.py:91

commit v12 on v8

--- a/solution.py
+++ b/solution.py
@@ -77,9 +77,8 @@
     return x
 
 
-def halving_scatter(held, axis, n):
+def halving_rest(held, axis, n, step):
     me = lax.axis_index(axis)
-    step = 1
     while step < n:
         m = held.shape[0]
         pairs = held.reshape(m // 2, 2, *held.shape[1:])
@@ -103,13 +102,24 @@
         channels = site_strengths.shape[0]
         n_local = cell_coordinates_frac.shape[1]
         atoms_total = n_local * n_dom
-        live = jnp.arange(n_local) < occupied_site_tally[0]
-        charge_live = jnp.where(live[None, :], site_strengths, jnp.zeros_like(site_strengths))
+        rows = n_local // n_ka
+        bit0 = lax.axis_index("ka") % 2
+        odd_first = [b for b in range(1, n_ka, 2)] + [b for b in range(0, n_ka, 2)]
+        even_first = [b for b in range(0, n_ka, 2)] + [b for b in range(1, n_ka, 2)]
+
+        def ordered(x):
+            x4 = x.reshape(x.shape[0], n_ka, rows)
+            return jnp.where(bit0 == 0, x4[:, odd_first], x4[:, even_first]).reshape(x.shape)
+
+        slots = ordered(jnp.arange(n_local, dtype=jnp.int32)[None, :])[0]
+        live = slots < occupied_site_tally[0]
+        pos = ordered(cell_coordinates_frac)
+        charge_live = jnp.where(live[None, :], ordered(site_strengths), jnp.zeros_like(site_strengths))
         cartesian_mode_vector = miller_indices.astype(jnp.float32)
         t = (
-            cartesian_mode_vector[0][:, None] * cell_coordinates_frac[0][None, :]
-            + cartesian_mode_vector[1][:, None] * cell_coordinates_frac[1][None, :]
-            + cartesian_mode_vector[2][:, None] * cell_coordinates_frac[2][None, :]
+            cartesian_mode_vector[0][:, None] * pos[0][None, :]
+            + cartesian_mode_vector[1][:, None] * pos[1][None, :]
+            + cartesian_mode_vector[2][:, None] * pos[2][None, :]
         )
         cos_f, sin_f = turns_cos_sin(t)
         cos_table = cos_f.astype(jnp.bfloat16)
@@ -126,18 +136,26 @@
         cos_side, sin_side = reciprocal_filter_weight(
             s_both[0], s_both[1], cartesian_mode_vector, gaussian_spread, atoms_total
         )
-        field = jnp.dot(cos_side, cos_table, preferred_element_type=jnp.float32)
-        field = field + jnp.dot(sin_side, sin_table, preferred_element_type=jnp.float32)
         charge_f = charge_live.astype(jnp.float32)
-        head = jnp.where(live[None, :], field[:channels], 0.0)
-        force_rows = [
-            jnp.sum(charge_f * field[channels * (1 + d) : channels * (2 + d)], 0, keepdims=True)
-            for d in range(3)
-        ]
-        partial = jnp.concatenate([head] + force_rows, 0)
-        rows = n_local // n_ka
-        blocks = jnp.stack([partial[:, b * rows : (b + 1) * rows] for b in range(n_ka)], 0)
-        own = halving_scatter(blocks, "ka", n_ka)
+        half = n_local // 2
+
+        def partial_blocks(lo):
+            cols = slice(lo, lo + half)
+            field = jnp.dot(cos_side, cos_table[:, cols], preferred_element_type=jnp.float32)
+            field = field + jnp.dot(sin_side, sin_table[:, cols], preferred_element_type=jnp.float32)
+            head = jnp.where(live[None, cols], field[:channels], 0.0)
+            force_rows = [
+                jnp.sum(charge_f[:, cols] * field[channels * (1 + d) : channels * (2 + d)], 0, keepdims=True)
+                for d in range(3)
+            ]
+            partial = jnp.concatenate([head] + force_rows, 0)
+            return jnp.stack([partial[:, j * rows : (j + 1) * rows] for j in range(n_ka // 2)], 0)
+
+        sent = partial_blocks(0)
+        sent, cos_side, sin_side = lax.optimization_barrier((sent, cos_side, sin_side))
+        recv = lax.ppermute(sent, "ka", [(i, i ^ 1) for i in range(n_ka)])
+        held = partial_blocks(half) + recv
+        own = halving_rest(held, "ka", n_ka, 2)
         return (own[:channels], own[channels:])
 
     return local

time: 54.8 us -> 59.9 us (1.093)
  local copies, waits for them, and re-layouts: 3.14 us -> 8.55 us
  other arithmetic: 14.8 us -> 16.2 us
  waiting for transfers between devices: 16.6 us -> 15.5 us
  matrix products: 8.92 us -> 8.13 us
    gather x0 -> x6, local copies, waits for them, and re-layouts: none -> 3.5 us  [the longest x3 1.75 us: ordered(): x4[:, odd_first]]
    unnamed x12 -> x14, local copies, waits for them, and re-layouts: 0.66 us -> 2.5 us
    gather x0 -> x2, other arithmetic: none -> 1.35 us  [the longest x1 0.69 us: ordered(): x4[:, odd_first]]
    reshape x0 -> x1, local copies, waits for them, and re-layouts: none -> 1.02 us  [ordered(): x4 = x.reshape(x.shape[0], n_ka, rows)]
    slice x1 -> x4, local copies, waits for them, and re-layouts: 1.12 us -> 0.11 us  [the longest x3 0.06 us: partial_blocks(): head = jnp.where(live[None, cols], field[:channels], 0.0)]
    ppermute x2, waiting for transfers between devices: 5.47 us -> 4.6 us  [the longest x1 3.65 us: halving_rest(): lax.ppermute(send.astype(jnp.bfloat16), axis, pairs_list)]
    dot_general x2 -> x4, matrix products: 5 us -> 4.22 us  [the longest x2 3.04 us: partial_blocks(): jnp.dot(cos_side, cos_table[:, cols], preferred_element_type=jnp.float32)]
  transfers between devices with their start and end apart: 5 -> 5, of which waited for: 5 -> 5; matrix products, arithmetic and copies ran while one was open for 0% -> 2% of each run, Pallas kernels for 0% -> 0%
where the time goes in v12:
time: 59.9 us; the launch traced here: 59.7 us
  other arithmetic  16.2 us (27%)
  waiting for transfers between devices  15.5 us (26%)
  starting transfers between devices  9.62 us (16%)
  local copies, waits for them, and re-layouts  8.55 us (14%)
  matrix products  8.13 us (14%)
  between operations  1.66 us (3%)
    convert_element_type x1, other arithmetic, local(): sin_table = sin_f.astype(jnp.bfloat16)  13 us
    ppermute x3, waiting for transfers between devices, butterfly_sum(): x = x + lax.ppermute(x, axis, [(i, i ^ step) for i in range(n)])  10.9 us
    ppermute x3, starting transfers between devices, butterfly_sum(): x = x + lax.ppermute(x, axis, [(i, i ^ step) for i in range(n)])  7.77 us
    ppermute x1, waiting for transfers between devices, halving_rest(): lax.ppermute(send.astype(jnp.bfloat16), axis, pairs_list)  3.65 us
    dot_general x2, matrix products, partial_blocks(): jnp.dot(cos_side, cos_table[:, cols], preferred_element_type=jnp.float32)  3.04 us
    unnamed x14, local copies, waits for them, and re-layouts  2.5 us
    dot_general x1, matrix products, local(): lax.dot_general(charge_live, sin_table, tensor_product, preferred_element...  1.96 us
    dot_general x1, matrix products, local(): lax.dot_general(charge_live, cos_table, tensor_product, preferred_element...  1.95 us
  transfers between devices with their start and end apart: 5, of which 5 were waited for; matrix products, arithmetic and copies ran while one was open for 2% of the time, Pallas kernels for 0%

profile of v12, /device:TPU:0, one launch (start us, length us, event | category | flops | bytes accessed | tf_op | source)
XLA Modules:
  0.0 59.7 jit_solution(11582892880745461956)
XLA Ops:
  0.6 0.0 copy-start
  0.7 0.7 %pad_clamp_fusion.1 = s32[1024]{0:T(1024)S(1)} fusion(s32[4]{0:T(128)} %constant.94), kind=kLoop, calls=%fused_computation.76 | loop fusion | flops 1024 | bytes 4112 | tf_op jit(solution)/shard_map/gather | solution.py:112
  1.4 0.7 %pad_clamp_fusion = s32[1024]{0:T(1024)S(1)} fusion(s32[4]{0:T(128)} %constant.95), kind=kLoop, calls=%fused_computation.75 | loop fusion | flops 1024 | bytes 4112 | tf_op jit(solution)/shard_map/gather | solution.py:112
  2.0 0.6 gather_fusion.1
  2.6 0.6 gather_fusion
  3.2 0.0 copy-done
  3.2 0.6 %gather_fusion.5 = f32[4,3,1536]{2,1,0:T(4,128)S(1)} fusion(f32[3,4,1536]{2,0,1:T(4,128)S(1)} %bitcast.73, s32[1024]{0:T(1024)S(1)} %pad_clamp_fusion), kind=kCustom, calls=%fused_computation.5 | custom fusion | bytes 147472 | tf_op jit(solution)/shard_map/gather | solution.py:112
  3.8 0.6 %gather_fusion.4 = f32[4,3,1536]{2,1,0:T(4,128)S(1)} fusion(f32[3,4,1536]{2,0,1:T(4,128)S(1)} %bitcast.72, s32[1024]{0:T(1024)S(1)} %pad_clamp_fusion.1), kind=kCustom, calls=%fused_computation.4 | custom fusion | bytes 147472 | tf_op jit(solution)/shard_map/gather | solution.py:112
  4.4 1.0 %copy.20 = bf16[4,4,8,1536]{3,2,0,1:T(8,128)(2,1)S(1)} copy(bf16[4,4,8,1536]{3,2,1,0:T(8,128)(2,1)} %bitcast.81) | data formatting | bytes 786432 | tf_op jit(solution)/shard_map/reshape | solution.py:111
  5.4 0.6 gather_fusion.3
  6.0 0.6 gather_fusion.2
  7.2 0.7 %convert_element_type.31 = f32[3,512]{1,0:T(4,128)S(1)} convert(s32[3,512]{1,0:T(4,128)} %param.13) | non-fusion elementwise | flops 1536 | bytes 12288 | tf_op jit(solution)/shard_map/convert_element_type | solution.py:118
  8.0 0.1 fusion.27
  8.2 13.0 %multiply_convert_fusion = (bf16[512,6144]{1,0:T(8,128)(2,1)S(1)}, bf16[512,6144]{1,0:T(8,128)(2,1)S(1)}) fusion(f32[6144]{0:T(1024)S(1)} %bitcast.84, f32[512]{0:T(512)S(1)} %bitcast.100, f32[6144]{0:T(1024)S(1)} %bitcast.85, f32[512]{0:T(512)S(1)} %bitcast.101, f32[6144]{0:T(1024)S(1)} %bitcast.83, f32[512]{0:T(512)S(1)} %bitcast.102), kind=kLoop, calls=%fused_computation.6 | loop fusion | flops 97517568 | bytes 12662784 | tf_op jit(solution)/shard_map/convert_element_type | solution.py:126
  21.2 0.0 copy-start.1
  21.2 0.0 copy-start.3
  21.2 2.0 %convolution_bitcast_fusion.1 = f32[1,32,512]{2,1,0:T(8,128)S(1)} fusion(bf16[512,6144]{1,0:T(8,128)(2,1)S(1)} %get-tuple-element.7, bf16[32,6144]{1,0:T(8,128)(2,1)S(1)} %bitcast.76, pred[6144]{0:T(1024)(128)(4,1)S(1)} %lt.47), kind=kOutput, calls=%fused_computation.23 | convolution fusion | flops 201523200 | bytes 6756352 | tf_op jit(solution)/shard_map/dot_general | solution.py:129
  23.2 2.0 %convolution_bitcast_fusion = f32[1,32,512]{2,1,0:T(8,128)S(1)} fusion(bf16[512,6144]{1,0:T(8,128)(2,1)S(1)} %get-tuple-element.8, bf16[32,6144]{1,0:T(8,128)(2,1)S(1)} %bitcast.77, pred[6144]{0:T(1024)(128)(4,1)S(1)} %lt.47), kind=kOutput, calls=%fused_computation.22 | convolution fusion | flops 201523200 | bytes 6756352 | tf_op jit(solution)/shard_map/dot_general | solution.py:132
  25.2 0.0 copy-done.1
  25.2 0.6 copy-done.3
  25.8 3.0 %collective-permute-start = (f32[2,32,512]{2,1,0:T(8,128)S(1)}, f32[2,32,512]{2,1,0:T(8,128)S(1)}, u32[]{:S(2)}, u32[]{:S(2)}) collective-permute-start(f32[2,32,512]{2,1,0:T(8,128)S(1)} %pad_maximum_fusion.3), channel_id=1, source_target_pairs={{0,4},{4,0},{8,12},{12,8},{16,20},{20,16},{24,28},{28,24},{1,5},{5... | collective-permute-start | bytes 393224 | tf_op jit(solution)/shard_map/ppermute | solution.py:75
  28.8 0.1 fusion.15
  28.9 3.4 %collective-permute-done = f32[2,32,512]{2,1,0:T(8,128)S(1)} collective-permute-done((f32[2,32,512]{2,1,0:T(8,128)S(1)}, f32[2,32,512]{2,1,0:T(8,128)S(1)}, u32[]{:S(2)}, u32[]{:S(2)}) %collective-permute-start) | collective-permute-done | bytes 131104 | tf_op jit(solution)/shard_map/ppermute | solution.py:75
  32.3 1.9 %collective-permute-start.1 = (f32[2,32,512]{2,1,0:T(8,128)S(1)}, f32[2,32,512]{2,1,0:T(8,128)S(1)}, u32[]{:S(2)}, u32[]{:S(2)}) collective-permute-start(f32[2,32,512]{2,1,0:T(8,128)S(1)} %fusion.23), channel_id=1, source_target_pairs={{0,8},{4,12},{8,0},{12,4},{16,24},{20,28},{24,16},{28,20},{1,9},{5... | collective-permute-start | bytes 393224 | tf_op jit(solution)/shard_map/ppermute | solution.py:75
  34.3 3.1 %collective-permute-done.1 = f32[2,32,512]{2,1,0:T(8,128)S(1)} collective-permute-done((f32[2,32,512]{2,1,0:T(8,128)S(1)}, f32[2,32,512]{2,1,0:T(8,128)S(1)}, u32[]{:S(2)}, u32[]{:S(2)}) %collective-permute-start.1) | collective-permute-done | bytes 131104 | tf_op jit(solution)/shard_map/ppermute | solution.py:75
  37.4 2.9 %collective-permute-start.2 = (f32[2,32,512]{2,1,0:T(8,128)S(1)}, f32[2,32,512]{2,1,0:T(8,128)S(1)}, u32[]{:S(2)}, u32[]{:S(2)}) collective-permute-start(f32[2,32,512]{2,1,0:T(8,128)S(1)} %fusion.33), channel_id=1, source_target_pairs={{0,16},{4,20},{8,24},{12,28},{16,0},{20,4},{24,8},{28,12},{1,17},{... | collective-permute-start | bytes 393224 | tf_op jit(solution)/shard_map/ppermute | solution.py:75
  40.3 0.0 copy-done.4
  40.3 4.5 %collective-permute-done.2 = f32[2,32,512]{2,1,0:T(8,128)S(1)} collective-permute-done((f32[2,32,512]{2,1,0:T(8,128)S(1)}, f32[2,32,512]{2,1,0:T(8,128)S(1)}, u32[]{:S(2)}, u32[]{:S(2)}) %collective-permute-start.2) | collective-permute-done | bytes 131104 | tf_op jit(solution)/shard_map/ppermute | solution.py:75
  44.8 0.1 multiply_convert_fusion.3
  44.9 2.5 %fusion.6 = f32[128,3072]{1,0:T(8,128)S(1)} fusion(bf16[512,6144]{1,0:T(8,128)(2,1)} %copy-done.3, bf16[32,512]{1,0:T(8,128)(2,1)S(1)} %get-tuple-element.57, bf16[32,512]{1,0:T(8,128)(2,1)S(1)} %get-tuple-element.56, bf16[32,512]{1,0:T(8,128)(2,1)S(1)} %get-tuple-element.58, bf16[32,512]{1,0:T(8,128)(2,1)S(1)} %get-tuple-element.39), kind=kOutput, calls=%fused_computation.20 | convolution fusion | flops 403177472 | bytes 4849664 | tf_op jit(solution)/shard_map/dot_general | solution.py:144
  47.4 0.0 slice-start
  47.4 0.0 slice-start.1
  47.4 0.6 convolution_add_fusion.1
  48.0 0.2 fusion.14
  48.2 0.1 pad_maximum_fusion
  48.4 1.2 %slice-done = s8[4194304]{0:T(1024)(128)(4,1)S(1)} async-done(((s8[6291456]{0:T(1024)(128)(4,1)}), s8[4194304]{0:T(1024)(128)(4,1)S(1)}, s32[]{:S(2)}) %slice-start) | async-done | bytes 4194328
  49.6 0.7 %slice-done.1 = s8[2097152]{0:T(1024)(128)(4,1)S(1)} async-done(((s8[6291456]{0:T(1024)(128)(4,1)}), s8[2097152]{0:T(1024)(128)(4,1)S(1)}, s32[]{:S(2)}) %slice-start.1) | async-done | bytes 2097176
  50.3 0.6 fusion.3
  50.8 0.1 collective-permute-start.3
  50.9 0.6 convolution_add_fusion
  51.5 0.2 fusion.11
  51.7 0.1 pad_maximum_fusion.2
  51.8 0.9 %collective-permute-done.3 = f32[2,35,1536]{2,1,0:T(8,128)S(1)} collective-permute-done((f32[2,35,1536]{2,1,0:T(8,128)S(1)}, f32[2,35,1536]{2,1,0:T(8,128)S(1)}, u32[]{:S(2)}, u32[]{:S(2)}) %collective-permute-start.3) | collective-permute-done | bytes 430112 | tf_op jit(solution)/shard_map/ppermute | solution.py:156
  52.8 0.1 fusion.8
  52.9 1.8 %collective-permute-start.4 = (bf16[1,35,1536]{2,1,0:T(8,128)(2,1)S(1)}, bf16[1,35,1536]{2,1,0:T(8,128)(2,1)S(1)}, u32[]{:S(2)}, u32[]{:S(2)}) collective-permute-start(bf16[1,35,1536]{2,1,0:T(8,128)(2,1)S(1)} %fusion.18), channel_id=1, source_target_pairs={{0,2},{1,3},{2,0},{3,1},{4,6},{5,7},{6,4},{7,5},{8,10},{9,11},{10,... | collective-permute-start | bytes 322568 | tf_op jit(solution)/shard_map/ppermute | solution.py:90
  54.7 3.6 %collective-permute-done.4 = bf16[1,35,1536]{2,1,0:T(8,128)(2,1)S(1)} collective-permute-done((bf16[1,35,1536]{2,1,0:T(8,128)(2,1)S(1)}, bf16[1,35,1536]{2,1,0:T(8,128)(2,1)S(1)}, u32[]{:S(2)}, u32[]{:S(2)}) %collective-permute-start.4) | collective-permute-done | bytes 107552 | tf_op jit(solution)/shard_map/ppermute | solution.py:90
  58.4 0.6 %slice_bitcast_fusion.7 = f32[3,1536]{1,0:T(4,128)} fusion(f32[1,35,1536]{2,1,0:T(8,128)S(1)} %bitcast_add_fusion), kind=kLoop, calls=%fused_computation.72 | loop fusion | bytes 36864 | tf_op jit(solution)/shard_map/slice | solution.py:159
  59.0 0.7 %slice_bitcast_fusion.4 = f32[32,1536]{1,0:T(8,128)} fusion(f32[1,35,1536]{2,1,0:T(8,128)S(1)} %bitcast_add_fusion), kind=kLoop, calls=%fused_computation.53 | loop fusion | bytes 393216 | tf_op jit(solution)/shard_map/slice | solution.py:159
  (27 shorter events, 0.5 us)
Async XLA Ops:
  0.6 2.5 %copy-start = (f32[3,6144]{1,0:T(4,128)S(1)}, f32[3,6144]{1,0:T(4,128)}, u32[]{:S(2)}) copy-start(f32[3,6144]{1,0:T(4,128)} %param.11) | copy-start | bytes 221188
  21.2 4.0 %copy-start.1 = (bf16[512,6144]{1,0:T(8,128)(2,1)}, bf16[512,6144]{1,0:T(8,128)(2,1)S(1)}, u32[]{:S(2)}) copy-start(bf16[512,6144]{1,0:T(8,128)(2,1)S(1)} %get-tuple-element.8) | copy-start | bytes 18874372
  21.2 4.5 %copy-start.3 = (bf16[512,6144]{1,0:T(8,128)(2,1)}, bf16[512,6144]{1,0:T(8,128)(2,1)S(1)}, u32[]{:S(2)}) copy-start(bf16[512,6144]{1,0:T(8,128)(2,1)S(1)} %get-tuple-element.7) | copy-start | bytes 18874372
  23.2 17.1 %copy-start.4 = (f32[32]{0:T(128)S(1)}, f32[32]{0:T(128)}, u32[]{:S(2)}) copy-start(f32[32]{0:T(128)} %param.15) | copy-start | bytes 388
  25.8 6.5 %collective-permute-start = (f32[2,32,512]{2,1,0:T(8,128)S(1)}, f32[2,32,512]{2,1,0:T(8,128)S(1)}, u32[]{:S(2)}, u32[]{:S(2)}) collective-permute-start(f32[2,32,512]{2,1,0:T(8,128)S(1)} %pad_maximum_fusion.3), channel_id=1, source_target_pairs={{0,4},{4,0},{8,12},{12,8},{16,20},{20,16},{24,28},{28,24},{1,5},{5... | collective-permute-start | bytes 393224 | tf_op jit(solution)/shard_map/ppermute | solution.py:75
  32.3 5.0 %collective-permute-start.1 = (f32[2,32,512]{2,1,0:T(8,128)S(1)}, f32[2,32,512]{2,1,0:T(8,128)S(1)}, u32[]{:S(2)}, u32[]{:S(2)}) collective-permute-start(f32[2,32,512]{2,1,0:T(8,128)S(1)} %fusion.23), channel_id=1, source_target_pairs={{0,8},{4,12},{8,0},{12,4},{16,24},{20,28},{24,16},{28,20},{1,9},{5... | collective-permute-start | bytes 393224 | tf_op jit(solution)/shard_map/ppermute | solution.py:75
  34.3 13.1 %copy-start.2 = (bf16[512,6144]{1,0:T(8,128)(2,1)S(1)}, bf16[512,6144]{1,0:T(8,128)(2,1)}, u32[]{:S(2)}) copy-start(bf16[512,6144]{1,0:T(8,128)(2,1)} %copy-done.1) | copy-start | bytes 18874372
  37.4 7.3 %collective-permute-start.2 = (f32[2,32,512]{2,1,0:T(8,128)S(1)}, f32[2,32,512]{2,1,0:T(8,128)S(1)}, u32[]{:S(2)}, u32[]{:S(2)}) collective-permute-start(f32[2,32,512]{2,1,0:T(8,128)S(1)} %fusion.33), channel_id=1, source_target_pairs={{0,16},{4,20},{8,24},{12,28},{16,0},{20,4},{24,8},{28,12},{1,17},{... | collective-permute-start | bytes 393224 | tf_op jit(solution)/shard_map/ppermute | solution.py:75
  47.4 2.2 %slice-start = ((s8[6291456]{0:T(1024)(128)(4,1)}), s8[4194304]{0:T(1024)(128)(4,1)S(1)}, s32[]{:S(2)}) async-start(s8[6291456]{0:T(1024)(128)(4,1)} %bitcast.74), calls=%async_computation | async-start | bytes 8388608
  47.4 2.8 %slice-start.1 = ((s8[6291456]{0:T(1024)(128)(4,1)}), s8[2097152]{0:T(1024)(128)(4,1)S(1)}, s32[]{:S(2)}) async-start(s8[6291456]{0:T(1024)(128)(4,1)} %bitcast.74), calls=%async_computation.1 | async-start | bytes 4194304
  50.8 1.9 %collective-permute-start.3 = (f32[2,35,1536]{2,1,0:T(8,128)S(1)}, f32[2,35,1536]{2,1,0:T(8,128)S(1)}, u32[]{:S(2)}, u32[]{:S(2)}) collective-permute-start(f32[2,35,1536]{2,1,0:T(8,128)S(1)} %pad_maximum_fusion.1), channel_id=1, source_target_pairs={{0,1},{1,0},{2,3},{3,2},{4,5},{5,4},{6,7},{7,6},{8,9},{9,8},{10,11... | collective-permute-start | bytes 1290248 | tf_op jit(solution)/shard_map/ppermute | solution.py:156
  52.9 5.4 %collective-permute-start.4 = (bf16[1,35,1536]{2,1,0:T(8,128)(2,1)S(1)}, bf16[1,35,1536]{2,1,0:T(8,128)(2,1)S(1)}, u32[]{:S(2)}, u32[]{:S(2)}) collective-permute-start(bf16[1,35,1536]{2,1,0:T(8,128)(2,1)S(1)} %fusion.18), channel_id=1, source_target_pairs={{0,2},{1,3},{2,0},{3,1},{4,6},{5,7},{6,4},{7,5},{8,10},{9,11},{10,... | collective-permute-start | bytes 322568 | tf_op jit(solution)/shard_map/ppermute | solution.py:90

commit v13 on v8

--- a/solution.py
+++ b/solution.py
@@ -88,12 +88,15 @@
         send = jnp.where(bit == 0, pairs[:, 1], pairs[:, 0])
         pairs_list = [(i, i ^ step) for i in range(n)]
         if step >= 2:
-            recv = lax.ppermute(send.astype(jnp.bfloat16), axis, pairs_list).astype(jnp.float32)
+            recv = lax.ppermute(send.astype(jnp.bfloat16), axis, pairs_list)
         else:
             recv = lax.ppermute(send, axis, pairs_list)
+        if step * 2 >= n:
+            return keep[0], recv[0]
+        recv = recv.astype(jnp.float32)
         held = keep + recv
         step *= 2
-    return held[0]
+    return held[0], jnp.zeros_like(held[0])
 
 
 def make_local(n_dom, n_ka):
@@ -137,8 +140,10 @@
         partial = jnp.concatenate([head] + force_rows, 0)
         rows = n_local // n_ka
         blocks = jnp.stack([partial[:, b * rows : (b + 1) * rows] for b in range(n_ka)], 0)
-        own = halving_scatter(blocks, "ka", n_ka)
-        return (own[:channels], own[channels:])
+        own, other = halving_scatter(blocks, "ka", n_ka)
+        potential = own[:channels] + other[:channels].astype(jnp.float32)
+        forces = own[channels:] + other[channels:].astype(jnp.float32)
+        return (potential, forces)
 
     return local
 

time: 54.8 us -> 54.8 us (level)
  other arithmetic: 14.8 us -> 16.1 us
  local copies, waits for them, and re-layouts: 3.14 us -> 1.84 us
    slice x2 -> x0, local copies, waits for them, and re-layouts: 1.3 us -> none  [local(): return (own[:channels], own[channels:])]
    add x1 -> x2, other arithmetic: 0.04 us -> 1.31 us  [the longest x1 0.7 us: local(): potential = own[:channels] + other[:channels].astype(jnp.float32)]
where the time goes in v13:
time: 54.8 us; the launch traced here: 54.6 us
  waiting for transfers between devices  16.6 us (30%)
  other arithmetic  16.1 us (29%)
  starting transfers between devices  9.62 us (18%)
  matrix products  8.92 us (16%)
  local copies, waits for them, and re-layouts  1.84 us (3%)
  between operations  1.54 us (3%)
    convert_element_type x1, other arithmetic, local(): sin_table = sin_f.astype(jnp.bfloat16)  13 us
    ppermute x3, waiting for transfers between devices, butterfly_sum(): x = x + lax.ppermute(x, axis, [(i, i ^ step) for i in range(n)])  11.1 us
    ppermute x3, starting transfers between devices, butterfly_sum(): x = x + lax.ppermute(x, axis, [(i, i ^ step) for i in range(n)])  7.77 us
    dot_general x1, matrix products, local(): field = jnp.dot(cos_side, cos_table, preferred_element_type=jnp.float32)  4 us
    ppermute x1, waiting for transfers between devices, halving_scatter(): recv = lax.ppermute(send.astype(jnp.bfloat16), axis, pairs_list)  3.62 us
    dot_general x1, matrix products, local(): lax.dot_general(charge_live, cos_table, tensor_product, preferred_element...  1.97 us
    dot_general x1, matrix products, local(): lax.dot_general(charge_live, sin_table, tensor_product, preferred_element...  1.95 us
    ppermute x1, waiting for transfers between devices, halving_scatter(): recv = lax.ppermute(send, axis, pairs_list)  1.82 us
  transfers between devices with their start and end apart: 5, of which 5 were waited for; matrix products, arithmetic and copies ran while one was open for 0% of the time, Pallas kernels for 0%

profile of v13, /device:TPU:0, one launch (start us, length us, event | category | flops | bytes accessed | tf_op | source)
XLA Modules:
  0.0 54.6 jit_solution(12713519879195174549)
XLA Ops:
  0.6 0.7 %convert_element_type.36 = f32[3,512]{1,0:T(4,128)S(1)} convert(s32[3,512]{1,0:T(4,128)} %param.7) | non-fusion elementwise | flops 1536 | bytes 12288 | tf_op jit(solution)/shard_map/convert_element_type | solution.py:111
  1.4 1.1 %fusion.34 = (f32[1,6144]{1,0:T(1,128)S(1)}, f32[1,6144]{1,0:T(1,128)S(1)}, f32[1,6144]{1,0:T(1,128)S(1)}) fusion(f32[3,6144]{1,0:T(4,128)} %param.5), kind=kLoop, calls=%fused_computation.80 | loop fusion | bytes 147456 | tf_op jit(solution)/shard_map/slice | solution.py:113
  2.5 0.0 copy-start.2
  2.5 13.0 %multiply_convert_fusion = (bf16[512,6144]{1,0:T(8,128)(2,1)S(1)}, bf16[512,6144]{1,0:T(8,128)(2,1)S(1)}) fusion(f32[6144]{0:T(1024)S(1)} %bitcast.82, f32[512]{0:T(512)S(1)} %bitcast.92, f32[6144]{0:T(1024)S(1)} %bitcast.83, f32[512]{0:T(512)S(1)} %bitcast.93, f32[6144]{0:T(1024)S(1)} %bitcast.81, f32[512]{0:T(512)S(1)} %bitcast.94), kind=kLoop, calls=%fused_computation | loop fusion | flops 97517568 | bytes 12662784 | tf_op jit(solution)/shard_map/convert_element_type | solution.py:119
  15.5 0.0 copy-start
  15.5 0.0 copy-start.1
  16.2 0.0 copy-done.2
  16.2 0.0 copy-start.3
  16.2 2.0 %convolution_bitcast_fusion = f32[1,32,512]{2,1,0:T(8,128)S(1)} fusion(bf16[512,6144]{1,0:T(8,128)(2,1)S(1)} %get-tuple-element.5, bf16[32,6144]{1,0:T(8,128)(2,1)S(1)} %copy-done.2, pred[6144]{0:T(1024)(128)(4,1)S(1)} %iota_compare_fusion), kind=kOutput, calls=%fused_computation.12 | convolution fusion | flops 201523200 | bytes 6756352 | tf_op jit(solution)/shard_map/dot_general | solution.py:125
  18.2 2.0 %convolution_bitcast_fusion.1 = f32[1,32,512]{2,1,0:T(8,128)S(1)} fusion(bf16[512,6144]{1,0:T(8,128)(2,1)S(1)} %get-tuple-element.4, bf16[32,6144]{1,0:T(8,128)(2,1)S(1)} %copy-done.2, pred[6144]{0:T(1024)(128)(4,1)S(1)} %iota_compare_fusion), kind=kOutput, calls=%fused_computation.13 | convolution fusion | flops 201523200 | bytes 6756352 | tf_op jit(solution)/shard_map/dot_general | solution.py:122
  20.2 0.0 copy-done
  20.2 0.0 copy-done.1
  20.2 3.0 %collective-permute-start = (f32[2,32,512]{2,1,0:T(8,128)S(1)}, f32[2,32,512]{2,1,0:T(8,128)S(1)}, u32[]{:S(2)}, u32[]{:S(2)}) collective-permute-start(f32[2,32,512]{2,1,0:T(8,128)S(1)} %pad_maximum_fusion.2), channel_id=1, source_target_pairs={{0,4},{4,0},{8,12},{12,8},{16,20},{20,16},{24,28},{28,24},{1,5},{5... | collective-permute-start | bytes 393224 | tf_op jit(solution)/shard_map/ppermute | solution.py:75
  23.2 3.5 %collective-permute-done = f32[2,32,512]{2,1,0:T(8,128)S(1)} collective-permute-done((f32[2,32,512]{2,1,0:T(8,128)S(1)}, f32[2,32,512]{2,1,0:T(8,128)S(1)}, u32[]{:S(2)}, u32[]{:S(2)}) %collective-permute-start) | collective-permute-done | bytes 131104 | tf_op jit(solution)/shard_map/ppermute | solution.py:75
  26.8 1.9 %collective-permute-start.1 = (f32[2,32,512]{2,1,0:T(8,128)S(1)}, f32[2,32,512]{2,1,0:T(8,128)S(1)}, u32[]{:S(2)}, u32[]{:S(2)}) collective-permute-start(f32[2,32,512]{2,1,0:T(8,128)S(1)} %fusion.30), channel_id=1, source_target_pairs={{0,8},{4,12},{8,0},{12,4},{16,24},{20,28},{24,16},{28,20},{1,9},{5... | collective-permute-start | bytes 393224 | tf_op jit(solution)/shard_map/ppermute | solution.py:75
  28.6 3.2 %collective-permute-done.1 = f32[2,32,512]{2,1,0:T(8,128)S(1)} collective-permute-done((f32[2,32,512]{2,1,0:T(8,128)S(1)}, f32[2,32,512]{2,1,0:T(8,128)S(1)}, u32[]{:S(2)}, u32[]{:S(2)}) %collective-permute-start.1) | collective-permute-done | bytes 131104 | tf_op jit(solution)/shard_map/ppermute | solution.py:75
  31.8 2.9 %collective-permute-start.2 = (f32[2,32,512]{2,1,0:T(8,128)S(1)}, f32[2,32,512]{2,1,0:T(8,128)S(1)}, u32[]{:S(2)}, u32[]{:S(2)}) collective-permute-start(f32[2,32,512]{2,1,0:T(8,128)S(1)} %fusion.39), channel_id=1, source_target_pairs={{0,16},{4,20},{8,24},{12,28},{16,0},{20,4},{24,8},{28,12},{1,17},{... | collective-permute-start | bytes 393224 | tf_op jit(solution)/shard_map/ppermute | solution.py:75
  34.7 0.0 copy-done.3
  34.7 4.5 %collective-permute-done.2 = f32[2,32,512]{2,1,0:T(8,128)S(1)} collective-permute-done((f32[2,32,512]{2,1,0:T(8,128)S(1)}, f32[2,32,512]{2,1,0:T(8,128)S(1)}, u32[]{:S(2)}, u32[]{:S(2)}) %collective-permute-start.2) | collective-permute-done | bytes 131104 | tf_op jit(solution)/shard_map/ppermute | solution.py:75
  39.2 0.1 multiply_convert_fusion.3
  39.3 0.0 slice-start
  39.3 0.0 slice-start.1
  39.3 4.0 %fusion.7 = f32[128,6144]{1,0:T(8,128)S(1)} fusion(bf16[512,6144]{1,0:T(8,128)(2,1)} %copy-done.1, bf16[32,512]{1,0:T(8,128)(2,1)S(1)} %get-tuple-element.45, bf16[32,512]{1,0:T(8,128)(2,1)S(1)} %get-tuple-element.44, bf16[32,512]{1,0:T(8,128)(2,1)S(1)} %get-tuple-element.46, bf16[32,512]{1,0:T(8,128)(2,1)S(1)} %get-tuple-element.29), kind=kOutput, calls=%fused_computation.35 | convolution fusion | flops 805830656 | bytes 9568256 | tf_op jit(solution)/shard_map/dot_general | solution.py:132
  43.4 0.0 slice-done
  43.4 0.6 %slice-done.1 = s8[2097152]{0:T(1024)(128)(4,1)S(1)} async-done(((s8[6291456]{0:T(1024)(128)(4,1)}), s8[2097152]{0:T(1024)(128)(4,1)S(1)}, s32[]{:S(2)}) %slice-start.1) | async-done | bytes 2097176
  44.0 1.0 %convolution_add_fusion = f32[128,6144]{1,0:T(8,128)S(1)} fusion(f32[128,6144]{1,0:T(8,128)S(1)} %fusion.7, bf16[512,6144]{1,0:T(8,128)(2,1)S(1)} %bitcast.75, bf16[32,512]{1,0:T(8,128)(2,1)S(1)} %get-tuple-element.28, bf16[32,512]{1,0:T(8,128)(2,1)S(1)} %get-tuple-element.27, bf16[32,512]{1,0:T(8,128)(2,1)S(1)} %get-tuple-element.11, ...), kind=kOutput, calls=%fused_computation.8 | convolution fusion | flops 806617088 | bytes 12713984 | tf_op jit(solution)/shard_map/dot_general | solution.py:133
  45.0 0.4 fusion.2
  45.4 0.1 pad_maximum_fusion
  45.6 0.1 slice_bitcast_fusion.5
  45.6 0.1 pad_maximum_fusion.1
  45.7 0.1 select_bitcast_fusion
  45.8 0.1 collective-permute-start.3
  45.9 1.8 %collective-permute-done.3 = f32[2,35,1536]{2,1,0:T(8,128)S(1)} collective-permute-done((f32[2,35,1536]{2,1,0:T(8,128)S(1)}, f32[2,35,1536]{2,1,0:T(8,128)S(1)}, u32[]{:S(2)}, u32[]{:S(2)}) %collective-permute-start.3) | collective-permute-done | bytes 430112 | tf_op jit(solution)/shard_map/ppermute | solution.py:93
  47.7 0.1 fusion.5
  47.8 1.8 %collective-permute-start.4 = (bf16[1,35,1536]{2,1,0:T(8,128)(2,1)S(1)}, bf16[1,35,1536]{2,1,0:T(8,128)(2,1)S(1)}, u32[]{:S(2)}, u32[]{:S(2)}) collective-permute-start(bf16[1,35,1536]{2,1,0:T(8,128)(2,1)S(1)} %fusion.22), channel_id=1, source_target_pairs={{0,2},{1,3},{2,0},{3,1},{4,6},{5,7},{6,4},{7,5},{8,10},{9,11},{10,... | collective-permute-start | bytes 322568 | tf_op jit(solution)/shard_map/ppermute | solution.py:91
  49.6 3.6 %collective-permute-done.4 = bf16[1,35,1536]{2,1,0:T(8,128)(2,1)S(1)} collective-permute-done((bf16[1,35,1536]{2,1,0:T(8,128)(2,1)S(1)}, bf16[1,35,1536]{2,1,0:T(8,128)(2,1)S(1)}, u32[]{:S(2)}, u32[]{:S(2)}) %collective-permute-start.4) | collective-permute-done | bytes 107552 | tf_op jit(solution)/shard_map/ppermute | solution.py:91
  53.2 0.6 %fusion.25 = f32[3,1536]{1,0:T(4,128)} fusion(f32[1,35,1536]{2,1,0:T(8,128)S(1)} %select_bitcast_fusion.1, bf16[1,35,1536]{2,1,0:T(8,128)(2,1)S(1)} %collective-permute-done.4), kind=kLoop, calls=%fused_computation.63 | loop fusion | flops 9216 | bytes 46080 | tf_op jit(solution)/shard_map/add | solution.py:145
  53.9 0.7 %fusion.6 = f32[32,1536]{1,0:T(8,128)} fusion(f32[1,35,1536]{2,1,0:T(8,128)S(1)} %select_bitcast_fusion.1, bf16[1,35,1536]{2,1,0:T(8,128)(2,1)S(1)} %collective-permute-done.4), kind=kLoop, calls=%fused_computation.33 | loop fusion | flops 98304 | bytes 491520 | tf_op jit(solution)/shard_map/add | solution.py:144
  (11 shorter events, 0.2 us)
Async XLA Ops:
  2.5 13.8 %copy-start.2 = (bf16[32,6144]{1,0:T(8,128)(2,1)S(1)}, bf16[32,6144]{1,0:T(8,128)(2,1)}, u32[]{:S(2)}) copy-start(bf16[32,6144]{1,0:T(8,128)(2,1)} %param.6) | copy-start | bytes 1179652
  15.5 4.7 %copy-start = (bf16[512,6144]{1,0:T(8,128)(2,1)}, bf16[512,6144]{1,0:T(8,128)(2,1)S(1)}, u32[]{:S(2)}) copy-start(bf16[512,6144]{1,0:T(8,128)(2,1)S(1)} %get-tuple-element.5) | copy-start | bytes 18874372
  15.5 4.7 %copy-start.1 = (bf16[512,6144]{1,0:T(8,128)(2,1)}, bf16[512,6144]{1,0:T(8,128)(2,1)S(1)}, u32[]{:S(2)}) copy-start(bf16[512,6144]{1,0:T(8,128)(2,1)S(1)} %get-tuple-element.4) | copy-start | bytes 18874372
  16.2 18.5 %copy-start.3 = (f32[32]{0:T(128)S(1)}, f32[32]{0:T(128)}, u32[]{:S(2)}) copy-start(f32[32]{0:T(128)} %param.9) | copy-start | bytes 388
  20.2 6.5 %collective-permute-start = (f32[2,32,512]{2,1,0:T(8,128)S(1)}, f32[2,32,512]{2,1,0:T(8,128)S(1)}, u32[]{:S(2)}, u32[]{:S(2)}) collective-permute-start(f32[2,32,512]{2,1,0:T(8,128)S(1)} %pad_maximum_fusion.2), channel_id=1, source_target_pairs={{0,4},{4,0},{8,12},{12,8},{16,20},{20,16},{24,28},{28,24},{1,5},{5... | collective-permute-start | bytes 393224 | tf_op jit(solution)/shard_map/ppermute | solution.py:75
  26.8 5.0 %collective-permute-start.1 = (f32[2,32,512]{2,1,0:T(8,128)S(1)}, f32[2,32,512]{2,1,0:T(8,128)S(1)}, u32[]{:S(2)}, u32[]{:S(2)}) collective-permute-start(f32[2,32,512]{2,1,0:T(8,128)S(1)} %fusion.30), channel_id=1, source_target_pairs={{0,8},{4,12},{8,0},{12,4},{16,24},{20,28},{24,16},{28,20},{1,9},{5... | collective-permute-start | bytes 393224 | tf_op jit(solution)/shard_map/ppermute | solution.py:75
  31.8 7.3 %collective-permute-start.2 = (f32[2,32,512]{2,1,0:T(8,128)S(1)}, f32[2,32,512]{2,1,0:T(8,128)S(1)}, u32[]{:S(2)}, u32[]{:S(2)}) collective-permute-start(f32[2,32,512]{2,1,0:T(8,128)S(1)} %fusion.39), channel_id=1, source_target_pairs={{0,16},{4,20},{8,24},{12,28},{16,0},{20,4},{24,8},{28,12},{1,17},{... | collective-permute-start | bytes 393224 | tf_op jit(solution)/shard_map/ppermute | solution.py:75
  39.3 4.1 %slice-start = ((s8[6291456]{0:T(1024)(128)(4,1)}), s8[4194304]{0:T(1024)(128)(4,1)S(1)}, s32[]{:S(2)}) async-start(s8[6291456]{0:T(1024)(128)(4,1)} %bitcast.74), calls=%async_computation | async-start | bytes 8388608
  39.3 4.6 %slice-start.1 = ((s8[6291456]{0:T(1024)(128)(4,1)}), s8[2097152]{0:T(1024)(128)(4,1)S(1)}, s32[]{:S(2)}) async-start(s8[6291456]{0:T(1024)(128)(4,1)} %bitcast.74), calls=%async_computation.1 | async-start | bytes 4194304
  45.8 1.9 %collective-permute-start.3 = (f32[2,35,1536]{2,1,0:T(8,128)S(1)}, f32[2,35,1536]{2,1,0:T(8,128)S(1)}, u32[]{:S(2)}, u32[]{:S(2)}) collective-permute-start(f32[2,35,1536]{2,1,0:T(8,128)S(1)} %select_bitcast_fusion), channel_id=1, source_target_pairs={{0,1},{1,0},{2,3},{3,2},{4,5},{5,4},{6,7},{7,6},{8,9},{9,8},{10,11... | collective-permute-start | bytes 1290248 | tf_op jit(solution)/shard_map/ppermute | solution.py:93
  47.8 5.4 %collective-permute-start.4 = (bf16[1,35,1536]{2,1,0:T(8,128)(2,1)S(1)}, bf16[1,35,1536]{2,1,0:T(8,128)(2,1)S(1)}, u32[]{:S(2)}, u32[]{:S(2)}) collective-permute-start(bf16[1,35,1536]{2,1,0:T(8,128)(2,1)S(1)} %fusion.22), channel_id=1, source_target_pairs={{0,2},{1,3},{2,0},{3,1},{4,6},{5,7},{6,4},{7,5},{8,10},{9,11},{10,... | collective-permute-start | bytes 322568 | tf_op jit(solution)/shard_map/ppermute | solution.py:91

commit v14 on v13

--- a/solution.py
+++ b/solution.py
@@ -69,11 +69,20 @@
     return (cos_side.astype(jnp.bfloat16), sin_side.astype(jnp.bfloat16))
 
 
-def butterfly_sum(x, axis, n):
+def butterfly_sum(x, n_dom, n_ka):
+    bits = []
     step = 1
-    while step < n:
-        x = x + lax.ppermute(x, axis, [(i, i ^ step) for i in range(n)])
+    while step < n_dom:
+        bits.append(step)
         step *= 2
+    turn = (len(bits) + 1) // 2
+    orders = (bits, bits[turn:] + bits[:turn])
+    for j in range(len(bits)):
+        pairs = []
+        for i in range(n_dom * n_ka):
+            d, a = divmod(i, n_ka)
+            pairs.append((i, (d ^ orders[a % 2][j]) * n_ka + a))
+        x = x + lax.ppermute(x, ("dom", "ka"), pairs)
     return x
 
 
@@ -125,7 +134,7 @@
         s_sin = lax.dot_general(
             charge_live, sin_table, tensor_product, preferred_element_type=jnp.float32
         )
-        s_both = butterfly_sum(jnp.stack([s_cos, s_sin], 0), "dom", n_dom)
+        s_both = butterfly_sum(jnp.stack([s_cos, s_sin], 0), n_dom, n_ka)
         cos_side, sin_side = reciprocal_filter_weight(
             s_both[0], s_both[1], cartesian_mode_vector, gaussian_spread, atoms_total
         )

time: 54.8 us -> 53.4 us (0.974)
  waiting for transfers between devices: 16.6 us -> 14.3 us
  starting transfers between devices: 9.62 us -> 10.6 us
    ppermute x3, waiting for transfers between devices: 11.1 us -> 8.89 us  [butterfly_sum(): x = x + lax.ppermute(x, ('dom', 'ka'), pairs)]
where the time goes in v14:
time: 53.4 us; the launch traced here: 53.2 us
  other arithmetic  16.1 us (30%)
  waiting for transfers between devices  14.3 us (27%)
  starting transfers between devices  10.6 us (20%)
  matrix products  8.93 us (17%)
  local copies, waits for them, and re-layouts  1.83 us (3%)
  between operations  1.54 us (3%)
    convert_element_type x1, other arithmetic, local(): sin_table = sin_f.astype(jnp.bfloat16)  13 us
    ppermute x3, waiting for transfers between devices, butterfly_sum(): x = x + lax.ppermute(x, ('dom', 'ka'), pairs)  8.89 us
    ppermute x3, starting transfers between devices, butterfly_sum(): x = x + lax.ppermute(x, ('dom', 'ka'), pairs)  8.27 us
    dot_general x1, matrix products, local(): field = jnp.dot(cos_side, cos_table, preferred_element_type=jnp.float32)  4.01 us
    ppermute x1, waiting for transfers between devices, halving_scatter(): recv = lax.ppermute(send.astype(jnp.bfloat16), axis, pairs_list)  3.59 us
    ppermute x1, starting transfers between devices, halving_scatter(): recv = lax.ppermute(send.astype(jnp.bfloat16), axis, pairs_list)  2.21 us
    dot_general x1, matrix products, local(): lax.dot_general(charge_live, cos_table, tensor_product, preferred_element...  1.97 us
    dot_general x1, matrix products, local(): lax.dot_general(charge_live, sin_table, tensor_product, preferred_element...  1.95 us
  transfers between devices with their start and end apart: 5, of which 5 were waited for; matrix products, arithmetic and copies ran while one was open for 0% of the time, Pallas kernels for 0%

profile of v14, /device:TPU:0, one launch (start us, length us, event | category | flops | bytes accessed | tf_op | source)
XLA Modules:
  0.0 53.2 jit_solution(4833582057293268538)
XLA Ops:
  0.6 0.7 %convert_element_type.36 = f32[3,512]{1,0:T(4,128)S(1)} convert(s32[3,512]{1,0:T(4,128)} %param.7) | non-fusion elementwise | flops 1536 | bytes 12288 | tf_op jit(solution)/shard_map/convert_element_type | solution.py:120
  1.4 1.1 %fusion.34 = (f32[1,6144]{1,0:T(1,128)S(1)}, f32[1,6144]{1,0:T(1,128)S(1)}, f32[1,6144]{1,0:T(1,128)S(1)}) fusion(f32[3,6144]{1,0:T(4,128)} %param.5), kind=kLoop, calls=%fused_computation.80 | loop fusion | bytes 147456 | tf_op jit(solution)/shard_map/slice | solution.py:122
  2.5 0.0 copy-start.2
  2.5 13.0 %multiply_convert_fusion = (bf16[512,6144]{1,0:T(8,128)(2,1)S(1)}, bf16[512,6144]{1,0:T(8,128)(2,1)S(1)}) fusion(f32[6144]{0:T(1024)S(1)} %bitcast.82, f32[512]{0:T(512)S(1)} %bitcast.92, f32[6144]{0:T(1024)S(1)} %bitcast.83, f32[512]{0:T(512)S(1)} %bitcast.93, f32[6144]{0:T(1024)S(1)} %bitcast.81, f32[512]{0:T(512)S(1)} %bitcast.94), kind=kLoop, calls=%fused_computation | loop fusion | flops 97517568 | bytes 12662784 | tf_op jit(solution)/shard_map/convert_element_type | solution.py:128
  15.5 0.0 copy-start
  15.5 0.0 copy-start.1
  16.2 0.0 copy-done.2
  16.2 0.0 copy-start.3
  16.2 2.0 %convolution_bitcast_fusion = f32[1,32,512]{2,1,0:T(8,128)S(1)} fusion(bf16[512,6144]{1,0:T(8,128)(2,1)S(1)} %get-tuple-element.5, bf16[32,6144]{1,0:T(8,128)(2,1)S(1)} %copy-done.2, pred[6144]{0:T(1024)(128)(4,1)S(1)} %iota_compare_fusion), kind=kOutput, calls=%fused_computation.12 | convolution fusion | flops 201523200 | bytes 6756352 | tf_op jit(solution)/shard_map/dot_general | solution.py:134
  18.2 2.0 %convolution_bitcast_fusion.1 = f32[1,32,512]{2,1,0:T(8,128)S(1)} fusion(bf16[512,6144]{1,0:T(8,128)(2,1)S(1)} %get-tuple-element.4, bf16[32,6144]{1,0:T(8,128)(2,1)S(1)} %copy-done.2, pred[6144]{0:T(1024)(128)(4,1)S(1)} %iota_compare_fusion), kind=kOutput, calls=%fused_computation.13 | convolution fusion | flops 201523200 | bytes 6756352 | tf_op jit(solution)/shard_map/dot_general | solution.py:131
  20.2 0.0 copy-done
  20.2 0.0 copy-done.1
  20.2 3.0 %collective-permute-start = (f32[2,32,512]{2,1,0:T(8,128)S(1)}, f32[2,32,512]{2,1,0:T(8,128)S(1)}, u32[]{:S(2)}, u32[]{:S(2)}) collective-permute-start(f32[2,32,512]{2,1,0:T(8,128)S(1)} %pad_maximum_fusion.2), channel_id=1, source_target_pairs={{0,4},{1,17},{2,6},{3,19},{4,0},{5,21},{6,2},{7,23},{8,12},{9,25},... | collective-permute-start | bytes 393224 | tf_op jit(solution)/shard_map/ppermute | solution.py:85
  23.2 2.9 %collective-permute-done = f32[2,32,512]{2,1,0:T(8,128)S(1)} collective-permute-done((f32[2,32,512]{2,1,0:T(8,128)S(1)}, f32[2,32,512]{2,1,0:T(8,128)S(1)}, u32[]{:S(2)}, u32[]{:S(2)}) %collective-permute-start) | collective-permute-done | bytes 131104 | tf_op jit(solution)/shard_map/ppermute | solution.py:85
  26.2 2.1 %collective-permute-start.1 = (f32[2,32,512]{2,1,0:T(8,128)S(1)}, f32[2,32,512]{2,1,0:T(8,128)S(1)}, u32[]{:S(2)}, u32[]{:S(2)}) collective-permute-start(f32[2,32,512]{2,1,0:T(8,128)S(1)} %fusion.30), channel_id=1, source_target_pairs={{0,8},{1,5},{2,10},{3,7},{4,12},{5,1},{6,14},{7,3},{8,0},{9,13},{1... | collective-permute-start | bytes 393224 | tf_op jit(solution)/shard_map/ppermute | solution.py:85
  28.4 2.9 %collective-permute-done.1 = f32[2,32,512]{2,1,0:T(8,128)S(1)} collective-permute-done((f32[2,32,512]{2,1,0:T(8,128)S(1)}, f32[2,32,512]{2,1,0:T(8,128)S(1)}, u32[]{:S(2)}, u32[]{:S(2)}) %collective-permute-start.1) | collective-permute-done | bytes 131104 | tf_op jit(solution)/shard_map/ppermute | solution.py:85
  31.3 3.1 %collective-permute-start.2 = (f32[2,32,512]{2,1,0:T(8,128)S(1)}, f32[2,32,512]{2,1,0:T(8,128)S(1)}, u32[]{:S(2)}, u32[]{:S(2)}) collective-permute-start(f32[2,32,512]{2,1,0:T(8,128)S(1)} %fusion.39), channel_id=1, source_target_pairs={{0,16},{1,9},{2,18},{3,11},{4,20},{5,13},{6,22},{7,15},{8,24},{9,1... | collective-permute-start | bytes 393224 | tf_op jit(solution)/shard_map/ppermute | solution.py:85
  34.4 0.0 copy-done.3
  34.4 3.0 %collective-permute-done.2 = f32[2,32,512]{2,1,0:T(8,128)S(1)} collective-permute-done((f32[2,32,512]{2,1,0:T(8,128)S(1)}, f32[2,32,512]{2,1,0:T(8,128)S(1)}, u32[]{:S(2)}, u32[]{:S(2)}) %collective-permute-start.2) | collective-permute-done | bytes 131104 | tf_op jit(solution)/shard_map/ppermute | solution.py:85
  37.5 0.1 multiply_convert_fusion.3
  37.6 0.0 slice-start
  37.6 0.0 slice-start.1
  37.6 4.0 %fusion.7 = f32[128,6144]{1,0:T(8,128)S(1)} fusion(bf16[512,6144]{1,0:T(8,128)(2,1)} %copy-done.1, bf16[32,512]{1,0:T(8,128)(2,1)S(1)} %get-tuple-element.45, bf16[32,512]{1,0:T(8,128)(2,1)S(1)} %get-tuple-element.44, bf16[32,512]{1,0:T(8,128)(2,1)S(1)} %get-tuple-element.46, bf16[32,512]{1,0:T(8,128)(2,1)S(1)} %get-tuple-element.29), kind=kOutput, calls=%fused_computation.35 | convolution fusion | flops 805830656 | bytes 9568256 | tf_op jit(solution)/shard_map/dot_general | solution.py:141
  41.6 0.0 slice-done
  41.6 0.6 %slice-done.1 = s8[2097152]{0:T(1024)(128)(4,1)S(1)} async-done(((s8[6291456]{0:T(1024)(128)(4,1)}), s8[2097152]{0:T(1024)(128)(4,1)S(1)}, s32[]{:S(2)}) %slice-start.1) | async-done | bytes 2097176
  42.3 1.0 %convolution_add_fusion = f32[128,6144]{1,0:T(8,128)S(1)} fusion(f32[128,6144]{1,0:T(8,128)S(1)} %fusion.7, bf16[512,6144]{1,0:T(8,128)(2,1)S(1)} %bitcast.75, bf16[32,512]{1,0:T(8,128)(2,1)S(1)} %get-tuple-element.28, bf16[32,512]{1,0:T(8,128)(2,1)S(1)} %get-tuple-element.27, bf16[32,512]{1,0:T(8,128)(2,1)S(1)} %get-tuple-element.11, ...), kind=kOutput, calls=%fused_computation.8 | convolution fusion | flops 806617088 | bytes 12713984 | tf_op jit(solution)/shard_map/dot_general | solution.py:142
  43.3 0.4 fusion.2
  43.7 0.1 pad_maximum_fusion
  43.8 0.1 slice_bitcast_fusion.5
  43.9 0.1 pad_maximum_fusion.1
  44.0 0.1 select_bitcast_fusion
  44.0 0.1 collective-permute-start.3
  44.2 1.8 %collective-permute-done.3 = f32[2,35,1536]{2,1,0:T(8,128)S(1)} collective-permute-done((f32[2,35,1536]{2,1,0:T(8,128)S(1)}, f32[2,35,1536]{2,1,0:T(8,128)S(1)}, u32[]{:S(2)}, u32[]{:S(2)}) %collective-permute-start.3) | collective-permute-done | bytes 430112 | tf_op jit(solution)/shard_map/ppermute | solution.py:102
  46.0 0.1 fusion.5
  46.1 2.2 %collective-permute-start.4 = (bf16[1,35,1536]{2,1,0:T(8,128)(2,1)S(1)}, bf16[1,35,1536]{2,1,0:T(8,128)(2,1)S(1)}, u32[]{:S(2)}, u32[]{:S(2)}) collective-permute-start(bf16[1,35,1536]{2,1,0:T(8,128)(2,1)S(1)} %fusion.22), channel_id=1, source_target_pairs={{0,2},{1,3},{2,0},{3,1},{4,6},{5,7},{6,4},{7,5},{8,10},{9,11},{10,... | collective-permute-start | bytes 322568 | tf_op jit(solution)/shard_map/ppermute | solution.py:100
  48.3 3.6 %collective-permute-done.4 = bf16[1,35,1536]{2,1,0:T(8,128)(2,1)S(1)} collective-permute-done((bf16[1,35,1536]{2,1,0:T(8,128)(2,1)S(1)}, bf16[1,35,1536]{2,1,0:T(8,128)(2,1)S(1)}, u32[]{:S(2)}, u32[]{:S(2)}) %collective-permute-start.4) | collective-permute-done | bytes 107552 | tf_op jit(solution)/shard_map/ppermute | solution.py:100
  51.9 0.6 %fusion.25 = f32[3,1536]{1,0:T(4,128)} fusion(f32[1,35,1536]{2,1,0:T(8,128)S(1)} %select_bitcast_fusion.1, bf16[1,35,1536]{2,1,0:T(8,128)(2,1)S(1)} %collective-permute-done.4), kind=kLoop, calls=%fused_computation.63 | loop fusion | flops 9216 | bytes 46080 | tf_op jit(solution)/shard_map/add | solution.py:154
  52.5 0.7 %fusion.6 = f32[32,1536]{1,0:T(8,128)} fusion(f32[1,35,1536]{2,1,0:T(8,128)S(1)} %select_bitcast_fusion.1, bf16[1,35,1536]{2,1,0:T(8,128)(2,1)S(1)} %collective-permute-done.4), kind=kLoop, calls=%fused_computation.33 | loop fusion | flops 98304 | bytes 491520 | tf_op jit(solution)/shard_map/add | solution.py:153
  (11 shorter events, 0.2 us)
Async XLA Ops:
  2.5 13.8 %copy-start.2 = (bf16[32,6144]{1,0:T(8,128)(2,1)S(1)}, bf16[32,6144]{1,0:T(8,128)(2,1)}, u32[]{:S(2)}) copy-start(bf16[32,6144]{1,0:T(8,128)(2,1)} %param.6) | copy-start | bytes 1179652
  15.5 4.7 %copy-start = (bf16[512,6144]{1,0:T(8,128)(2,1)}, bf16[512,6144]{1,0:T(8,128)(2,1)S(1)}, u32[]{:S(2)}) copy-start(bf16[512,6144]{1,0:T(8,128)(2,1)S(1)} %get-tuple-element.5) | copy-start | bytes 18874372
  15.5 4.7 %copy-start.1 = (bf16[512,6144]{1,0:T(8,128)(2,1)}, bf16[512,6144]{1,0:T(8,128)(2,1)S(1)}, u32[]{:S(2)}) copy-start(bf16[512,6144]{1,0:T(8,128)(2,1)S(1)} %get-tuple-element.4) | copy-start | bytes 18874372
  16.2 18.2 %copy-start.3 = (f32[32]{0:T(128)S(1)}, f32[32]{0:T(128)}, u32[]{:S(2)}) copy-start(f32[32]{0:T(128)} %param.9) | copy-start | bytes 388
  20.2 6.0 %collective-permute-start = (f32[2,32,512]{2,1,0:T(8,128)S(1)}, f32[2,32,512]{2,1,0:T(8,128)S(1)}, u32[]{:S(2)}, u32[]{:S(2)}) collective-permute-start(f32[2,32,512]{2,1,0:T(8,128)S(1)} %pad_maximum_fusion.2), channel_id=1, source_target_pairs={{0,4},{1,17},{2,6},{3,19},{4,0},{5,21},{6,2},{7,23},{8,12},{9,25},... | collective-permute-start | bytes 393224 | tf_op jit(solution)/shard_map/ppermute | solution.py:85
  26.2 5.1 %collective-permute-start.1 = (f32[2,32,512]{2,1,0:T(8,128)S(1)}, f32[2,32,512]{2,1,0:T(8,128)S(1)}, u32[]{:S(2)}, u32[]{:S(2)}) collective-permute-start(f32[2,32,512]{2,1,0:T(8,128)S(1)} %fusion.30), channel_id=1, source_target_pairs={{0,8},{1,5},{2,10},{3,7},{4,12},{5,1},{6,14},{7,3},{8,0},{9,13},{1... | collective-permute-start | bytes 393224 | tf_op jit(solution)/shard_map/ppermute | solution.py:85
  31.3 6.1 %collective-permute-start.2 = (f32[2,32,512]{2,1,0:T(8,128)S(1)}, f32[2,32,512]{2,1,0:T(8,128)S(1)}, u32[]{:S(2)}, u32[]{:S(2)}) collective-permute-start(f32[2,32,512]{2,1,0:T(8,128)S(1)} %fusion.39), channel_id=1, source_target_pairs={{0,16},{1,9},{2,18},{3,11},{4,20},{5,13},{6,22},{7,15},{8,24},{9,1... | collective-permute-start | bytes 393224 | tf_op jit(solution)/shard_map/ppermute | solution.py:85
  37.6 4.1 %slice-start = ((s8[6291456]{0:T(1024)(128)(4,1)}), s8[4194304]{0:T(1024)(128)(4,1)S(1)}, s32[]{:S(2)}) async-start(s8[6291456]{0:T(1024)(128)(4,1)} %bitcast.74), calls=%async_computation | async-start | bytes 8388608
  37.6 4.6 %slice-start.1 = ((s8[6291456]{0:T(1024)(128)(4,1)}), s8[2097152]{0:T(1024)(128)(4,1)S(1)}, s32[]{:S(2)}) async-start(s8[6291456]{0:T(1024)(128)(4,1)} %bitcast.74), calls=%async_computation.1 | async-start | bytes 4194304
  44.0 1.9 %collective-permute-start.3 = (f32[2,35,1536]{2,1,0:T(8,128)S(1)}, f32[2,35,1536]{2,1,0:T(8,128)S(1)}, u32[]{:S(2)}, u32[]{:S(2)}) collective-permute-start(f32[2,35,1536]{2,1,0:T(8,128)S(1)} %select_bitcast_fusion), channel_id=1, source_target_pairs={{0,1},{1,0},{2,3},{3,2},{4,5},{5,4},{6,7},{7,6},{8,9},{9,8},{10,11... | collective-permute-start | bytes 1290248 | tf_op jit(solution)/shard_map/ppermute | solution.py:102
  46.1 5.8 %collective-permute-start.4 = (bf16[1,35,1536]{2,1,0:T(8,128)(2,1)S(1)}, bf16[1,35,1536]{2,1,0:T(8,128)(2,1)S(1)}, u32[]{:S(2)}, u32[]{:S(2)}) collective-permute-start(bf16[1,35,1536]{2,1,0:T(8,128)(2,1)S(1)} %fusion.22), channel_id=1, source_target_pairs={{0,2},{1,3},{2,0},{3,1},{4,6},{5,7},{6,4},{7,5},{8,10},{9,11},{10,... | collective-permute-start | bytes 322568 | tf_op jit(solution)/shard_map/ppermute | solution.py:100

commit v15 on v14

--- a/solution.py
+++ b/solution.py
@@ -16,7 +16,7 @@
 
 
 def turns_cos_sin(t):
-    r = t - jnp.floor(t + 0.5)
+    r = t - lax.round(t, lax.RoundingMethod.TO_NEAREST_EVEN)
     r2 = r * r
     s = jnp.float32(_SIN_C[-1] * _ROOT2)
     for coef in _SIN_C[-2::-1]:

time: 53.4 us -> 53 us (level)
  no operation moved by 1% of the time
where the time goes in v15:
time: 53 us; the launch traced here: 52.8 us
  other arithmetic  15.7 us (30%)
  waiting for transfers between devices  14.3 us (27%)
  starting transfers between devices  10.6 us (20%)
  matrix products  8.93 us (17%)
  local copies, waits for them, and re-layouts  1.83 us (3%)
  between operations  1.54 us (3%)
    convert_element_type x1, other arithmetic, local(): sin_table = sin_f.astype(jnp.bfloat16)  12.6 us
    ppermute x3, waiting for transfers between devices, butterfly_sum(): x = x + lax.ppermute(x, ('dom', 'ka'), pairs)  8.89 us
    ppermute x3, starting transfers between devices, butterfly_sum(): x = x + lax.ppermute(x, ('dom', 'ka'), pairs)  8.27 us
    dot_general x1, matrix products, local(): field = jnp.dot(cos_side, cos_table, preferred_element_type=jnp.float32)  4.01 us
    ppermute x1, waiting for transfers between devices, halving_scatter(): recv = lax.ppermute(send.astype(jnp.bfloat16), axis, pairs_list)  3.59 us
    ppermute x1, starting transfers between devices, halving_scatter(): recv = lax.ppermute(send.astype(jnp.bfloat16), axis, pairs_list)  2.21 us
    dot_general x1, matrix products, local(): lax.dot_general(charge_live, cos_table, tensor_product, preferred_element...  1.97 us
    dot_general x1, matrix products, local(): lax.dot_general(charge_live, sin_table, tensor_product, preferred_element...  1.95 us
  transfers between devices with their start and end apart: 5, of which 5 were waited for; matrix products, arithmetic and copies ran while one was open for 0% of the time, Pallas kernels for 0%

profile of v15, /device:TPU:0, one launch (start us, length us, event | category | flops | bytes accessed | tf_op | source)
XLA Modules:
  0.0 52.8 jit_solution(7432004497594042862)
XLA Ops:
  0.6 0.7 %convert_element_type.36 = f32[3,512]{1,0:T(4,128)S(1)} convert(s32[3,512]{1,0:T(4,128)} %param.7) | non-fusion elementwise | flops 1536 | bytes 12288 | tf_op jit(solution)/shard_map/convert_element_type | solution.py:120
  1.4 1.1 %fusion.34 = (f32[1,6144]{1,0:T(1,128)S(1)}, f32[1,6144]{1,0:T(1,128)S(1)}, f32[1,6144]{1,0:T(1,128)S(1)}) fusion(f32[3,6144]{1,0:T(4,128)} %param.5), kind=kLoop, calls=%fused_computation.80 | loop fusion | bytes 147456 | tf_op jit(solution)/shard_map/slice | solution.py:122
  2.5 0.0 copy-start.2
  2.5 12.6 %multiply_convert_fusion = (bf16[512,6144]{1,0:T(8,128)(2,1)S(1)}, bf16[512,6144]{1,0:T(8,128)(2,1)S(1)}) fusion(f32[6144]{0:T(1024)S(1)} %bitcast.82, f32[512]{0:T(512)S(1)} %bitcast.92, f32[6144]{0:T(1024)S(1)} %bitcast.83, f32[512]{0:T(512)S(1)} %bitcast.93, f32[6144]{0:T(1024)S(1)} %bitcast.81, f32[512]{0:T(512)S(1)} %bitcast.94), kind=kLoop, calls=%fused_computation.1 | loop fusion | flops 94371840 | bytes 12662784 | tf_op jit(solution)/shard_map/convert_element_type | solution.py:128
  15.1 0.0 copy-start
  15.1 0.0 copy-start.1
  15.8 0.0 copy-done.2
  15.8 0.0 copy-start.3
  15.8 2.0 %convolution_bitcast_fusion = f32[1,32,512]{2,1,0:T(8,128)S(1)} fusion(bf16[512,6144]{1,0:T(8,128)(2,1)S(1)} %get-tuple-element.5, bf16[32,6144]{1,0:T(8,128)(2,1)S(1)} %copy-done.2, pred[6144]{0:T(1024)(128)(4,1)S(1)} %iota_compare_fusion), kind=kOutput, calls=%fused_computation.12 | convolution fusion | flops 201523200 | bytes 6756352 | tf_op jit(solution)/shard_map/dot_general | solution.py:134
  17.8 2.0 %convolution_bitcast_fusion.1 = f32[1,32,512]{2,1,0:T(8,128)S(1)} fusion(bf16[512,6144]{1,0:T(8,128)(2,1)S(1)} %get-tuple-element.4, bf16[32,6144]{1,0:T(8,128)(2,1)S(1)} %copy-done.2, pred[6144]{0:T(1024)(128)(4,1)S(1)} %iota_compare_fusion), kind=kOutput, calls=%fused_computation.13 | convolution fusion | flops 201523200 | bytes 6756352 | tf_op jit(solution)/shard_map/dot_general | solution.py:131
  19.7 0.0 copy-done
  19.8 0.0 copy-done.1
  19.8 3.0 %collective-permute-start = (f32[2,32,512]{2,1,0:T(8,128)S(1)}, f32[2,32,512]{2,1,0:T(8,128)S(1)}, u32[]{:S(2)}, u32[]{:S(2)}) collective-permute-start(f32[2,32,512]{2,1,0:T(8,128)S(1)} %pad_maximum_fusion.2), channel_id=1, source_target_pairs={{0,4},{1,17},{2,6},{3,19},{4,0},{5,21},{6,2},{7,23},{8,12},{9,25},... | collective-permute-start | bytes 393224 | tf_op jit(solution)/shard_map/ppermute | solution.py:85
  22.8 2.9 %collective-permute-done = f32[2,32,512]{2,1,0:T(8,128)S(1)} collective-permute-done((f32[2,32,512]{2,1,0:T(8,128)S(1)}, f32[2,32,512]{2,1,0:T(8,128)S(1)}, u32[]{:S(2)}, u32[]{:S(2)}) %collective-permute-start) | collective-permute-done | bytes 131104 | tf_op jit(solution)/shard_map/ppermute | solution.py:85
  25.8 2.1 %collective-permute-start.1 = (f32[2,32,512]{2,1,0:T(8,128)S(1)}, f32[2,32,512]{2,1,0:T(8,128)S(1)}, u32[]{:S(2)}, u32[]{:S(2)}) collective-permute-start(f32[2,32,512]{2,1,0:T(8,128)S(1)} %fusion.30), channel_id=1, source_target_pairs={{0,8},{1,5},{2,10},{3,7},{4,12},{5,1},{6,14},{7,3},{8,0},{9,13},{1... | collective-permute-start | bytes 393224 | tf_op jit(solution)/shard_map/ppermute | solution.py:85
  27.9 2.9 %collective-permute-done.1 = f32[2,32,512]{2,1,0:T(8,128)S(1)} collective-permute-done((f32[2,32,512]{2,1,0:T(8,128)S(1)}, f32[2,32,512]{2,1,0:T(8,128)S(1)}, u32[]{:S(2)}, u32[]{:S(2)}) %collective-permute-start.1) | collective-permute-done | bytes 131104 | tf_op jit(solution)/shard_map/ppermute | solution.py:85
  30.9 3.1 %collective-permute-start.2 = (f32[2,32,512]{2,1,0:T(8,128)S(1)}, f32[2,32,512]{2,1,0:T(8,128)S(1)}, u32[]{:S(2)}, u32[]{:S(2)}) collective-permute-start(f32[2,32,512]{2,1,0:T(8,128)S(1)} %fusion.39), channel_id=1, source_target_pairs={{0,16},{1,9},{2,18},{3,11},{4,20},{5,13},{6,22},{7,15},{8,24},{9,1... | collective-permute-start | bytes 393224 | tf_op jit(solution)/shard_map/ppermute | solution.py:85
  34.0 0.0 copy-done.3
  34.0 3.0 %collective-permute-done.2 = f32[2,32,512]{2,1,0:T(8,128)S(1)} collective-permute-done((f32[2,32,512]{2,1,0:T(8,128)S(1)}, f32[2,32,512]{2,1,0:T(8,128)S(1)}, u32[]{:S(2)}, u32[]{:S(2)}) %collective-permute-start.2) | collective-permute-done | bytes 131104 | tf_op jit(solution)/shard_map/ppermute | solution.py:85
  37.0 0.1 multiply_convert_fusion.3
  37.1 0.0 slice-start
  37.2 0.0 slice-start.1
  37.2 4.0 %fusion.7 = f32[128,6144]{1,0:T(8,128)S(1)} fusion(bf16[512,6144]{1,0:T(8,128)(2,1)} %copy-done.1, bf16[32,512]{1,0:T(8,128)(2,1)S(1)} %get-tuple-element.45, bf16[32,512]{1,0:T(8,128)(2,1)S(1)} %get-tuple-element.44, bf16[32,512]{1,0:T(8,128)(2,1)S(1)} %get-tuple-element.46, bf16[32,512]{1,0:T(8,128)(2,1)S(1)} %get-tuple-element.29), kind=kOutput, calls=%fused_computation.35 | convolution fusion | flops 805830656 | bytes 9568256 | tf_op jit(solution)/shard_map/dot_general | solution.py:141
  41.2 0.0 slice-done
  41.2 0.6 %slice-done.1 = s8[2097152]{0:T(1024)(128)(4,1)S(1)} async-done(((s8[6291456]{0:T(1024)(128)(4,1)}), s8[2097152]{0:T(1024)(128)(4,1)S(1)}, s32[]{:S(2)}) %slice-start.1) | async-done | bytes 2097176
  41.8 1.0 %convolution_add_fusion = f32[128,6144]{1,0:T(8,128)S(1)} fusion(f32[128,6144]{1,0:T(8,128)S(1)} %fusion.7, bf16[512,6144]{1,0:T(8,128)(2,1)S(1)} %bitcast.75, bf16[32,512]{1,0:T(8,128)(2,1)S(1)} %get-tuple-element.28, bf16[32,512]{1,0:T(8,128)(2,1)S(1)} %get-tuple-element.27, bf16[32,512]{1,0:T(8,128)(2,1)S(1)} %get-tuple-element.11, ...), kind=kOutput, calls=%fused_computation.8 | convolution fusion | flops 806617088 | bytes 12713984 | tf_op jit(solution)/shard_map/dot_general | solution.py:142
  42.8 0.4 fusion.2
  43.3 0.1 pad_maximum_fusion
  43.4 0.1 slice_bitcast_fusion.5
  43.5 0.1 pad_maximum_fusion.1
  43.6 0.1 select_bitcast_fusion
  43.6 0.1 collective-permute-start.3
  43.7 1.8 %collective-permute-done.3 = f32[2,35,1536]{2,1,0:T(8,128)S(1)} collective-permute-done((f32[2,35,1536]{2,1,0:T(8,128)S(1)}, f32[2,35,1536]{2,1,0:T(8,128)S(1)}, u32[]{:S(2)}, u32[]{:S(2)}) %collective-permute-start.3) | collective-permute-done | bytes 430112 | tf_op jit(solution)/shard_map/ppermute | solution.py:102
  45.5 0.1 fusion.5
  45.7 2.2 %collective-permute-start.4 = (bf16[1,35,1536]{2,1,0:T(8,128)(2,1)S(1)}, bf16[1,35,1536]{2,1,0:T(8,128)(2,1)S(1)}, u32[]{:S(2)}, u32[]{:S(2)}) collective-permute-start(bf16[1,35,1536]{2,1,0:T(8,128)(2,1)S(1)} %fusion.22), channel_id=1, source_target_pairs={{0,2},{1,3},{2,0},{3,1},{4,6},{5,7},{6,4},{7,5},{8,10},{9,11},{10,... | collective-permute-start | bytes 322568 | tf_op jit(solution)/shard_map/ppermute | solution.py:100
  47.9 3.6 %collective-permute-done.4 = bf16[1,35,1536]{2,1,0:T(8,128)(2,1)S(1)} collective-permute-done((bf16[1,35,1536]{2,1,0:T(8,128)(2,1)S(1)}, bf16[1,35,1536]{2,1,0:T(8,128)(2,1)S(1)}, u32[]{:S(2)}, u32[]{:S(2)}) %collective-permute-start.4) | collective-permute-done | bytes 107552 | tf_op jit(solution)/shard_map/ppermute | solution.py:100
  51.5 0.6 %fusion.25 = f32[3,1536]{1,0:T(4,128)} fusion(f32[1,35,1536]{2,1,0:T(8,128)S(1)} %select_bitcast_fusion.1, bf16[1,35,1536]{2,1,0:T(8,128)(2,1)S(1)} %collective-permute-done.4), kind=kLoop, calls=%fused_computation.63 | loop fusion | flops 9216 | bytes 46080 | tf_op jit(solution)/shard_map/add | solution.py:154
  52.1 0.7 %fusion.6 = f32[32,1536]{1,0:T(8,128)} fusion(f32[1,35,1536]{2,1,0:T(8,128)S(1)} %select_bitcast_fusion.1, bf16[1,35,1536]{2,1,0:T(8,128)(2,1)S(1)} %collective-permute-done.4), kind=kLoop, calls=%fused_computation.33 | loop fusion | flops 98304 | bytes 491520 | tf_op jit(solution)/shard_map/add | solution.py:153
  (11 shorter events, 0.2 us)
Async XLA Ops:
  2.5 13.3 %copy-start.2 = (bf16[32,6144]{1,0:T(8,128)(2,1)S(1)}, bf16[32,6144]{1,0:T(8,128)(2,1)}, u32[]{:S(2)}) copy-start(bf16[32,6144]{1,0:T(8,128)(2,1)} %param.6) | copy-start | bytes 1179652
  15.1 4.7 %copy-start = (bf16[512,6144]{1,0:T(8,128)(2,1)}, bf16[512,6144]{1,0:T(8,128)(2,1)S(1)}, u32[]{:S(2)}) copy-start(bf16[512,6144]{1,0:T(8,128)(2,1)S(1)} %get-tuple-element.5) | copy-start | bytes 18874372
  15.1 4.7 %copy-start.1 = (bf16[512,6144]{1,0:T(8,128)(2,1)}, bf16[512,6144]{1,0:T(8,128)(2,1)S(1)}, u32[]{:S(2)}) copy-start(bf16[512,6144]{1,0:T(8,128)(2,1)S(1)} %get-tuple-element.4) | copy-start | bytes 18874372
  15.8 18.2 %copy-start.3 = (f32[32]{0:T(128)S(1)}, f32[32]{0:T(128)}, u32[]{:S(2)}) copy-start(f32[32]{0:T(128)} %param.9) | copy-start | bytes 388
  19.8 6.0 %collective-permute-start = (f32[2,32,512]{2,1,0:T(8,128)S(1)}, f32[2,32,512]{2,1,0:T(8,128)S(1)}, u32[]{:S(2)}, u32[]{:S(2)}) collective-permute-start(f32[2,32,512]{2,1,0:T(8,128)S(1)} %pad_maximum_fusion.2), channel_id=1, source_target_pairs={{0,4},{1,17},{2,6},{3,19},{4,0},{5,21},{6,2},{7,23},{8,12},{9,25},... | collective-permute-start | bytes 393224 | tf_op jit(solution)/shard_map/ppermute | solution.py:85
  25.8 5.1 %collective-permute-start.1 = (f32[2,32,512]{2,1,0:T(8,128)S(1)}, f32[2,32,512]{2,1,0:T(8,128)S(1)}, u32[]{:S(2)}, u32[]{:S(2)}) collective-permute-start(f32[2,32,512]{2,1,0:T(8,128)S(1)} %fusion.30), channel_id=1, source_target_pairs={{0,8},{1,5},{2,10},{3,7},{4,12},{5,1},{6,14},{7,3},{8,0},{9,13},{1... | collective-permute-start | bytes 393224 | tf_op jit(solution)/shard_map/ppermute | solution.py:85
  30.9 6.1 %collective-permute-start.2 = (f32[2,32,512]{2,1,0:T(8,128)S(1)}, f32[2,32,512]{2,1,0:T(8,128)S(1)}, u32[]{:S(2)}, u32[]{:S(2)}) collective-permute-start(f32[2,32,512]{2,1,0:T(8,128)S(1)} %fusion.39), channel_id=1, source_target_pairs={{0,16},{1,9},{2,18},{3,11},{4,20},{5,13},{6,22},{7,15},{8,24},{9,1... | collective-permute-start | bytes 393224 | tf_op jit(solution)/shard_map/ppermute | solution.py:85
  37.1 4.1 %slice-start = ((s8[6291456]{0:T(1024)(128)(4,1)}), s8[4194304]{0:T(1024)(128)(4,1)S(1)}, s32[]{:S(2)}) async-start(s8[6291456]{0:T(1024)(128)(4,1)} %bitcast.74), calls=%async_computation | async-start | bytes 8388608
  37.2 4.6 %slice-start.1 = ((s8[6291456]{0:T(1024)(128)(4,1)}), s8[2097152]{0:T(1024)(128)(4,1)S(1)}, s32[]{:S(2)}) async-start(s8[6291456]{0:T(1024)(128)(4,1)} %bitcast.74), calls=%async_computation.1 | async-start | bytes 4194304
  43.6 1.9 %collective-permute-start.3 = (f32[2,35,1536]{2,1,0:T(8,128)S(1)}, f32[2,35,1536]{2,1,0:T(8,128)S(1)}, u32[]{:S(2)}, u32[]{:S(2)}) collective-permute-start(f32[2,35,1536]{2,1,0:T(8,128)S(1)} %select_bitcast_fusion), channel_id=1, source_target_pairs={{0,1},{1,0},{2,3},{3,2},{4,5},{5,4},{6,7},{7,6},{8,9},{9,8},{10,11... | collective-permute-start | bytes 1290248 | tf_op jit(solution)/shard_map/ppermute | solution.py:102
  45.7 5.8 %collective-permute-start.4 = (bf16[1,35,1536]{2,1,0:T(8,128)(2,1)S(1)}, bf16[1,35,1536]{2,1,0:T(8,128)(2,1)S(1)}, u32[]{:S(2)}, u32[]{:S(2)}) collective-permute-start(bf16[1,35,1536]{2,1,0:T(8,128)(2,1)S(1)} %fusion.22), channel_id=1, source_target_pairs={{0,2},{1,3},{2,0},{3,1},{4,6},{5,7},{6,4},{7,5},{8,10},{9,11},{10,... | collective-permute-start | bytes 322568 | tf_op jit(solution)/shard_map/ppermute | solution.py:100
